TPU v7x, 512 devices: a whole 4x4x16 slice. The times are simulated.
512 devices in a mesh: dp: 32 (over y, z_hi, x), tensor: 16 (over z_lo, core).
Axes of the slice: x: 4, y: 4, z: 16 (z_hi: 2, z_lo: 8; z = z_hi * 8 + z_lo), core: 2. Of those that a mesh axis runs over, the one named last changes fastest.
Arguments:
- inner_x: bfloat16 [32768, 8192], P(('dp', 'tensor')), parts along dimension 0, may hold values from -6 to 6
- inner_bc: bfloat16 [32768, 2048], P(('dp', 'tensor')), parts along dimension 0, may hold values from -6 to 6
- step_raw: bfloat16 [32768, 128], P(('dp', 'tensor')), parts along dimension 0, may hold values from -5 to 5
- conv_state_x: bfloat16 [96, 8192], P('dp', 'tensor'), parts along dimension 0, may hold values from -6 to 6
- conv_state_bc: bfloat16 [96, 2048], P('dp'), parts along dimension 0, may hold values from -6 to 6
- conv_weight_x: bfloat16 [4, 8192], P(None, 'tensor'), may hold values from -3 to 3
- conv_bias_x: bfloat16 [8192], P('tensor'), may hold values from -3 to 3
- conv_weight_bc: bfloat16 [4, 2048], replicated, may hold values from -3 to 3
- conv_bias_bc: bfloat16 [2048], replicated, may hold values from -3 to 3
- step_bias: float32 [128], P('tensor'), may hold values from -4 to -2
- decay_rate: float32 [128], P('tensor'), may hold values from 0 to 1, as said below
- skip_gain: float32 [128], P('tensor'), may hold values from 0.5 to 1.5
- norm_weight: bfloat16 [8192], replicated, may hold values from 0.5 to 1.5
- scan_state: float32 [4096, 64, 256], P(('dp', 'tensor')), parts along dimension 0, may hold values from -3 to 3
Outputs:
- normed: bfloat16 [32768, 8192], P(('dp', 'tensor')), parts along dimension 0
- final_state: float32 [4096, 64, 256], P(('dp', 'tensor')), parts along dimension 0
- conv_tail_x: bfloat16 [96, 8192], P('dp', 'tensor'), parts along dimension 0
- conv_tail_bc: bfloat16 [96, 2048], P('dp', 'tensor'), parts along dimension 0
There are 32 independent parts, one for each index of `dp`. A program takes and returns all parts, laid end to end along the dimension named above; an argument that names none is the same for every part. Nothing has to cross between parts.
Inputs may be any that keep to these rules, and one draw needn't show every extreme that they name: decay_rate lies between 2 / 1024 and 1 / 2.
All inputs are finite; a program needn't handle non-finite values.
Results may differ from a plain program's by a relative error of at most 0.0051.
Values may be sent and summed in bfloat16 or wider, within the bound.
No kernel may reach another device: no remote copies, remote signals or barrier semaphores. Data moves between devices by JAX's collectives and lax.ppermute only.
A program may use at most 64 MiB of HBM per device.

v0:
```python
import jax
import jax.numpy as jnp
from jax import lax
from jax.sharding import PartitionSpec as P

HEAD_DIM = 64
STATE = 256
GROUPS = 4
CONV_K = 4
INNER = 8192


EPSILON = 1e-05


def causal_conv(raw, state, weight, bias):
    length = raw.shape[0]
    padded = jnp.concatenate([state.astype(jnp.float32), raw.astype(jnp.float32)], axis=0)
    total = jnp.zeros(raw.shape, jnp.float32) + bias.astype(jnp.float32)[None, :]
    for kernel_tap in range(CONV_K):
        total = (
            total
            + weight[kernel_tap].astype(jnp.float32)[None, :]
            * padded[kernel_tap : kernel_tap + length]
        )
    return jax.nn.silu(total).astype(jnp.bfloat16)


def state_mix(
    mixed_x, mixed_bc, step_raw, step_bias, decay_rate, skip_gain, scan_state, groups_here
):
    length = mixed_x.shape[0]
    heads_here = step_raw.shape[1]
    per_group = heads_here // groups_here
    step_size = jax.nn.softplus(step_raw.astype(jnp.float32) + step_bias[None, :])
    running = jnp.cumsum(-step_size * decay_rate[None, :], axis=0)
    halves = mixed_bc.reshape(length, groups_here, 2, STATE)
    input_map = halves[:, :, 0, :]
    output_map = halves[:, :, 1, :]
    step_cols = jnp.transpose(step_size)
    running_cols = jnp.transpose(running)
    query_rows = min(512, length)
    pieces = []
    for row_start in range(0, length, query_rows):
        row_stop = row_start + query_rows
        scores = jnp.einsum(
            "tgn,sgn->gts",
            output_map[row_start:row_stop],
            input_map[:row_stop],
            preferred_element_type=jnp.float32,
        )
        causal = row_start + lax.broadcasted_iota(
            jnp.int32, (query_rows, row_stop), 0
        ) >= lax.broadcasted_iota(jnp.int32, (query_rows, row_stop), 1)
        visible = mixed_x[:row_stop]

        def one_head(
            item,
            scores=scores,
            causal=causal,
            visible=visible,
            row_start=row_start,
            row_stop=row_stop,
        ):
            head_index, step_head, running_head = item
            group_scores = lax.dynamic_index_in_dim(
                scores, head_index // per_group, 0, keepdims=False
            )
            log_gap = running_head[row_start:row_stop, None] - running_head[None, :row_stop]
            decayed = jnp.exp(jnp.where(causal, log_gap, 0.0))
            weights = jnp.where(
                causal, group_scores * decayed * step_head[None, :row_stop], 0.0
            ).astype(jnp.bfloat16)
            values = lax.dynamic_slice_in_dim(visible, head_index * HEAD_DIM, HEAD_DIM, 1)
            return jnp.dot(weights, values, preferred_element_type=jnp.float32)

        local_mix = lax.map(
            one_head, (jnp.arange(heads_here, dtype=jnp.int32), step_cols, running_cols)
        )
        pieces.append(
            jnp.transpose(local_mix, (1, 0, 2)).reshape(query_rows, heads_here * HEAD_DIM)
        )
    local_all = jnp.concatenate(pieces, axis=0)
    grouped_state = scan_state.reshape(groups_here, per_group, HEAD_DIM, STATE)
    carried = jnp.einsum(
        "tgn,ghpn->tghp",
        output_map.astype(jnp.float32),
        grouped_state,
        precision=lax.Precision.HIGHEST,
    )
    carried = carried.reshape(length, heads_here, HEAD_DIM) * jnp.exp(running)[:, :, None]
    channels = mixed_x.reshape(length, heads_here, HEAD_DIM).astype(jnp.float32)
    mixed = (
        local_all.reshape(length, heads_here, HEAD_DIM)
        + carried
        + skip_gain[None, :, None] * channels
    )
    mixed_y = mixed.reshape(length, heads_here * HEAD_DIM).astype(jnp.bfloat16)
    tail_decay = jnp.exp(running[length - 1][None, :] - running) * step_size
    weighted = (
        input_map.astype(jnp.float32)[:, :, None, :]
        * tail_decay.reshape(length, groups_here, per_group)[:, :, :, None]
    ).astype(jnp.bfloat16)
    gathered_in = jnp.einsum(
        "tghp,tghn->ghpn",
        mixed_x.reshape(length, groups_here, per_group, HEAD_DIM),
        weighted,
        preferred_element_type=jnp.float32,
    )
    final = (
        jnp.exp(running[length - 1]).reshape(groups_here, per_group)[:, :, None, None]
        * grouped_state
        + gathered_in
    )
    return (mixed_y, final.reshape(heads_here, HEAD_DIM, STATE))


def group_norm(mixed_y, norm_weight):
    rows = mixed_y.shape[0]
    values = mixed_y.astype(jnp.float32).reshape(rows, GROUPS, INNER // GROUPS)
    mean_square = jnp.mean(values * values, axis=2, keepdims=True)
    scaled = (values * lax.rsqrt(mean_square + EPSILON)).reshape(rows, INNER)
    return (scaled * norm_weight.astype(jnp.float32)[None, :]).astype(jnp.bfloat16)


def local(
    inner_x,
    inner_bc,
    step_raw,
    conv_state_x,
    conv_state_bc,
    conv_weight_x,
    conv_bias_x,
    conv_weight_bc,
    conv_bias_bc,
    step_bias,
    decay_rate,
    skip_gain,
    norm_weight,
    scan_state,
):
    tensor_count = lax.axis_size("tensor")
    device_rank = lax.axis_index("tensor")
    token_rows = inner_x.shape[0]
    heads_here = step_bias.shape[0]
    group_width = 2 * STATE
    groups_here = max(1, GROUPS // tensor_count)
    first_group = device_rank * GROUPS // tensor_count
    column_start = first_group * group_width
    x_send = inner_x.reshape(token_rows, tensor_count, heads_here * HEAD_DIM)
    step_send = step_raw.reshape(token_rows, tensor_count, heads_here)
    whole_bc = lax.all_gather(inner_bc, "tensor", axis=0, tiled=True)
    head_x, head_step = (
        lax.all_to_all(x_send, "tensor", split_axis=1, concat_axis=0, tiled=True),
        lax.all_to_all(step_send, "tensor", split_axis=1, concat_axis=0, tiled=True),
    )
    head_bc = lax.dynamic_slice_in_dim(whole_bc, column_start, groups_here * group_width, 1)
    length = head_x.shape[0]
    head_x = head_x.reshape(length, heads_here * HEAD_DIM)
    head_step = head_step.reshape(length, heads_here)
    own_state_bc = lax.dynamic_slice_in_dim(
        conv_state_bc, column_start, groups_here * group_width, 1
    )
    own_weight_bc = lax.dynamic_slice_in_dim(
        conv_weight_bc, column_start, groups_here * group_width, 1
    )
    own_bias_bc = lax.dynamic_slice_in_dim(conv_bias_bc, column_start, groups_here * group_width, 0)
    mixed_x = causal_conv(head_x, conv_state_x, conv_weight_x, conv_bias_x)
    mixed_bc = causal_conv(head_bc, own_state_bc, own_weight_bc, own_bias_bc)
    mixed_y, final_state = state_mix(
        mixed_x, mixed_bc, head_step, step_bias, decay_rate, skip_gain, scan_state, groups_here
    )
    token_y = lax.all_to_all(mixed_y, "tensor", split_axis=0, concat_axis=1, tiled=True)
    normed = group_norm(token_y, norm_weight)
    tail_x = head_x[length - CONV_K + 1 :]
    columns_here = 2 * GROUPS * STATE // tensor_count
    offset = device_rank * columns_here - column_start
    tail_bc = lax.dynamic_slice_in_dim(head_bc[length - CONV_K + 1 :], offset, columns_here, 1)
    return (normed, final_state, tail_x, tail_bc)


def solution(mesh):
    return jax.shard_map(
        local,
        mesh=mesh,
        in_specs=(
            P(("dp", "tensor"), None),
            P(("dp", "tensor"), None),
            P(("dp", "tensor"), None),
            P("dp", "tensor"),
            P("dp", None),
            P(None, "tensor"),
            P("tensor"),
            P(),
            P(),
            P("tensor"),
            P("tensor"),
            P("tensor"),
            P(),
            P(("dp", "tensor"), None, None),
        ),
        out_specs=(
            P(("dp", "tensor"), None),
            P(("dp", "tensor"), None, None),
            P("dp", "tensor"),
            P("dp", "tensor"),
        ),
        check_vma=False,
    )
```

profile of v0, /device:TPU:57, one launch (start us, length us, event | category | flops | bytes accessed | tf_op | source)
XLA Modules:
  0.0 271.9 jit_solution(6294751855197410412)
XLA Ops:
  7.2 0.7 all-gather.2.cloned.1.call-update
  7.9 0.8 copy.85
  8.8 0.7 reshape.180
  9.5 12.9 %all-to-all-start = ((bf16[16,2,256]{2,1,0:T(2,128)(2,1)}), bf16[16,2,256]{2,1,0:T(2,128)(2,1)S(1)}, u32[]{:S(2)}, u32[]{:S(2)}) async-start(bf16[16,2,256]{2,1,0:T(2,128)(2,1)} %reshape.180), calls=%async_computation | async-start | bytes 32768 | tf_op jit(solution)/shard_map/all_to_all | solution.py:155
  22.4 2.3 copy.116
  24.8 6.5 %all-to-all-done = bf16[16,2,256]{2,1,0:T(2,128)(2,1)S(1)} async-done(((bf16[16,2,256]{2,1,0:T(2,128)(2,1)}), bf16[16,2,256]{2,1,0:T(2,128)(2,1)S(1)}, u32[]{:S(2)}, u32[]{:S(2)}) %all-to-all-start) | async-done | bytes 16416 | tf_op jit(solution)/shard_map/all_to_all | solution.py:155
  31.3 5.1 %all-to-all-start.1 = ((bf16[64,16,512]{2,0,1:T(8,128)(2,1)}), bf16[64,16,512]{2,0,1:T(8,128)(2,1)S(1)}, u32[]{:S(2)}, u32[]{:S(2)}) async-start(bf16[64,16,512]{2,0,1:T(8,128)(2,1)} %bitcast.140), calls=%async_computation.1 | async-start | bytes 2097152 | tf_op jit(solution)/shard_map/all_to_all | solution.py:154
  36.4 0.6 convert_element_type.105
  37.1 0.7 mul.286
  38.0 0.9 copy.90
  38.8 0.6 iota_add_fusion
  39.4 1.3 dynamic-slice_convert_fusion.4
  40.7 0.7 dynamic-slice_convert_fusion.3
  41.4 0.6 slice_convert_fusion.3
  42.4 2.3 reduce-window.6
  45.3 53.4 %all-to-all-done.1 = bf16[64,16,512]{2,0,1:T(8,128)(2,1)S(1)} async-done(((bf16[64,16,512]{2,0,1:T(8,128)(2,1)}), bf16[64,16,512]{2,0,1:T(8,128)(2,1)S(1)}, u32[]{:S(2)}, u32[]{:S(2)}) %all-to-all-start.1) | async-done | bytes 1048608 | tf_op jit(solution)/shard_map/all_to_all | solution.py:154
  100.2 2.5 multiply_convert_fusion.3
  102.8 27.2 %all-gather.2.cloned.1.call-done = bf16[1024,2048]{1,0:T(8,128)(2,1)} async-done(((bf16[64,2048]{1,0:T(8,128)(2,1)}), bf16[1024,2048]{1,0:T(8,128)(2,1)}) %all-gather.2.cloned.1.call-update) | async-done | bytes 4194320 | tf_op jit(solution)/shard_map/all_gather | solution.py:152
  130.0 1.3 constant_dynamic-slice_fusion.5
  132.1 0.7 copy-done.4
  132.8 2.5 multiply_convert_fusion.4
  135.4 1.3 convolution_bitcast_fusion.3
  136.7 1.8 convolution_bitcast_fusion.2
  138.5 1.1 broadcast.48.clone.1
  139.6 28.1 %while.24 = (s32[]{:T(128)}, f32[8,512,64]{1,2,0:T(8,128)}, f32[1,512,512]{2,1,0:T(8,128)}, f32[8,1024]{1,0:T(8,128)S(1)}, f32[8,1024]{1,0:T(8,128)S(1)}, /*inde...) while((s32[]{:T(128)}, f32[8,512,64]{1,2,0:T(8,128)}, ...), condition=%wide.region_3.4_spmd.clone.clone, body=%wide.region_2.3_spmd.clone.clone.sunk | while | flops 35389444 | bytes 1259707 | solution.py:77
  139.6 0.6 dynamic_slice.82
  140.8 2.3 fusion.67
  144.4 2.3 fusion.67
  147.9 2.3 fusion.67
  151.4 2.3 fusion.67
  154.9 2.3 fusion.67
  158.4 2.3 fusion.67
  162.0 2.3 fusion.67
  165.5 2.3 fusion.67
  167.9 30.1 %while.25 = (s32[]{:T(128)}, f32[8,512,64]{1,2,0:T(8,128)S(1)}, f32[1,512,1024]{2,1,0:T(8,128)}, f32[8,1024]{1,0:T(8,128)S(1)}, f32[8,1024]{1,0:T(8,128)S(1)}, /...) while((s32[]{:T(128)}, f32[8,512,64]{1,2,0:T(8,128)S(1)}, ...), condition=%wide.region_5.6_spmd.clone.clone, body=%wide.region_4.5_spmd.clone.clone.sunk | while | flops 70778888 | bytes 2392283 | solution.py:77
  167.9 0.6 dynamic_slice.85
  169.2 2.4 fusion.70
  171.7 0.6 dynamic_slice.85
  173.0 2.4 fusion.70
  175.4 0.6 dynamic_slice.85
  176.8 2.4 fusion.70
  179.2 0.6 dynamic_slice.85
  180.5 2.4 fusion.70
  182.9 0.6 dynamic_slice.85
  184.3 2.4 fusion.70
  186.7 0.6 dynamic_slice.85
  188.0 2.4 fusion.70
  190.5 0.6 dynamic_slice.85
  191.8 2.4 fusion.70
  194.2 0.6 dynamic_slice.85
  195.6 2.4 fusion.70
  198.0 2.1 fusion.53
  200.1 1.4 fusion.51
  201.5 2.3 copy.94
  203.8 9.6 %all-to-all-start.2 = ((bf16[16,64,512]{2,1,0:T(8,128)(2,1)}), bf16[16,64,512]{2,1,0:T(8,128)(2,1)S(1)}, u32[]{:S(2)}, u32[]{:S(2)}) async-start(bf16[16,64,512]{2,1,0:T(8,128)(2,1)} %bitcast.36), calls=%async_computation.2 | async-start | bytes 2097152 | tf_op jit(solution)/shard_map/all_to_all | solution.py:173
  213.5 1.4 slice.142
  214.8 1.0 slice.143
  215.9 0.7 copy.98
  216.5 1.1 fusion.54
  217.6 2.6 copy.97
  220.2 3.4 %fusion.52 = f32[8,64,256]{2,1,0:T(8,128)} fusion(bf16[1024,8,64]{0,2,1:T(8,128)(2,1)S(1)} %bitcast.173, f32[1024,8]{0,1:T(8,128)S(1)} %get-tuple-element.300, f32[1024,256]{1,0:T(8,128)} %copy.97, f32[8,64,256]{2,1,0:T(8,128)S(1)} %copy-done.7, f32[8]{0:T(128)S(1)} %exp.34), kind=kOutput, calls=%fused_computation.78 | convolution fusion | flops 272891904 | bytes 3178528 | tf_op jit(solution)/shard_map/tghp,tghn->ghpn/dot_general | solution.py:104
  223.7 37.8 %all-to-all-done.2 = bf16[16,64,512]{2,1,0:T(8,128)(2,1)S(1)} async-done(((bf16[16,64,512]{2,1,0:T(8,128)(2,1)}), bf16[16,64,512]{2,1,0:T(8,128)(2,1)S(1)}, u32[]{:S(2)}, u32[]{:S(2)}) %all-to-all-start.2) | async-done | bytes 1048608 | tf_op jit(solution)/shard_map/all_to_all | solution.py:173
  262.7 1.2 copy.107
  263.9 1.2 multiply_convert_fusion.2
  (129 shorter events, 9.9 us)
Async XLA Ops:
  7.2 30.6 %copy-start = (bf16[3,2048]{1,0:T(4,128)(2,1)S(1)}, bf16[3,2048]{1,0:T(4,128)(2,1)}, u32[]{:S(2)}) copy-start(bf16[3,2048]{1,0:T(4,128)(2,1)} %param.22) | copy-start | bytes 36868
  7.2 122.8 %all-gather.2.cloned.1.call-start = ((), (), s32[]{:S(2)}) async-start(), calls=%async_computation.3 | async-start | bytes 4456448 | tf_op jit(solution)/shard_map/all_gather | solution.py:152
  9.5 21.9 %all-to-all-start = ((bf16[16,2,256]{2,1,0:T(2,128)(2,1)}), bf16[16,2,256]{2,1,0:T(2,128)(2,1)S(1)}, u32[]{:S(2)}, u32[]{:S(2)}) async-start(bf16[16,2,256]{2,1,0:T(2,128)(2,1)} %reshape.180), calls=%async_computation | async-start | bytes 32768 | tf_op jit(solution)/shard_map/all_to_all | solution.py:155
  22.4 14.0 %copy-start.28 = (bf16[512]{0:T(512)(128)(2,1)S(1)}, bf16[512]{0:T(512)(128)(2,1)}, u32[]{:S(2)}) copy-start(bf16[512]{0:T(512)(128)(2,1)} %param.24) | copy-start | bytes 3076
  22.4 14.6 %copy-start.30 = (f32[8]{0:T(128)S(1)}, f32[8]{0:T(128)}, u32[]{:S(2)}) copy-start(f32[8]{0:T(128)} %param.29) | copy-start | bytes 100
  22.4 15.5 %copy-start.22 = (bf16[3,512]{1,0:T(4,128)(2,1)S(1)}, bf16[3,512]{1,0:T(4,128)(2,1)}, u32[]{:S(2)}) copy-start(bf16[3,512]{1,0:T(4,128)(2,1)} %param.21) | copy-start | bytes 9220
  22.4 18.3 %copy-start.23 = (bf16[4,2048]{1,0:T(4,128)(2,1)S(1)}, bf16[4,2048]{1,0:T(4,128)(2,1)}, u32[]{:S(2)}) copy-start(bf16[4,2048]{1,0:T(4,128)(2,1)} %param.25) | copy-start | bytes 49156
  22.4 19.0 %copy-start.10 = (bf16[4,512]{1,0:T(4,128)(2,1)S(1)}, bf16[4,512]{1,0:T(4,128)(2,1)}, u32[]{:S(2)}) copy-start(bf16[4,512]{1,0:T(4,128)(2,1)} %param.23) | copy-start | bytes 12292
  24.8 17.5 %copy-start.24 = (f32[8]{0:T(128)S(1)}, f32[8]{0:T(128)}, u32[]{:S(2)}) copy-start(f32[8]{0:T(128)} %param.27) | copy-start | bytes 100
  24.8 17.5 %copy-start.29 = (f32[8]{0:T(128)S(1)}, f32[8]{0:T(128)}, u32[]{:S(2)}) copy-start(f32[8]{0:T(128)} %param.28) | copy-start | bytes 100
  31.3 67.4 %all-to-all-start.1 = ((bf16[64,16,512]{2,0,1:T(8,128)(2,1)}), bf16[64,16,512]{2,0,1:T(8,128)(2,1)S(1)}, u32[]{:S(2)}, u32[]{:S(2)}) async-start(bf16[64,16,512]{2,0,1:T(8,128)(2,1)} %bitcast.140), calls=%async_computation.1 | async-start | bytes 2097152 | tf_op jit(solution)/shard_map/all_to_all | solution.py:154
  45.2 53.5 %copy-start.25 = (f32[8]{0:T(128)}, f32[8]{0:T(128)S(1)}, u32[]{:S(2)}) copy-start(f32[8]{0:T(128)S(1)} %slice_reduce_fusion.1) | copy-start | bytes 100
  98.7 1.0 copy-start.5
  99.3 1.0 copy-start.8
  99.3 0.9 copy-start.17
  99.3 0.9 copy-start.18
  99.3 0.9 copy-start.19
  99.3 0.9 copy-start.20
  99.3 0.9 copy-start.21
  102.8 29.0 %copy-start.1 = (bf16[1024,512]{0,1:T(8,128)(2,1)}, bf16[1024,512]{0,1:T(8,128)(2,1)S(1)}, u32[]{:S(2)}) copy-start(bf16[1024,512]{0,1:T(8,128)(2,1)S(1)} %multiply_convert_fusion.3) | copy-start | bytes 3145732
  131.8 1.0 copy-start.4
  131.8 1.0 copy-start.12
  131.8 1.0 copy-start.13
  131.9 1.0 copy-start.14
  131.9 1.0 copy-start.15
  131.9 1.0 copy-start.16
  136.7 2.9 %slice-start = ((bf16[1024,512]{0,1:T(8,128)(2,1)}), bf16[512,512]{0,1:T(8,128)(2,1)S(1)}, s32[]{:S(2)}) async-start(bf16[1024,512]{0,1:T(8,128)(2,1)} %copy-done.1), calls=%async_computation.4 | async-start | bytes 1048576 | tf_op jit(solution)/shard_map/slice | solution.py:55
  139.6 28.3 %copy-start.2 = (bf16[1024,512]{0,1:T(8,128)(2,1)S(1)}, bf16[1024,512]{0,1:T(8,128)(2,1)}, u32[]{:S(2)}) copy-start(bf16[1024,512]{0,1:T(8,128)(2,1)} %copy-done.1) | copy-start | bytes 3145732
  139.6 28.3 %copy-start.27 = (s32[512]{0:T(512)S(1)}, s32[512]{0:T(512)}, u32[]{:S(2)}) copy-start(s32[512]{0:T(512)} %iota_add_fusion) | copy-start | bytes 6148
  198.0 2.1 copy-start.6
  198.0 2.1 copy-start.11
  201.5 11.9 %copy-start.9 = (bf16[8192]{0:T(1024)(128)(2,1)S(1)}, bf16[8192]{0:T(1024)(128)(2,1)}, u32[]{:S(2)}) copy-start(bf16[8192]{0:T(1024)(128)(2,1)} %param.30) | copy-start | bytes 49156
  201.5 11.9 %copy-start.26 = (f32[8]{0:T(128)S(1)}, f32[8]{0:T(128)}, u32[]{:S(2)}) copy-start(f32[8]{0:T(128)} %copy-done.25) | copy-start | bytes 100
  203.8 57.7 %all-to-all-start.2 = ((bf16[16,64,512]{2,1,0:T(8,128)(2,1)}), bf16[16,64,512]{2,1,0:T(8,128)(2,1)S(1)}, u32[]{:S(2)}, u32[]{:S(2)}) async-start(bf16[16,64,512]{2,1,0:T(8,128)(2,1)} %bitcast.36), calls=%async_computation.2 | async-start | bytes 2097152 | tf_op jit(solution)/shard_map/all_to_all | solution.py:173
  213.4 6.8 %copy-start.3 = (bf16[1024,512]{0,1:T(8,128)(2,1)S(1)}, bf16[1024,512]{0,1:T(8,128)(2,1)}, u32[]{:S(2)}) copy-start(bf16[1024,512]{0,1:T(8,128)(2,1)} %copy-done.1) | copy-start | bytes 3145732
  217.6 2.6 copy-start.7
Sparse Core Ops, SparseCore 0:
  10.1 119.8 all-gather.1
where the time goes:
time: 273 us; the launch traced here: 272 us
  waiting for transfers between devices  126 us (46%)
  matrix products  45.9 us (17%)
  local copies, waits for them, and re-layouts  31.2 us (11%)
  starting transfers between devices  27.6 us (10%)
  other arithmetic  16.3 us (6%)
  between operations  14.6 us (5%)
  loops' own time  10.8 us (4%)
    all_to_all x1, waiting for transfers between devices, local(): lax.all_to_all(x_send, 'tensor', split_axis=1, concat_axis=0, tiled=True)  53.4 us
    all_to_all x1, waiting for transfers between devices, local(): lax.all_to_all(mixed_y, 'tensor', split_axis=0, concat_axis=1, tiled=True)  37.8 us
    dot_general x16, matrix products, one_head(): return jnp.dot(weights, values, preferred_element_type=jnp.float32)  37.3 us
    all_gather x1, waiting for transfers between devices, local(): whole_bc = lax.all_gather(inner_bc, 'tensor', axis=0, tiled=True)  27.2 us
    all_to_all x1, starting transfers between devices, local(): lax.all_to_all(step_send, 'tensor', split_axis=1, concat_axis=0, tiled=True)  12.9 us
    another operation x2, loops' own time, state_mix(): lax.map(one_head, (jnp.arange(heads_here, dtype=jnp.int32), step_cols, ru...  10.8 us
    all_to_all x1, starting transfers between devices, local(): lax.all_to_all(mixed_y, 'tensor', split_axis=0, concat_axis=1, tiled=True)  9.57 us
    dynamic_slice x24, local copies, waits for them, and re-layouts, state_mix(): lax.map(one_head, (jnp.arange(heads_here, dtype=jnp.int32), step_cols, ru...  9.43 us
  transfers between devices with their start and end apart: 4, of which 4 were waited for; matrix products, arithmetic and copies ran while one was open for 10% of the time, Pallas kernels for 0%

commit v1 on v0

--- a/solution.py
+++ b/solution.py
@@ -1,7 +1,10 @@
+import functools
+
 import jax
 import jax.numpy as jnp
 from jax import lax
-from jax.sharding import PartitionSpec as P
+import numpy as np
+from jax.sharding import Mesh, PartitionSpec as P
 
 HEAD_DIM = 64
 STATE = 256
@@ -11,6 +14,7 @@
 
 
 EPSILON = 1e-05
+TENSOR = ("tg", "tj")
 
 
 def causal_conv(raw, state, weight, bias):
@@ -138,72 +142,82 @@
     skip_gain,
     norm_weight,
     scan_state,
+    *,
+    group_size,
+    tensor_count,
 ):
-    tensor_count = lax.axis_size("tensor")
-    device_rank = lax.axis_index("tensor")
+    device_rank = lax.axis_index("tg") * group_size + lax.axis_index("tj")
     token_rows = inner_x.shape[0]
     heads_here = step_bias.shape[0]
-    group_width = 2 * STATE
-    groups_here = max(1, GROUPS // tensor_count)
-    first_group = device_rank * GROUPS // tensor_count
-    column_start = first_group * group_width
-    x_send = inner_x.reshape(token_rows, tensor_count, heads_here * HEAD_DIM)
-    step_send = step_raw.reshape(token_rows, tensor_count, heads_here)
-    whole_bc = lax.all_gather(inner_bc, "tensor", axis=0, tiled=True)
-    head_x, head_step = (
-        lax.all_to_all(x_send, "tensor", split_axis=1, concat_axis=0, tiled=True),
-        lax.all_to_all(step_send, "tensor", split_axis=1, concat_axis=0, tiled=True),
-    )
-    head_bc = lax.dynamic_slice_in_dim(whole_bc, column_start, groups_here * group_width, 1)
-    length = head_x.shape[0]
-    head_x = head_x.reshape(length, heads_here * HEAD_DIM)
-    head_step = head_step.reshape(length, heads_here)
-    own_state_bc = lax.dynamic_slice_in_dim(
-        conv_state_bc, column_start, groups_here * group_width, 1
-    )
-    own_weight_bc = lax.dynamic_slice_in_dim(
-        conv_weight_bc, column_start, groups_here * group_width, 1
-    )
-    own_bias_bc = lax.dynamic_slice_in_dim(conv_bias_bc, column_start, groups_here * group_width, 0)
+    x_width = heads_here * HEAD_DIM
+    bc_width = inner_bc.shape[1] // tensor_count
+    x_send = jnp.transpose(inner_x.reshape(token_rows, tensor_count, x_width), (1, 0, 2))
+    bc_send = jnp.transpose(inner_bc.reshape(token_rows, tensor_count, bc_width), (1, 0, 2))
+    step_send = jnp.transpose(step_raw.reshape(token_rows, tensor_count, heads_here), (1, 0, 2))
+    send = jnp.concatenate(
+        [
+            x_send.reshape(tensor_count, -1),
+            bc_send.reshape(tensor_count, -1),
+            step_send.reshape(tensor_count, -1),
+        ],
+        axis=1,
+    )
+    recv = lax.all_to_all(send, TENSOR, 0, 0, tiled=True)
+    length = tensor_count * token_rows
+    x_end = token_rows * x_width
+    bc_end = x_end + token_rows * bc_width
+    head_x = recv[:, :x_end].reshape(length, x_width)
+    head_bc_part = recv[:, x_end:bc_end].reshape(length, bc_width)
+    head_step = recv[:, bc_end:].reshape(length, heads_here)
+    column_start = device_rank * bc_width
+    own_state_bc = lax.dynamic_slice_in_dim(conv_state_bc, column_start, bc_width, 1)
+    own_weight_bc = lax.dynamic_slice_in_dim(conv_weight_bc, column_start, bc_width, 1)
+    own_bias_bc = lax.dynamic_slice_in_dim(conv_bias_bc, column_start, bc_width, 0)
+    mixed_bc_part = causal_conv(head_bc_part, own_state_bc, own_weight_bc, own_bias_bc)
+    mixed_bc = lax.all_gather(mixed_bc_part, "tj", axis=1, tiled=True)
     mixed_x = causal_conv(head_x, conv_state_x, conv_weight_x, conv_bias_x)
-    mixed_bc = causal_conv(head_bc, own_state_bc, own_weight_bc, own_bias_bc)
     mixed_y, final_state = state_mix(
-        mixed_x, mixed_bc, head_step, step_bias, decay_rate, skip_gain, scan_state, groups_here
-    )
-    token_y = lax.all_to_all(mixed_y, "tensor", split_axis=0, concat_axis=1, tiled=True)
+        mixed_x, mixed_bc, head_step, step_bias, decay_rate, skip_gain, scan_state, 1
+    )
+    token_y = lax.all_to_all(mixed_y, TENSOR, split_axis=0, concat_axis=1, tiled=True)
     normed = group_norm(token_y, norm_weight)
     tail_x = head_x[length - CONV_K + 1 :]
-    columns_here = 2 * GROUPS * STATE // tensor_count
-    offset = device_rank * columns_here - column_start
-    tail_bc = lax.dynamic_slice_in_dim(head_bc[length - CONV_K + 1 :], offset, columns_here, 1)
+    tail_bc = head_bc_part[length - CONV_K + 1 :]
     return (normed, final_state, tail_x, tail_bc)
 
 
 def solution(mesh):
+    dp_count = mesh.shape["dp"]
+    tensor_count = mesh.shape["tensor"]
+    group_size = tensor_count // GROUPS
+    grouped = Mesh(
+        np.asarray(mesh.devices).reshape(dp_count, GROUPS, group_size), ("dp", "tg", "tj")
+    )
+    rows = ("dp",) + TENSOR
     return jax.shard_map(
-        local,
-        mesh=mesh,
+        functools.partial(local, group_size=group_size, tensor_count=tensor_count),
+        mesh=grouped,
         in_specs=(
-            P(("dp", "tensor"), None),
-            P(("dp", "tensor"), None),
-            P(("dp", "tensor"), None),
-            P("dp", "tensor"),
+            P(rows, None),
+            P(rows, None),
+            P(rows, None),
+            P("dp", TENSOR),
             P("dp", None),
-            P(None, "tensor"),
-            P("tensor"),
+            P(None, TENSOR),
+            P(TENSOR),
             P(),
             P(),
-            P("tensor"),
-            P("tensor"),
-            P("tensor"),
+            P(TENSOR),
+            P(TENSOR),
+            P(TENSOR),
             P(),
-            P(("dp", "tensor"), None, None),
+            P(rows, None, None),
         ),
         out_specs=(
-            P(("dp", "tensor"), None),
-            P(("dp", "tensor"), None, None),
-            P("dp", "tensor"),
-            P("dp", "tensor"),
+            P(rows, None),
+            P(rows, None, None),
+            P("dp", TENSOR),
+            P("dp", TENSOR),
         ),
         check_vma=False,
     )

time: 273 us -> 249 us (0.912)
  the two profiles are of different devices: /device:TPU:57 before, /device:TPU:65 now
where the time goes in v1:
time: 249 us; the launch traced here: 248 us
  waiting for transfers between devices  113 us (45%)
  local copies, waits for them, and re-layouts  39.5 us (16%)
  matrix products  31.5 us (13%)
  starting transfers between devices  22.7 us (9%)
  other arithmetic  15.3 us (6%)
  between operations  14.5 us (6%)
  loops' own time  10.8 us (4%)
    all_to_all x1, waiting for transfers between devices, local(): recv = lax.all_to_all(send, TENSOR, 0, 0, tiled=True)  58 us
    all_to_all x1, waiting for transfers between devices, local(): lax.all_to_all(mixed_y, TENSOR, split_axis=0, concat_axis=1, tiled=True)  39.6 us
    dot_general x16, matrix products, one_head(): return jnp.dot(weights, values, preferred_element_type=jnp.float32)  23.5 us
    all_gather x1, waiting for transfers between devices, local(): mixed_bc = lax.all_gather(mixed_bc_part, 'tj', axis=1, tiled=True)  15.7 us
    all_to_all x1, starting transfers between devices, local(): recv = lax.all_to_all(send, TENSOR, 0, 0, tiled=True)  12.5 us
    another operation x2, loops' own time, state_mix(): lax.map(one_head, (jnp.arange(heads_here, dtype=jnp.int32), step_cols, ru...  10.8 us
    all_to_all x1, starting transfers between devices, local(): lax.all_to_all(mixed_y, TENSOR, split_axis=0, concat_axis=1, tiled=True)  10.2 us
    unnamed x44, local copies, waits for them, and re-layouts  9.96 us
  transfers between devices with their start and end apart: 3, of which 3 were waited for; matrix products, arithmetic and copies ran while one was open for 9% of the time, Pallas kernels for 0%

profile of v1, /device:TPU:65, one launch (start us, length us, event | category | flops | bytes accessed | tf_op | source)
XLA Modules:
  0.0 247.7 jit_solution(4635555850143321165)
XLA Ops:
  7.2 0.9 copy.152
  8.7 0.6 copy.173
  9.4 0.5 broadcast.53
  9.9 1.7 reduce.7
  11.7 1.3 reshape.197
  12.9 12.5 %all-to-all-start = ((bf16[16,2,20736]{2,1,0:T(2,128)(2,1)}), bf16[16,2,20736]{2,1,0:T(2,128)(2,1)}, u32[]{:S(2)}, u32[]{:S(2)}) async-start(bf16[16,2,20736]{2,1,0:T(2,128)(2,1)} %reshape.197), calls=%async_computation | async-start | bytes 2654208 | tf_op jit(solution)/shard_map/all_to_all | solution.py:165
  25.6 0.8 dynamic-slice_convert_fusion.1
  26.4 0.7 constant_dynamic-slice_fusion.4
  27.1 0.7 dynamic-slice_convert_fusion
  27.8 58.0 %all-to-all-done = bf16[16,2,20736]{2,1,0:T(2,128)(2,1)} async-done(((bf16[16,2,20736]{2,1,0:T(2,128)(2,1)}), bf16[16,2,20736]{2,1,0:T(2,128)(2,1)}, u32[]{:S(2)}, u32[]{:S(2)}) %all-to-all-start) | async-done | bytes 1327136 | tf_op jit(solution)/shard_map/all_to_all | solution.py:165
  85.7 4.4 %reshape.198 = bf16[16,1,41472]{2,1,0:T(2,128)(2,1)S(1)} reshape(bf16[16,2,20736]{2,1,0:T(2,128)(2,1)} %all-to-all-done) | data formatting | bytes 2654208
  90.3 1.1 copy-done.5
  91.6 1.1 multiply_convert_fusion.6
  92.8 1.0 slice.147
  93.8 1.6 reshape.178
  96.1 2.3 reduce-window.6
  99.0 1.4 multiply_convert_fusion.3
  101.0 1.8 copy.163
  102.8 15.7 %all-gather.2.cloned.1.call-done = bf16[1024,512]{1,0:T(8,128)(2,1)} async-done(((bf16[1024,128]{1,0:T(8,128)(2,1)}), bf16[1024,512]{1,0:T(8,128)(2,1)}) %all-gather.2.cloned.1.call-update) | async-done | bytes 1048592 | tf_op jit(solution)/shard_map/all_gather | solution.py:177
  118.6 1.5 copy.156
  120.4 1.8 convolution_bitcast_fusion.2
  122.3 13.6 %while.24 = (s32[]{:T(128)}, f32[8,512,64]{1,2,0:T(8,128)S(1)}, f32[1,512,512]{2,1,0:T(8,128)S(1)}, f32[8,1024]{1,0:T(8,128)S(1)}, f32[8,1024]{1,0:T(8,128)S(1)}...) while((s32[]{:T(128)}, f32[8,512,64]{1,2,0:T(8,128)S(1)}, ...), condition=%wide.region_3.4_spmd.clone.clone, body=%wide.region_2.3_spmd.clone.clone.sunk | while | flops 35389444 | bytes 1325243 | solution.py:81
  122.3 0.6 dynamic_slice.73
  124.0 0.6 dynamic_slice.73
  125.7 0.6 dynamic_slice.73
  127.0 0.4 fusion.68
  127.4 0.6 dynamic_slice.73
  129.1 0.6 dynamic_slice.73
  130.8 0.6 dynamic_slice.73
  132.1 0.4 fusion.68
  132.5 0.6 dynamic_slice.73
  134.2 0.6 dynamic_slice.73
  135.5 0.4 fusion.68
  135.9 1.3 copy.159
  137.4 30.9 %while.25 = (s32[]{:T(128)}, f32[8,512,64]{1,2,0:T(8,128)S(1)}, f32[1,512,1024]{2,1,0:T(8,128)}, f32[8,1024]{1,0:T(8,128)S(1)}, f32[8,1024]{1,0:T(8,128)S(1)}, /...) while((s32[]{:T(128)}, f32[8,512,64]{1,2,0:T(8,128)S(1)}, ...), condition=%wide.region_5.6_spmd.clone.clone, body=%wide.region_4.5_spmd.clone.clone.sunk | while | flops 70778888 | bytes 2523355 | solution.py:81
  137.4 0.6 dynamic_slice.76
  138.7 2.5 %fusion.71 = f32[8,512,64]{1,2,0:T(8,128)S(1)} fusion(f32[8,512,64]{1,2,0:T(8,128)S(1)} %get-tuple-element.426, s32[]{:T(128)S(6)} %copy.197, f32[1,512,1024]{2,1,0:T(8,128)} %get-tuple-element.440, s32[512]{0:T(512)S(1)} %get-tuple-element.445, f32[1024]{0:T(1024)S(1)} %bitcast.197, f32[1024]{0:T(1024)S(1)} %bitcast.198, f32[512]{0:T(512)S(1)} %bitcast.201, ...), kind=kOutput, calls=%fused_computation.28.clone.1 | convolution fusion | flops 70778880 | bytes 2502664 | tf_op jit(solution)/shard_map/while/body/eval_jaxpr/dot_general | solution.py:79
  141.3 0.6 dynamic_slice.76
  142.6 2.5 %fusion.71 = f32[8,512,64]{1,2,0:T(8,128)S(1)} fusion(f32[8,512,64]{1,2,0:T(8,128)S(1)} %get-tuple-element.426, s32[]{:T(128)S(6)} %copy.197, f32[1,512,1024]{2,1,0:T(8,128)} %get-tuple-element.440, s32[512]{0:T(512)S(1)} %get-tuple-element.445, f32[1024]{0:T(1024)S(1)} %bitcast.197, f32[1024]{0:T(1024)S(1)} %bitcast.198, f32[512]{0:T(512)S(1)} %bitcast.201, ...), kind=kOutput, calls=%fused_computation.28.clone.1 | convolution fusion | flops 70778880 | bytes 2502664 | tf_op jit(solution)/shard_map/while/body/eval_jaxpr/dot_general | solution.py:79
  145.1 0.6 dynamic_slice.76
  146.5 2.5 %fusion.71 = f32[8,512,64]{1,2,0:T(8,128)S(1)} fusion(f32[8,512,64]{1,2,0:T(8,128)S(1)} %get-tuple-element.426, s32[]{:T(128)S(6)} %copy.197, f32[1,512,1024]{2,1,0:T(8,128)} %get-tuple-element.440, s32[512]{0:T(512)S(1)} %get-tuple-element.445, f32[1024]{0:T(1024)S(1)} %bitcast.197, f32[1024]{0:T(1024)S(1)} %bitcast.198, f32[512]{0:T(512)S(1)} %bitcast.201, ...), kind=kOutput, calls=%fused_computation.28.clone.1 | convolution fusion | flops 70778880 | bytes 2502664 | tf_op jit(solution)/shard_map/while/body/eval_jaxpr/dot_general | solution.py:79
  149.0 0.6 dynamic_slice.76
  150.3 2.5 %fusion.71 = f32[8,512,64]{1,2,0:T(8,128)S(1)} fusion(f32[8,512,64]{1,2,0:T(8,128)S(1)} %get-tuple-element.426, s32[]{:T(128)S(6)} %copy.197, f32[1,512,1024]{2,1,0:T(8,128)} %get-tuple-element.440, s32[512]{0:T(512)S(1)} %get-tuple-element.445, f32[1024]{0:T(1024)S(1)} %bitcast.197, f32[1024]{0:T(1024)S(1)} %bitcast.198, f32[512]{0:T(512)S(1)} %bitcast.201, ...), kind=kOutput, calls=%fused_computation.28.clone.1 | convolution fusion | flops 70778880 | bytes 2502664 | tf_op jit(solution)/shard_map/while/body/eval_jaxpr/dot_general | solution.py:79
  152.9 0.6 dynamic_slice.76
  154.2 2.5 %fusion.71 = f32[8,512,64]{1,2,0:T(8,128)S(1)} fusion(f32[8,512,64]{1,2,0:T(8,128)S(1)} %get-tuple-element.426, s32[]{:T(128)S(6)} %copy.197, f32[1,512,1024]{2,1,0:T(8,128)} %get-tuple-element.440, s32[512]{0:T(512)S(1)} %get-tuple-element.445, f32[1024]{0:T(1024)S(1)} %bitcast.197, f32[1024]{0:T(1024)S(1)} %bitcast.198, f32[512]{0:T(512)S(1)} %bitcast.201, ...), kind=kOutput, calls=%fused_computation.28.clone.1 | convolution fusion | flops 70778880 | bytes 2502664 | tf_op jit(solution)/shard_map/while/body/eval_jaxpr/dot_general | solution.py:79
  156.7 0.6 dynamic_slice.76
  158.1 2.5 %fusion.71 = f32[8,512,64]{1,2,0:T(8,128)S(1)} fusion(f32[8,512,64]{1,2,0:T(8,128)S(1)} %get-tuple-element.426, s32[]{:T(128)S(6)} %copy.197, f32[1,512,1024]{2,1,0:T(8,128)} %get-tuple-element.440, s32[512]{0:T(512)S(1)} %get-tuple-element.445, f32[1024]{0:T(1024)S(1)} %bitcast.197, f32[1024]{0:T(1024)S(1)} %bitcast.198, f32[512]{0:T(512)S(1)} %bitcast.201, ...), kind=kOutput, calls=%fused_computation.28.clone.1 | convolution fusion | flops 70778880 | bytes 2502664 | tf_op jit(solution)/shard_map/while/body/eval_jaxpr/dot_general | solution.py:79
  160.6 0.6 dynamic_slice.76
  161.9 2.5 %fusion.71 = f32[8,512,64]{1,2,0:T(8,128)S(1)} fusion(f32[8,512,64]{1,2,0:T(8,128)S(1)} %get-tuple-element.426, s32[]{:T(128)S(6)} %copy.197, f32[1,512,1024]{2,1,0:T(8,128)} %get-tuple-element.440, s32[512]{0:T(512)S(1)} %get-tuple-element.445, f32[1024]{0:T(1024)S(1)} %bitcast.197, f32[1024]{0:T(1024)S(1)} %bitcast.198, f32[512]{0:T(512)S(1)} %bitcast.201, ...), kind=kOutput, calls=%fused_computation.28.clone.1 | convolution fusion | flops 70778880 | bytes 2502664 | tf_op jit(solution)/shard_map/while/body/eval_jaxpr/dot_general | solution.py:79
  164.5 0.6 dynamic_slice.76
  165.8 2.5 %fusion.71 = f32[8,512,64]{1,2,0:T(8,128)S(1)} fusion(f32[8,512,64]{1,2,0:T(8,128)S(1)} %get-tuple-element.426, s32[]{:T(128)S(6)} %copy.197, f32[1,512,1024]{2,1,0:T(8,128)} %get-tuple-element.440, s32[512]{0:T(512)S(1)} %get-tuple-element.445, f32[1024]{0:T(1024)S(1)} %bitcast.197, f32[1024]{0:T(1024)S(1)} %bitcast.198, f32[512]{0:T(512)S(1)} %bitcast.201, ...), kind=kOutput, calls=%fused_computation.28.clone.1 | convolution fusion | flops 70778880 | bytes 2502664 | tf_op jit(solution)/shard_map/while/body/eval_jaxpr/dot_general | solution.py:79
  168.3 1.3 copy.160
  169.6 2.2 fusion.52
  171.8 1.8 copy.162
  173.7 4.8 %fusion.42 = bf16[1024,512]{1,0:T(8,128)(2,1)} fusion(f32[512,512]{1,0:T(8,128)} %copy.160, f32[512,512]{1,0:T(8,128)} %copy.159, bf16[1024,512]{1,0:T(8,128)(2,1)S(1)} %get-tuple-element.485, f32[1024,512]{1,0:T(8,128)} %copy.162, f32[1024,512]{1,0:T(8,128)} %copy.163, f32[512]{0:T(512)S(1)} %mul.284), kind=kLoop, calls=%fused_computation.55 | loop fusion | flops 3670016 | bytes 8390656 | tf_op jit(solution)/shard_map/convert_element_type | solution.py:102
  178.4 10.2 %all-to-all-start.1 = ((bf16[16,64,512]{2,1,0:T(8,128)(2,1)}), bf16[16,64,512]{2,1,0:T(8,128)(2,1)S(1)}, u32[]{:S(2)}, u32[]{:S(2)}) async-start(bf16[16,64,512]{2,1,0:T(8,128)(2,1)} %bitcast.184), calls=%async_computation.1 | async-start | bytes 2097152 | tf_op jit(solution)/shard_map/all_to_all | solution.py:182
  188.7 1.2 slice.158
  189.9 1.3 slice.157
  191.2 1.3 copy.166
  192.6 1.3 copy.167
  193.9 3.8 %fusion.43 = f32[8,64,256]{2,1,0:T(8,128)} fusion(bf16[1024,8,64]{0,2,1:T(8,128)(2,1)} %bitcast.190, f32[1024,8]{0,1:T(8,128)S(1)} %get-tuple-element.299, f32[1024,256]{1,0:T(8,128)} %copy.167, f32[8,64,256]{2,1,0:T(8,128)S(1)} %copy-done.8, f32[8]{0:T(128)S(1)} %exp.35), kind=kOutput, calls=%fused_computation.62 | convolution fusion | flops 272891904 | bytes 3178528 | tf_op jit(solution)/shard_map/tghp,tghn->ghpn/dot_general | solution.py:108
  197.7 39.6 %all-to-all-done.1 = bf16[16,64,512]{2,1,0:T(8,128)(2,1)S(1)} async-done(((bf16[16,64,512]{2,1,0:T(8,128)(2,1)}), bf16[16,64,512]{2,1,0:T(8,128)(2,1)S(1)}, u32[]{:S(2)}, u32[]{:S(2)}) %all-to-all-start.1) | async-done | bytes 1048608 | tf_op jit(solution)/shard_map/all_to_all | solution.py:182
  238.5 1.2 copy.176
  239.7 1.2 multiply_convert_fusion.2
  (113 shorter events, 8.1 us)
Async XLA Ops:
  7.2 1.2 copy-start
  7.2 1.4 copy-start.10
  11.6 13.8 %copy-start.15 = (bf16[512]{0:T(512)(128)(2,1)S(1)}, bf16[512]{0:T(512)(128)(2,1)}, u32[]{:S(2)}) copy-start(bf16[512]{0:T(512)(128)(2,1)} %param.24) | copy-start | bytes 3076
  11.6 13.8 %copy-start.17 = (f32[8]{0:T(128)S(1)}, f32[8]{0:T(128)}, u32[]{:S(2)}) copy-start(f32[8]{0:T(128)} %param.29) | copy-start | bytes 100
  11.6 14.0 %copy-start.13 = (bf16[3,512]{1,0:T(4,128)(2,1)S(1)}, bf16[3,512]{1,0:T(4,128)(2,1)}, u32[]{:S(2)}) copy-start(bf16[3,512]{1,0:T(4,128)(2,1)} %param.21) | copy-start | bytes 9220
  11.6 16.1 %copy-start.12 = (bf16[4,512]{1,0:T(4,128)(2,1)S(1)}, bf16[4,512]{1,0:T(4,128)(2,1)}, u32[]{:S(2)}) copy-start(bf16[4,512]{1,0:T(4,128)(2,1)} %param.23) | copy-start | bytes 12292
  12.9 72.8 %all-to-all-start = ((bf16[16,2,20736]{2,1,0:T(2,128)(2,1)}), bf16[16,2,20736]{2,1,0:T(2,128)(2,1)}, u32[]{:S(2)}, u32[]{:S(2)}) async-start(bf16[16,2,20736]{2,1,0:T(2,128)(2,1)} %reshape.197), calls=%async_computation | async-start | bytes 2654208 | tf_op jit(solution)/shard_map/all_to_all | solution.py:165
  25.4 93.2 %all-gather.2.cloned.1.call-start = ((), (), s32[]{:S(2)}) async-start(), calls=%async_computation.2 | async-start | bytes 1310720 | tf_op jit(solution)/shard_map/all_gather | solution.py:177
  90.3 1.1 copy-start.5
  91.4 1.4 copy-start.6
  91.5 3.9 %copy-start.9 = (bf16[1024,128]{1,0:T(8,128)(2,1)}, bf16[1024,128]{1,0:T(8,128)(2,1)S(1)}, u32[]{:S(2)}) copy-start(bf16[1024,128]{1,0:T(8,128)(2,1)S(1)} %reshape.172) | copy-start | bytes 786436
  93.8 2.1 copy-start.14
  93.8 2.1 copy-start.16
  95.4 3.6 %copy-start.7 = (bf16[1024,512]{1,0:T(8,128)(2,1)}, bf16[1024,512]{1,0:T(8,128)(2,1)S(1)}, u32[]{:S(2)}) copy-start(bf16[1024,512]{1,0:T(8,128)(2,1)S(1)} %reshape.178) | copy-start | bytes 3145732
  100.4 2.4 copy-start.1
  120.1 2.1 copy-start.3
  120.4 1.9 slice-start
  135.9 1.5 copy-start.2
  178.4 10.2 %copy-start.11 = (bf16[8192]{0:T(1024)(128)(2,1)S(1)}, bf16[8192]{0:T(1024)(128)(2,1)}, u32[]{:S(2)}) copy-start(bf16[8192]{0:T(1024)(128)(2,1)} %param.30) | copy-start | bytes 49156
  178.4 14.0 %copy-start.4 = (bf16[1024,512]{0,1:T(8,128)(2,1)S(1)}, bf16[1024,512]{0,1:T(8,128)(2,1)}, u32[]{:S(2)}) copy-start(bf16[1024,512]{0,1:T(8,128)(2,1)} %copy-done.3) | copy-start | bytes 3145732
  178.4 58.8 %all-to-all-start.1 = ((bf16[16,64,512]{2,1,0:T(8,128)(2,1)}), bf16[16,64,512]{2,1,0:T(8,128)(2,1)S(1)}, u32[]{:S(2)}, u32[]{:S(2)}) async-start(bf16[16,64,512]{2,1,0:T(8,128)(2,1)} %bitcast.184), calls=%async_computation.1 | async-start | bytes 2097152 | tf_op jit(solution)/shard_map/all_to_all | solution.py:182
  192.6 1.3 copy-start.8
Sparse Core Ops, SparseCore 0:
  92.8 25.7 all-gather.1

commit v2 on v1

v2 whole, which is shorter than its diff:
```python
import functools

import jax
import jax.numpy as jnp
from jax import lax
import numpy as np
from jax.sharding import Mesh, PartitionSpec as P

HEAD_DIM = 64
STATE = 256
GROUPS = 4
CONV_K = 4
INNER = 8192


EPSILON = 1e-05
TENSOR = ("tg", "tj")


def causal_conv(raw, state, weight, bias):
    length = raw.shape[0]
    padded = jnp.concatenate([state.astype(jnp.float32), raw.astype(jnp.float32)], axis=0)
    total = jnp.zeros(raw.shape, jnp.float32) + bias.astype(jnp.float32)[None, :]
    for kernel_tap in range(CONV_K):
        total = (
            total
            + weight[kernel_tap].astype(jnp.float32)[None, :]
            * padded[kernel_tap : kernel_tap + length]
        )
    return jax.nn.silu(total).astype(jnp.bfloat16)


def group_norm(mixed_y, norm_weight):
    rows = mixed_y.shape[0]
    values = mixed_y.astype(jnp.float32).reshape(rows, GROUPS, INNER // GROUPS)
    mean_square = jnp.mean(values * values, axis=2, keepdims=True)
    scaled = (values * lax.rsqrt(mean_square + EPSILON)).reshape(rows, INNER)
    return (scaled * norm_weight.astype(jnp.float32)[None, :]).astype(jnp.bfloat16)


def local(
    inner_x,
    inner_bc,
    step_raw,
    conv_state_x,
    conv_state_bc,
    conv_weight_x,
    conv_bias_x,
    conv_weight_bc,
    conv_bias_bc,
    step_bias,
    decay_rate,
    skip_gain,
    norm_weight,
    scan_state,
    *,
    group_size,
    tensor_count,
):
    device_rank = lax.axis_index("tg") * group_size + lax.axis_index("tj")
    token_rows = inner_x.shape[0]
    heads_here = step_bias.shape[0]
    x_width = heads_here * HEAD_DIM
    bc_width = inner_bc.shape[1] // tensor_count
    length = tensor_count * token_rows

    bc_send = jnp.transpose(inner_bc.reshape(token_rows, tensor_count, bc_width), (1, 0, 2))
    step_send = jnp.transpose(step_raw.reshape(token_rows, tensor_count, heads_here), (1, 0, 2))
    small_send = jnp.concatenate(
        [bc_send.reshape(tensor_count, -1), step_send.reshape(tensor_count, -1)], axis=1
    )
    small_recv = lax.all_to_all(small_send, TENSOR, 0, 0, tiled=True)
    bc_end = token_rows * bc_width
    head_bc_part = small_recv[:, :bc_end].reshape(length, bc_width)
    head_step = small_recv[:, bc_end:].reshape(length, heads_here)

    x_send = jnp.transpose(inner_x.reshape(token_rows, tensor_count, x_width), (1, 0, 2))
    x_recv = lax.all_to_all(x_send, TENSOR, 0, 0, tiled=True)
    head_x = x_recv.reshape(length, x_width)

    column_start = device_rank * bc_width
    own_state_bc = lax.dynamic_slice_in_dim(conv_state_bc, column_start, bc_width, 1)
    own_weight_bc = lax.dynamic_slice_in_dim(conv_weight_bc, column_start, bc_width, 1)
    own_bias_bc = lax.dynamic_slice_in_dim(conv_bias_bc, column_start, bc_width, 0)
    mixed_bc_part = causal_conv(head_bc_part, own_state_bc, own_weight_bc, own_bias_bc)
    mixed_bc = lax.all_gather(mixed_bc_part, "tj", axis=1, tiled=True)
    input_map = mixed_bc[:, :STATE]
    output_map = mixed_bc[:, STATE:]

    step_size = jax.nn.softplus(head_step.astype(jnp.float32) + step_bias[None, :])
    running = jnp.cumsum(-step_size * decay_rate[None, :], axis=0)
    step_cols = jnp.transpose(step_size)
    running_cols = jnp.transpose(running)

    mixed_x = causal_conv(head_x, conv_state_x, conv_weight_x, conv_bias_x)
    values = mixed_x.reshape(length, heads_here, HEAD_DIM)

    query_rows = min(256, length)
    pieces = []
    for row_start in range(0, length, query_rows):
        row_stop = row_start + query_rows
        scores = jnp.einsum(
            "tn,sn->ts",
            output_map[row_start:row_stop],
            input_map[:row_stop],
            preferred_element_type=jnp.float32,
        )
        causal = row_start + lax.broadcasted_iota(
            jnp.int32, (query_rows, row_stop), 0
        ) >= lax.broadcasted_iota(jnp.int32, (query_rows, row_stop), 1)
        log_gap = running_cols[:, row_start:row_stop, None] - running_cols[:, None, :row_stop]
        decayed = jnp.exp(jnp.where(causal[None], log_gap, 0.0))
        weights = jnp.where(
            causal[None], scores[None] * decayed * step_cols[:, None, :row_stop], 0.0
        ).astype(jnp.bfloat16)
        weights = lax.optimization_barrier(weights)
        pieces.append(
            jnp.einsum(
                "hts,shp->thp", weights, values[:row_stop], preferred_element_type=jnp.float32
            )
        )
    local_all = jnp.concatenate(pieces, axis=0)
    carried = jnp.einsum(
        "tn,hpn->thp",
        output_map.astype(jnp.float32),
        scan_state,
        precision=lax.Precision.HIGHEST,
    )
    carried = carried * jnp.exp(running)[:, :, None]
    channels = values.astype(jnp.float32)
    mixed = local_all + carried + skip_gain[None, :, None] * channels
    mixed_y = mixed.reshape(length, x_width).astype(jnp.bfloat16)
    tail_decay = jnp.exp(running[length - 1][None, :] - running) * step_size
    weighted = (input_map.astype(jnp.float32)[:, None, :] * tail_decay[:, :, None]).astype(
        jnp.bfloat16
    )
    gathered_in = jnp.einsum(
        "shp,shn->hpn", values, weighted, preferred_element_type=jnp.float32
    )
    final_state = jnp.exp(running[length - 1])[:, None, None] * scan_state + gathered_in

    token_y = lax.all_to_all(mixed_y, TENSOR, split_axis=0, concat_axis=1, tiled=True)
    normed = group_norm(token_y, norm_weight)
    tail_x = head_x[length - CONV_K + 1 :]
    tail_bc = head_bc_part[length - CONV_K + 1 :]
    return (normed, final_state, tail_x, tail_bc)


def solution(mesh):
    dp_count = mesh.shape["dp"]
    tensor_count = mesh.shape["tensor"]
    group_size = tensor_count // GROUPS
    grouped = Mesh(
        np.asarray(mesh.devices).reshape(dp_count, GROUPS, group_size), ("dp", "tg", "tj")
    )
    rows = ("dp",) + TENSOR
    return jax.shard_map(
        functools.partial(local, group_size=group_size, tensor_count=tensor_count),
        mesh=grouped,
        in_specs=(
            P(rows, None),
            P(rows, None),
            P(rows, None),
            P("dp", TENSOR),
            P("dp", None),
            P(None, TENSOR),
            P(TENSOR),
            P(),
            P(),
            P(TENSOR),
            P(TENSOR),
            P(TENSOR),
            P(),
            P(rows, None, None),
        ),
        out_specs=(
            P(rows, None),
            P(rows, None, None),
            P("dp", TENSOR),
            P("dp", TENSOR),
        ),
        check_vma=False,
    )
```

time: 249 us -> 202 us (0.81)
  matrix products: 31.5 us -> 13.2 us
  waiting for transfers between devices: 113 us -> 98.2 us
  local copies, waits for them, and re-layouts: 39.5 us -> 25.7 us
  loops' own time: 10.8 us -> 0 us
  other arithmetic: 15.3 us -> 22.3 us
  starting transfers between devices: 22.7 us -> 26.9 us
    all_to_all x1 -> x2, waiting for transfers between devices: 58 us -> 11.2 us  [the longest x1 11.2 us: local(): small_recv = lax.all_to_all(small_send, TENSOR, 0, 0, tiled=True)]
    all_gather x1, waiting for transfers between devices: 15.7 us -> 44.4 us  [local(): mixed_bc = lax.all_gather(mixed_bc_part, 'tj', axis=1, tiled=True)]
    dot_general x20 -> x10, matrix products: 31.5 us -> 13.2 us  [the longest x4 6.29 us: local(): jnp.einsum('hts,shp->thp', weights, values[:row_stop], preferred_element_...]
    another operation x2 -> x0, loops' own time: 10.8 us -> none  [state_mix(): lax.map(one_head, (jnp.arange(heads_here, dtype=jnp.int32), step_cols, ru...]
    dynamic_slice x24 -> x0, local copies, waits for them, and re-layouts: 9.47 us -> none  [state_mix(): lax.map(one_head, (jnp.arange(heads_here, dtype=jnp.int32), step_cols, ru...]
    slice x22 -> x16, local copies, waits for them, and re-layouts: 2.15 us -> 8.91 us  [the longest x7 6.15 us: local(): values[:row_stop]]
    all_to_all x1 -> x2, starting transfers between devices: 12.5 us -> 19.2 us  [the longest x1 12.5 us: local(): small_recv = lax.all_to_all(small_send, TENSOR, 0, 0, tiled=True)]
    convert_element_type x2 -> x6, other arithmetic: 4.76 us -> 9.69 us  [the longest x4 9.62 us: local(): weights = jnp.where(causal[None], scores[None] * decayed * step_cols[:, N...]
  transfers between devices with their start and end apart: 3 -> 4, of which waited for: 3 -> 3; matrix products, arithmetic and copies ran while one was open for 9% -> 16% of each run, Pallas kernels for 0% -> 0%
where the time goes in v2:
time: 202 us; the launch traced here: 201 us
  waiting for transfers between devices  98.2 us (49%)
  starting transfers between devices  26.9 us (13%)
  local copies, waits for them, and re-layouts  25.7 us (13%)
  other arithmetic  22.3 us (11%)
  between operations  14.7 us (7%)
  matrix products  13.2 us (7%)
    all_gather x1, waiting for transfers between devices, local(): mixed_bc = lax.all_gather(mixed_bc_part, 'tj', axis=1, tiled=True)  44.4 us
    all_to_all x1, waiting for transfers between devices, local(): lax.all_to_all(mixed_y, TENSOR, split_axis=0, concat_axis=1, tiled=True)  42.6 us
    all_to_all x1, starting transfers between devices, local(): small_recv = lax.all_to_all(small_send, TENSOR, 0, 0, tiled=True)  12.5 us
    all_to_all x1, waiting for transfers between devices, local(): small_recv = lax.all_to_all(small_send, TENSOR, 0, 0, tiled=True)  11.2 us
    convert_element_type x4, other arithmetic, local(): weights = jnp.where(causal[None], scores[None] * decayed * step_cols[:, N...  9.62 us
    all_to_all x1, starting transfers between devices, local(): lax.all_to_all(mixed_y, TENSOR, split_axis=0, concat_axis=1, tiled=True)  7.68 us
    all_to_all x1, starting transfers between devices, local(): x_recv = lax.all_to_all(x_send, TENSOR, 0, 0, tiled=True)  6.74 us
    dot_general x4, matrix products, local(): jnp.einsum('hts,shp->thp', weights, values[:row_stop], preferred_element_...  6.29 us
  transfers between devices with their start and end apart: 4, of which 3 were waited for; matrix products, arithmetic and copies ran while one was open for 16% of the time, Pallas kernels for 0%

profile of v2, /device:TPU:65, one launch (start us, length us, event | category | flops | bytes accessed | tf_op | source)
XLA Modules:
  0.0 201.1 jit_solution(4179824089006635973)
XLA Ops:
  7.2 0.9 copy.149
  8.7 0.5 broadcast.77
  9.2 0.8 reduce.7
  10.0 0.8 reshape.183
  10.8 12.5 %all-to-all-start.1 = ((bf16[16,2,4352]{2,1,0:T(2,128)(2,1)}), bf16[16,2,4352]{2,1,0:T(2,128)(2,1)S(1)}, u32[]{:S(2)}, u32[]{:S(2)}) async-start(bf16[16,2,4352]{2,1,0:T(2,128)(2,1)} %reshape.183), calls=%async_computation.1 | async-start | bytes 557056 | tf_op jit(solution)/shard_map/all_to_all | solution.py:72
  23.3 0.7 dynamic-slice_convert_fusion
  24.0 0.7 constant_dynamic-slice_fusion
  24.7 0.8 dynamic-slice_convert_fusion.1
  25.4 1.1 copy.180
  26.5 0.5 convert_element_type.96
  27.1 0.7 iota_compare_fusion.3
  27.9 0.2 iota_compare_fusion.1
  28.0 0.2 iota_compare_fusion
  28.3 11.2 %all-to-all-done.1 = bf16[16,2,4352]{2,1,0:T(2,128)(2,1)S(1)} async-done(((bf16[16,2,4352]{2,1,0:T(2,128)(2,1)}), bf16[16,2,4352]{2,1,0:T(2,128)(2,1)S(1)}, u32[]{:S(2)}, u32[]{:S(2)}) %all-to-all-start.1) | async-done | bytes 278560 | tf_op jit(solution)/shard_map/all_to_all | solution.py:72
  39.4 6.7 %all-to-all-start = ((bf16[16,64,512]{2,1,0:T(8,128)(2,1)}), bf16[16,64,512]{2,1,0:T(8,128)(2,1)S(1)}, u32[]{:S(2)}, u32[]{:S(2)}) async-start(bf16[16,64,512]{2,1,0:T(8,128)(2,1)} %bitcast.97), calls=%async_computation | async-start | bytes 2097152 | tf_op jit(solution)/shard_map/all_to_all | solution.py:78
  46.2 0.3 reshape.184
  46.8 1.1 multiply_convert_fusion.6
  47.9 0.6 slice_convert_fusion.5
  48.5 0.3 reshape.177
  49.1 2.3 %reduce-window.6 = f32[8,8,128]{2,1,0:T(8,128)S(1)} reduce-window(f32[8,8,128]{2,1,0:T(8,128)S(1)} %copy.154, f32[]{:T(128)} %constant.32.clone.1), window={size=1x1x128 pad=0_0x0_0x127_0}, to_apply=%region_0.1 | reduce-window | flops 1040384 | bytes 65540 | tf_op jit(solution)/shard_map/reduce-window
  51.8 0.2 slice_reduce_fusion.1
  52.0 0.7 exponential_multiply_fusion
  52.7 0.6 slice.210
  53.3 0.6 slice.209
  53.9 0.6 slice.204
  54.5 0.6 fusion.39
  55.1 44.4 %all-gather.2.cloned.1.call-done = bf16[1024,512]{1,0:T(8,128)(2,1)} async-done(((bf16[1024,128]{1,0:T(8,128)(2,1)}), bf16[1024,512]{1,0:T(8,128)(2,1)}) %all-gather.2.cloned.1.call-update) | async-done | bytes 1048592 | tf_op jit(solution)/shard_map/all_gather | solution.py:86
  99.5 1.4 fusion.25
  101.0 3.7 %select_convert_fusion = bf16[8,256,1024]{2,1,0:T(8,128)(2,1)} fusion(f32[8,1024]{1,0:T(8,128)S(1)} %get-tuple-element.5, f32[8,1024]{1,0:T(8,128)S(1)} %bitcast.122, f32[8,256]{1,0:T(8,128)S(1)} %get-tuple-element.10, f32[256,1024]{1,0:T(8,128)S(1)} %fusion.25, pred[256,1024]{1,0:T(8,128)(4,1)S(1)} %iota_compare_fusion), kind=kLoop, calls=%fused_computation.1 | loop fusion | flops 12582912 | bytes 5578752 | tf_op jit(solution)/shard_map/convert_element_type | solution.py:115
  104.7 0.3 fusion.27
  105.0 3.0 %select_convert_fusion.1 = bf16[8,256,768]{2,1,0:T(8,128)(2,1)} fusion(f32[8,768]{1,0:T(8,128)S(1)} %slice.216, f32[8,768]{1,0:T(8,128)S(1)} %slice.215, f32[8,256]{1,0:T(8,128)S(1)} %get-tuple-element.11, f32[256,768]{1,0:T(8,128)S(1)} %fusion.27, pred[256,768]{1,0:T(8,128)(4,1)S(1)} %iota_compare_fusion.1), kind=kLoop, calls=%fused_computation.2 | loop fusion | flops 9437184 | bytes 4186112 | tf_op jit(solution)/shard_map/convert_element_type | solution.py:115
  108.1 0.3 fusion.29
  108.3 1.3 select_convert_fusion.2
  109.6 0.2 fusion.34
  109.9 1.6 select_convert_fusion.3
  111.6 0.3 bitcast_convert_fusion.4
  111.9 0.7 copy-done.6
  112.6 1.4 multiply_convert_fusion.3
  114.0 1.4 copy.157
  115.4 1.0 slice.211
  116.4 0.8 slice.205
  117.2 1.4 copy.156
  118.7 2.1 %copy.155 = bf16[512,512]{0,1:T(8,128)(2,1)} copy(bf16[512,512]{1,0:T(8,128)(2,1)} %slice.205) | data formatting | bytes 1048576 | tf_op jit(solution)/shard_map/slice | solution.py:119
  120.7 0.8 copy.147
  121.6 4.0 %convolution_bitcast_fusion.3 = f32[256,8,64]{0,2,1:T(8,128)S(1)} fusion(bf16[1024,8,64]{0,2,1:T(8,128)(2,1)} %bitcast.107, bf16[8,256,1024]{2,1,0:T(8,128)(2,1)} %select_convert_fusion), kind=kOutput, calls=%fused_computation.32 | convolution fusion | flops 268435456 | bytes 5767168 | tf_op jit(solution)/shard_map/hts,shp->thp/dot_general | solution.py:118
  125.6 1.1 convolution_bitcast_fusion
  126.8 0.7 convolution_bitcast_fusion.1
  127.5 0.4 copy-done.7
  128.0 0.4 convolution_bitcast_fusion.2
  128.4 0.2 copy-done.8
  128.8 1.4 fusion.14
  130.2 1.3 reshape.180
  131.5 2.7 %copy.161 = bf16[16,64,512]{2,1,0:T(8,128)(2,1)} copy(bf16[16,64,512]{1,0,2:T(8,128)(2,1)S(1)} %reshape.180) | data formatting | bytes 2097152 | tf_op jit(solution)/shard_map/convert_element_type | solution.py:132
  134.2 7.7 %all-to-all-start.2 = ((bf16[16,64,512]{2,1,0:T(8,128)(2,1)}), bf16[16,64,512]{2,1,0:T(8,128)(2,1)S(1)}, u32[]{:S(2)}, u32[]{:S(2)}) async-start(bf16[16,64,512]{2,1,0:T(8,128)(2,1)} %copy.161), calls=%async_computation.2 | async-start | bytes 2097152 | tf_op jit(solution)/shard_map/all_to_all | solution.py:142
  141.9 1.2 slice.223
  143.2 1.3 slice.222
  144.5 3.3 %fusion.15 = f32[8,64,256]{2,1,0:T(8,128)} fusion(bf16[1024,8,64]{0,2,1:T(8,128)(2,1)S(1)} %bitcast.109, f32[1024,8]{0,1:T(8,128)S(1)} %copy-done.19, f32[1024,256]{1,0:T(8,128)S(1)} %slice_convert_fusion, f32[8,64,256]{2,1,0:T(8,128)} %param.27, f32[8]{0:T(128)S(1)} %exp.45), kind=kOutput, calls=%fused_computation.29 | convolution fusion | flops 272891904 | bytes 3178528 | tf_op jit(solution)/shard_map/shp,shn->hpn/dot_general | solution.py:137
  147.9 42.6 %all-to-all-done.2 = bf16[16,64,512]{2,1,0:T(8,128)(2,1)S(1)} async-done(((bf16[16,64,512]{2,1,0:T(8,128)(2,1)}), bf16[16,64,512]{2,1,0:T(8,128)(2,1)S(1)}, u32[]{:S(2)}, u32[]{:S(2)}) %all-to-all-start.2) | async-done | bytes 1048608 | tf_op jit(solution)/shard_map/all_to_all | solution.py:142
  190.5 0.3 convert_bitcast_fusion
  190.8 0.2 copy.165
  191.0 0.3 fusion.3
  191.4 0.3 mul.313
  191.7 1.2 copy.168
  192.9 1.3 multiply_convert_fusion.2
  (105 shorter events, 2.2 us)
Async XLA Ops:
  7.2 1.2 copy-start
  7.2 18.2 %copy-start.13 = (bf16[64,8192]{1,0:T(8,128)(2,1)S(1)}, bf16[64,8192]{1,0:T(8,128)(2,1)}, u32[]{:S(2)}) copy-start(bf16[64,8192]{1,0:T(8,128)(2,1)} %param.14) | copy-start | bytes 3145732
  8.6 17.9 %copy-start.28 = (bf16[3,512]{1,0:T(4,128)(2,1)S(1)}, bf16[3,512]{1,0:T(4,128)(2,1)}, u32[]{:S(2)}) copy-start(bf16[3,512]{1,0:T(4,128)(2,1)} %param.17) | copy-start | bytes 9220
  8.6 17.9 %copy-start.32 = (bf16[512]{0:T(512)(128)(2,1)S(1)}, bf16[512]{0:T(512)(128)(2,1)}, u32[]{:S(2)}) copy-start(bf16[512]{0:T(512)(128)(2,1)} %param.20) | copy-start | bytes 3076
  10.8 28.6 %all-to-all-start.1 = ((bf16[16,2,4352]{2,1,0:T(2,128)(2,1)}), bf16[16,2,4352]{2,1,0:T(2,128)(2,1)S(1)}, u32[]{:S(2)}, u32[]{:S(2)}) async-start(bf16[16,2,4352]{2,1,0:T(2,128)(2,1)} %reshape.183), calls=%async_computation.1 | async-start | bytes 557056 | tf_op jit(solution)/shard_map/all_to_all | solution.py:72
  39.4 72.1 %all-to-all-start = ((bf16[16,64,512]{2,1,0:T(8,128)(2,1)}), bf16[16,64,512]{2,1,0:T(8,128)(2,1)S(1)}, u32[]{:S(2)}, u32[]{:S(2)}) async-start(bf16[16,64,512]{2,1,0:T(8,128)(2,1)} %bitcast.97), calls=%async_computation | async-start | bytes 2097152 | tf_op jit(solution)/shard_map/all_to_all | solution.py:78
  46.2 1.7 copy-start.22
  46.2 53.4 %all-gather.2.cloned.1.call-start = ((), (), s32[]{:S(2)}) async-start(), calls=%async_computation.3 | async-start | bytes 1310720 | tf_op jit(solution)/shard_map/all_gather | solution.py:86
  46.5 2.4 %copy-start.29 = (f32[8]{0:T(128)S(1)}, f32[8]{0:T(128)}, u32[]{:S(2)}) copy-start(f32[8]{0:T(128)} %param.23) | copy-start | bytes 100
  46.5 2.4 %copy-start.33 = (f32[8]{0:T(128)S(1)}, f32[8]{0:T(128)}, u32[]{:S(2)}) copy-start(f32[8]{0:T(128)} %param.24) | copy-start | bytes 100
  46.7 1.8 copy-start.11
  52.0 1.9 copy-start.30
  101.0 3.7 %copy-start.3 = (bf16[1024,512]{1,0:T(8,128)(2,1)S(1)}, bf16[1024,512]{1,0:T(8,128)(2,1)}, u32[]{:S(2)}) copy-start(bf16[1024,512]{1,0:T(8,128)(2,1)} %all-gather.2.cloned.1.call-done) | copy-start | bytes 3145732
  105.0 3.3 %copy-start.15 = (f32[8,512]{1,0:T(8,128)S(1)}, f32[8,512]{1,0:T(8,128)}, u32[]{:S(2)}) copy-start(f32[8,512]{1,0:T(8,128)} %slice.210) | copy-start | bytes 49156
  105.0 3.3 %copy-start.16 = (f32[8,512]{1,0:T(8,128)S(1)}, f32[8,512]{1,0:T(8,128)}, u32[]{:S(2)}) copy-start(f32[8,512]{1,0:T(8,128)} %slice.209) | copy-start | bytes 49156
  105.0 3.3 %copy-start.18 = (f32[8,256]{1,0:T(8,128)S(1)}, f32[8,256]{1,0:T(8,128)}, u32[]{:S(2)}) copy-start(f32[8,256]{1,0:T(8,128)} %get-tuple-element.12) | copy-start | bytes 24580
  108.1 1.8 copy-start.14
  108.1 1.8 copy-start.17
  109.9 2.7 %copy-start.23 = (f32[512]{0:T(512)S(1)}, f32[512]{0:T(512)}, u32[]{:S(2)}) copy-start(f32[512]{0:T(512)} %convert_element_type.96) | copy-start | bytes 6148
  109.9 2.7 %copy-start.24 = (f32[1,512]{1,0:T(1,128)S(1)}, f32[1,512]{1,0:T(1,128)}, u32[]{:S(2)}) copy-start(f32[1,512]{1,0:T(1,128)} %get-tuple-element.13) | copy-start | bytes 6148
  109.9 2.7 %copy-start.25 = (f32[1,512]{1,0:T(1,128)S(1)}, f32[1,512]{1,0:T(1,128)}, u32[]{:S(2)}) copy-start(f32[1,512]{1,0:T(1,128)} %get-tuple-element.14) | copy-start | bytes 6148
  109.9 2.7 %copy-start.26 = (f32[1,512]{1,0:T(1,128)S(1)}, f32[1,512]{1,0:T(1,128)}, u32[]{:S(2)}) copy-start(f32[1,512]{1,0:T(1,128)} %get-tuple-element.15) | copy-start | bytes 6148
  109.9 2.7 %copy-start.27 = (f32[1,512]{1,0:T(1,128)S(1)}, f32[1,512]{1,0:T(1,128)}, u32[]{:S(2)}) copy-start(f32[1,512]{1,0:T(1,128)} %get-tuple-element.16) | copy-start | bytes 6148
  111.6 1.0 copy-start.6
  114.0 3.2 %copy-start.1 = (bf16[1024,512]{1,0:T(8,128)(2,1)}, bf16[1024,512]{1,0:T(8,128)(2,1)S(1)}, u32[]{:S(2)}) copy-start(bf16[1024,512]{1,0:T(8,128)(2,1)S(1)} %multiply_convert_fusion.3) | copy-start | bytes 3145732
  117.2 3.5 %slice-start = ((bf16[1024,512]{1,0:T(8,128)(2,1)}), bf16[256,512]{1,0:T(8,128)(2,1)S(1)}, s32[]{:S(2)}) async-start(bf16[1024,512]{1,0:T(8,128)(2,1)} %copy-done.1), calls=%async_computation.4 | async-start | bytes 524288 | tf_op jit(solution)/shard_map/slice | solution.py:119
  121.6 4.0 %copy-start.2 = (bf16[8,256,768]{2,1,0:T(8,128)(2,1)S(1)}, bf16[8,256,768]{2,1,0:T(8,128)(2,1)}, u32[]{:S(2)}) copy-start(bf16[8,256,768]{2,1,0:T(8,128)(2,1)} %select_convert_fusion.1) | copy-start | bytes 9437188
  125.6 1.1 copy-start.10
  126.7 1.2 copy-start.7
  126.7 1.3 copy-start.12
  126.7 1.7 copy-start.4
  126.7 1.9 copy-start.8
  126.8 1.9 copy-start.20
  126.8 2.0 %copy-start.34 = (f32[8,64,256]{2,1,0:T(8,128)S(1)}, f32[8,64,256]{2,1,0:T(8,128)}, u32[]{:S(2)}) copy-start(f32[8,64,256]{2,1,0:T(8,128)} %param.27) | copy-start | bytes 1572868
  126.8 2.0 %copy-start.35 = (f32[8]{0:T(128)S(1)}, f32[8]{0:T(128)}, u32[]{:S(2)}) copy-start(f32[8]{0:T(128)} %param.25) | copy-start | bytes 100
  131.5 10.4 %copy-start.21 = (bf16[8192]{0:T(1024)(128)(2,1)S(1)}, bf16[8192]{0:T(1024)(128)(2,1)}, u32[]{:S(2)}) copy-start(bf16[8192]{0:T(1024)(128)(2,1)} %param.26) | copy-start | bytes 49156
  131.5 10.4 %copy-start.31 = (f32[8]{0:T(128)S(1)}, f32[8]{0:T(128)}, u32[]{:S(2)}) copy-start(f32[8]{0:T(128)} %copy-done.30) | copy-start | bytes 100
  131.5 11.6 %copy-start.5 = (bf16[1024,512]{1,0:T(8,128)(2,1)S(1)}, bf16[1024,512]{1,0:T(8,128)(2,1)}, u32[]{:S(2)}) copy-start(bf16[1024,512]{1,0:T(8,128)(2,1)} %all-gather.2.cloned.1.call-done) | copy-start | bytes 3145732
  134.2 10.3 %copy-start.9 = (bf16[1024,512]{0,1:T(8,128)(2,1)S(1)}, bf16[1024,512]{0,1:T(8,128)(2,1)}, u32[]{:S(2)}) copy-start(bf16[1024,512]{0,1:T(8,128)(2,1)} %copy.157) | copy-start | bytes 3145732
  134.2 10.3 %copy-start.19 = (f32[1024,8]{0,1:T(8,128)S(1)}, f32[1024,8]{0,1:T(8,128)}, u32[]{:S(2)}) copy-start(f32[1024,8]{0,1:T(8,128)} %get-tuple-element.4) | copy-start | bytes 98308
  134.2 56.3 %all-to-all-start.2 = ((bf16[16,64,512]{2,1,0:T(8,128)(2,1)}), bf16[16,64,512]{2,1,0:T(8,128)(2,1)S(1)}, u32[]{:S(2)}, u32[]{:S(2)}) async-start(bf16[16,64,512]{2,1,0:T(8,128)(2,1)} %copy.161), calls=%async_computation.2 | async-start | bytes 2097152 | tf_op jit(solution)/shard_map/all_to_all | solution.py:142
Sparse Core Ops, SparseCore 0:
  49.7 49.8 all-gather.1

commit v3 on v2

--- a/solution.py
+++ b/solution.py
@@ -83,7 +83,20 @@
     own_weight_bc = lax.dynamic_slice_in_dim(conv_weight_bc, column_start, bc_width, 1)
     own_bias_bc = lax.dynamic_slice_in_dim(conv_bias_bc, column_start, bc_width, 0)
     mixed_bc_part = causal_conv(head_bc_part, own_state_bc, own_weight_bc, own_bias_bc)
-    mixed_bc = lax.all_gather(mixed_bc_part, "tj", axis=1, tiled=True)
+    group_rank = lax.axis_index("tj")
+    slabs = [mixed_bc_part]
+    for shift in range(1, group_size):
+        slabs.append(
+            lax.ppermute(
+                mixed_bc_part,
+                "tj",
+                [(source, (source + shift) % group_size) for source in range(group_size)],
+            )
+        )
+    stacked = jnp.stack(slabs)
+    order = (group_rank - jnp.arange(group_size, dtype=jnp.int32)) % group_size
+    ordered = jnp.take(stacked, order, axis=0)
+    mixed_bc = jnp.transpose(ordered, (1, 0, 2)).reshape(length, group_size * bc_width)
     input_map = mixed_bc[:, :STATE]
     output_map = mixed_bc[:, STATE:]
 

time: 202 us -> 196 us (0.970)
  the two profiles are of different devices: /device:TPU:65 before, /device:TPU:77 now
where the time goes in v3:
time: 196 us; the launch traced here: 195 us
  waiting for transfers between devices  86.9 us (44%)
  starting transfers between devices  38.2 us (19%)
  local copies, waits for them, and re-layouts  28.6 us (15%)
  other arithmetic  27.4 us (14%)
  matrix products  12.4 us (6%)
    all_to_all x1, waiting for transfers between devices, local(): lax.all_to_all(mixed_y, TENSOR, split_axis=0, concat_axis=1, tiled=True)  43 us
    ppermute x3, waiting for transfers between devices, local(): lax.ppermute(mixed_bc_part, 'tj', [(source, (source + shift) % group_size...  35.8 us
    all_to_all x1, starting transfers between devices, local(): small_recv = lax.all_to_all(small_send, TENSOR, 0, 0, tiled=True)  12.5 us
    convert_element_type x4, other arithmetic, local(): weights = jnp.where(causal[None], scores[None] * decayed * step_cols[:, N...  10.5 us
    all_to_all x1, starting transfers between devices, local(): lax.all_to_all(mixed_y, TENSOR, split_axis=0, concat_axis=1, tiled=True)  9.86 us
    ppermute x3, starting transfers between devices, local(): lax.ppermute(mixed_bc_part, 'tj', [(source, (source + shift) % group_size...  9.12 us
    all_to_all x1, waiting for transfers between devices, local(): small_recv = lax.all_to_all(small_send, TENSOR, 0, 0, tiled=True)  8.03 us
    all_to_all x1, starting transfers between devices, local(): x_recv = lax.all_to_all(x_send, TENSOR, 0, 0, tiled=True)  6.74 us
  transfers between devices with their start and end apart: 6, of which 4 were waited for; matrix products, arithmetic and copies ran while one was open for 19% of the time, Pallas kernels for 0%

profile of v3, /device:TPU:77, one launch (start us, length us, event | category | flops | bytes accessed | tf_op | source)
XLA Modules:
  0.0 194.8 jit_solution(9997651898985277987)
XLA Ops:
  0.7 0.9 copy.156
  2.1 0.5 broadcast.183
  2.7 0.8 reduce.7
  3.5 0.8 reshape.249
  4.3 12.5 %all-to-all-start.1 = ((bf16[16,2,4352]{2,1,0:T(2,128)(2,1)}), bf16[16,2,4352]{2,1,0:T(2,128)(2,1)S(1)}, u32[]{:S(2)}, u32[]{:S(2)}) async-start(bf16[16,2,4352]{2,1,0:T(2,128)(2,1)} %reshape.249), calls=%async_computation.1 | async-start | bytes 557056 | tf_op jit(solution)/shard_map/all_to_all | solution.py:72
  16.8 0.5 compare_and_fusion
  17.3 0.7 dynamic-slice_convert_fusion
  18.0 0.7 constant_dynamic-slice_fusion
  18.7 0.6 pad_clamp_fusion
  19.3 0.8 dynamic-slice_convert_fusion.1
  20.0 1.1 copy.190
  21.1 0.6 convert_element_type.96
  21.7 0.6 slice_convert_fusion.5
  22.3 0.8 iota_compare_fusion.2
  23.1 0.8 iota_compare_fusion.1
  24.0 0.9 iota_compare_fusion
  24.9 8.0 %all-to-all-done.1 = bf16[16,2,4352]{2,1,0:T(2,128)(2,1)S(1)} async-done(((bf16[16,2,4352]{2,1,0:T(2,128)(2,1)}), bf16[16,2,4352]{2,1,0:T(2,128)(2,1)S(1)}, u32[]{:S(2)}, u32[]{:S(2)}) %all-to-all-start.1) | async-done | bytes 278560 | tf_op jit(solution)/shard_map/all_to_all | solution.py:72
  32.9 6.7 %all-to-all-start = ((bf16[16,64,512]{2,1,0:T(8,128)(2,1)}), bf16[16,64,512]{2,1,0:T(8,128)(2,1)S(1)}, u32[]{:S(2)}, u32[]{:S(2)}) async-start(bf16[16,64,512]{2,1,0:T(8,128)(2,1)} %bitcast.109), calls=%async_computation | async-start | bytes 2097152 | tf_op jit(solution)/shard_map/all_to_all | solution.py:78
  40.2 0.4 multiply_convert_fusion.6
  40.5 2.3 %collective-permute-start.2 = (bf16[1024,128]{1,0:T(8,128)(2,1)S(1)}, bf16[1024,128]{1,0:T(8,128)(2,1)S(1)}, u32[]{:S(2)}, u32[]{:S(2)}) collective-permute-start(bf16[1024,128]{1,0:T(8,128)(2,1)S(1)} %multiply_convert_fusion.6), channel_id=1, source_target_pairs={{0,3},{1,0},{2,1},{3,2},{4,7},{5,4},{6,5},{7,6},{8,11},{9,8},{10,9... | collective-permute-start | bytes 786440 | tf_op jit(solution)/shard_map/ppermute | solution.py:90
  42.9 3.1 %collective-permute-start.1 = (bf16[1024,128]{1,0:T(8,128)(2,1)S(1)}, bf16[1024,128]{1,0:T(8,128)(2,1)S(1)}, u32[]{:S(2)}, u32[]{:S(2)}) collective-permute-start(bf16[1024,128]{1,0:T(8,128)(2,1)S(1)} %multiply_convert_fusion.6), channel_id=1, source_target_pairs={{0,2},{1,3},{2,0},{3,1},{4,6},{5,7},{6,4},{7,5},{8,10},{9,11},{10,... | collective-permute-start | bytes 786440 | tf_op jit(solution)/shard_map/ppermute | solution.py:90
  46.0 3.7 %collective-permute-start = (bf16[1024,128]{1,0:T(8,128)(2,1)S(1)}, bf16[1024,128]{1,0:T(8,128)(2,1)S(1)}, u32[]{:S(2)}, u32[]{:S(2)}) collective-permute-start(bf16[1024,128]{1,0:T(8,128)(2,1)S(1)} %multiply_convert_fusion.6), channel_id=1, source_target_pairs={{0,1},{1,2},{2,3},{3,0},{4,5},{5,6},{6,7},{7,4},{8,9},{9,10},{10,1... | collective-permute-start | bytes 786440 | tf_op jit(solution)/shard_map/ppermute | solution.py:90
  50.3 2.3 %reduce-window.6 = f32[8,8,128]{2,1,0:T(8,128)S(1)} reduce-window(f32[8,8,128]{2,1,0:T(8,128)S(1)} %copy.162, f32[]{:T(128)} %constant.59.clone.1), window={size=1x1x128 pad=0_0x0_0x127_0}, to_apply=%region_0.1 | reduce-window | flops 1040384 | bytes 65540 | tf_op jit(solution)/shard_map/reduce-window
  53.2 0.7 exponential_multiply_fusion
  53.9 0.6 slice.217
  54.5 0.6 slice.218
  55.1 0.6 slice.212
  55.7 0.6 slice.211
  56.3 0.6 slice.206
  56.9 0.6 fusion.42
  57.5 33.2 %collective-permute-done.2 = bf16[1024,128]{1,0:T(8,128)(2,1)S(1)} collective-permute-done((bf16[1024,128]{1,0:T(8,128)(2,1)S(1)}, bf16[1024,128]{1,0:T(8,128)(2,1)S(1)}, u32[]{:S(2)}, u32[]{:S(2)}) %collective-permute-start.2) | collective-permute-done | bytes 262176 | tf_op jit(solution)/shard_map/ppermute | solution.py:90
  90.7 2.7 %collective-permute-done = bf16[1024,128]{1,0:T(8,128)(2,1)S(1)} collective-permute-done((bf16[1024,128]{1,0:T(8,128)(2,1)S(1)}, bf16[1024,128]{1,0:T(8,128)(2,1)S(1)}, u32[]{:S(2)}, u32[]{:S(2)}) %collective-permute-start) | collective-permute-done | bytes 262176 | tf_op jit(solution)/shard_map/ppermute | solution.py:90
  93.3 0.7 copy-done.15
  94.0 1.2 pad_maximum_fusion.1
  95.3 0.9 gather_fusion
  96.2 1.1 copy_bitcast_fusion
  97.6 3.7 %select_convert_fusion = bf16[8,256,1024]{2,1,0:T(8,128)(2,1)} fusion(f32[8,1024]{1,0:T(8,128)S(1)} %get-tuple-element.5, f32[8,1024]{1,0:T(8,128)S(1)} %bitcast.135, f32[8,256]{1,0:T(8,128)S(1)} %copy-done.23, f32[256,1024]{1,0:T(8,128)S(1)} %fusion.25, pred[256,1024]{1,0:T(8,128)(4,1)S(1)} %copy-done.8), kind=kLoop, calls=%fused_computation.2 | loop fusion | flops 12582912 | bytes 5578752 | tf_op jit(solution)/shard_map/convert_element_type | solution.py:128
  101.7 2.9 %select_convert_fusion.1 = bf16[8,256,768]{2,1,0:T(8,128)(2,1)} fusion(f32[8,768]{1,0:T(8,128)S(1)} %copy-done.17, f32[8,768]{1,0:T(8,128)S(1)} %copy-done.16, f32[8,256]{1,0:T(8,128)S(1)} %copy-done.22, f32[256,768]{1,0:T(8,128)S(1)} %fusion.27, pred[256,768]{1,0:T(8,128)(4,1)S(1)} %copy-done.11), kind=kLoop, calls=%fused_computation.3 | loop fusion | flops 9437184 | bytes 4186112 | tf_op jit(solution)/shard_map/convert_element_type | solution.py:128
  105.0 2.3 %select_convert_fusion.2 = bf16[8,256,512]{2,1,0:T(8,128)(2,1)} fusion(f32[8,512]{1,0:T(8,128)S(1)} %copy-done.18, f32[8,512]{1,0:T(8,128)S(1)} %copy-done.19, f32[8,256]{1,0:T(8,128)S(1)} %copy-done.21, f32[256,512]{1,0:T(8,128)S(1)} %fusion.29, pred[256,512]{1,0:T(8,128)(4,1)S(1)} %copy-done.12), kind=kLoop, calls=%fused_computation.7 | loop fusion | flops 6291456 | bytes 2793472 | tf_op jit(solution)/shard_map/convert_element_type | solution.py:128
  107.5 1.6 select_convert_fusion.3
  109.2 0.3 bitcast_convert_fusion.4
  109.6 1.4 multiply_convert_fusion.3
  111.0 1.3 copy.165
  112.3 0.9 slice.213
  113.3 0.8 slice.207
  114.1 1.4 copy.164
  115.5 2.0 %copy.163 = bf16[512,512]{0,1:T(8,128)(2,1)} copy(bf16[512,512]{1,0:T(8,128)(2,1)} %slice.207) | data formatting | bytes 1048576 | tf_op jit(solution)/shard_map/slice | solution.py:132
  117.6 0.8 copy.154
  118.4 4.0 %convolution_bitcast_fusion.3 = f32[256,8,64]{0,2,1:T(8,128)S(1)} fusion(bf16[1024,8,64]{0,2,1:T(8,128)(2,1)} %bitcast.119, bf16[8,256,1024]{2,1,0:T(8,128)(2,1)} %select_convert_fusion), kind=kOutput, calls=%fused_computation.33 | convolution fusion | flops 268435456 | bytes 5767168 | tf_op jit(solution)/shard_map/hts,shp->thp/dot_general | solution.py:131
  122.5 1.1 convolution_bitcast_fusion
  123.6 0.5 copy-done.3
  124.2 0.8 convolution_bitcast_fusion.1
  125.0 0.4 convolution_bitcast_fusion.2
  125.6 1.4 fusion.14
  127.0 2.3 %reshape.246 = bf16[16,64,512]{1,0,2:T(8,128)(2,1)} reshape(bf16[1024,8,64]{0,2,1:T(8,128)(2,1)S(1)} %fusion.14) | data formatting | bytes 2097152 | tf_op jit(solution)/shard_map/convert_element_type | solution.py:145
  129.3 3.3 %copy.169 = bf16[16,64,512]{2,1,0:T(8,128)(2,1)} copy(bf16[16,64,512]{1,0,2:T(8,128)(2,1)} %reshape.246) | data formatting | bytes 2097152 | tf_op jit(solution)/shard_map/convert_element_type | solution.py:145
  132.6 9.9 %all-to-all-start.2 = ((bf16[16,64,512]{2,1,0:T(8,128)(2,1)}), bf16[16,64,512]{2,1,0:T(8,128)(2,1)S(1)}, u32[]{:S(2)}, u32[]{:S(2)}) async-start(bf16[16,64,512]{2,1,0:T(8,128)(2,1)} %copy.169), calls=%async_computation.2 | async-start | bytes 2097152 | tf_op jit(solution)/shard_map/all_to_all | solution.py:155
  142.5 1.2 slice.225
  143.9 0.6 slice.224
  144.5 3.6 %fusion.15 = f32[8,64,256]{2,1,0:T(8,128)} fusion(bf16[1024,8,64]{0,2,1:T(8,128)(2,1)} %bitcast.120, f32[1024,8]{0,1:T(8,128)S(1)} %copy-done.24, f32[1024,256]{1,0:T(8,128)S(1)} %slice_convert_fusion, f32[8,64,256]{2,1,0:T(8,128)} %param.27, f32[8]{0:T(128)S(1)} %exp.45), kind=kOutput, calls=%fused_computation.30 | convolution fusion | flops 272891904 | bytes 3178528 | tf_op jit(solution)/shard_map/shp,shn->hpn/dot_general | solution.py:150
  148.1 43.0 %all-to-all-done.2 = bf16[16,64,512]{2,1,0:T(8,128)(2,1)S(1)} async-done(((bf16[16,64,512]{2,1,0:T(8,128)(2,1)}), bf16[16,64,512]{2,1,0:T(8,128)(2,1)S(1)}, u32[]{:S(2)}, u32[]{:S(2)}) %all-to-all-start.2) | async-done | bytes 1048608 | tf_op jit(solution)/shard_map/all_to_all | solution.py:155
  192.0 0.3 mul.313
  192.3 1.2 copy.177
  193.5 1.3 multiply_convert_fusion.2
  (124 shorter events, 4.8 us)
Async XLA Ops:
  0.6 1.2 copy-start
  0.6 19.4 %copy-start.10 = (bf16[64,8192]{1,0:T(8,128)(2,1)S(1)}, bf16[64,8192]{1,0:T(8,128)(2,1)}, u32[]{:S(2)}) copy-start(bf16[64,8192]{1,0:T(8,128)(2,1)} %param.14) | copy-start | bytes 3145732
  2.1 19.0 %copy-start.33 = (bf16[3,512]{1,0:T(4,128)(2,1)S(1)}, bf16[3,512]{1,0:T(4,128)(2,1)}, u32[]{:S(2)}) copy-start(bf16[3,512]{1,0:T(4,128)(2,1)} %param.17) | copy-start | bytes 9220
  2.1 19.0 %copy-start.37 = (bf16[512]{0:T(512)(128)(2,1)S(1)}, bf16[512]{0:T(512)(128)(2,1)}, u32[]{:S(2)}) copy-start(bf16[512]{0:T(512)(128)(2,1)} %param.20) | copy-start | bytes 3076
  2.1 19.6 %copy-start.27 = (bf16[4,512]{1,0:T(4,128)(2,1)S(1)}, bf16[4,512]{1,0:T(4,128)(2,1)}, u32[]{:S(2)}) copy-start(bf16[4,512]{1,0:T(4,128)(2,1)} %param.19) | copy-start | bytes 12292
  4.3 28.6 %all-to-all-start.1 = ((bf16[16,2,4352]{2,1,0:T(2,128)(2,1)}), bf16[16,2,4352]{2,1,0:T(2,128)(2,1)S(1)}, u32[]{:S(2)}, u32[]{:S(2)}) async-start(bf16[16,2,4352]{2,1,0:T(2,128)(2,1)} %reshape.249), calls=%async_computation.1 | async-start | bytes 557056 | tf_op jit(solution)/shard_map/all_to_all | solution.py:72
  32.9 76.2 %all-to-all-start = ((bf16[16,64,512]{2,1,0:T(8,128)(2,1)}), bf16[16,64,512]{2,1,0:T(8,128)(2,1)S(1)}, u32[]{:S(2)}, u32[]{:S(2)}) async-start(bf16[16,64,512]{2,1,0:T(8,128)(2,1)} %bitcast.109), calls=%async_computation | async-start | bytes 2097152 | tf_op jit(solution)/shard_map/all_to_all | solution.py:78
  39.9 10.2 %copy-start.34 = (f32[8]{0:T(128)S(1)}, f32[8]{0:T(128)}, u32[]{:S(2)}) copy-start(f32[8]{0:T(128)} %param.23) | copy-start | bytes 100
  39.9 10.2 %copy-start.38 = (f32[8]{0:T(128)S(1)}, f32[8]{0:T(128)}, u32[]{:S(2)}) copy-start(f32[8]{0:T(128)} %param.24) | copy-start | bytes 100
  40.1 5.8 %copy-start.7 = (bf16[1024,128]{1,0:T(8,128)(2,1)}, bf16[1024,128]{1,0:T(8,128)(2,1)S(1)}, u32[]{:S(2)}) copy-start(bf16[1024,128]{1,0:T(8,128)(2,1)S(1)} %reshape.222) | copy-start | bytes 786436
  40.5 50.1 %collective-permute-start.2 = (bf16[1024,128]{1,0:T(8,128)(2,1)S(1)}, bf16[1024,128]{1,0:T(8,128)(2,1)S(1)}, u32[]{:S(2)}, u32[]{:S(2)}) collective-permute-start(bf16[1024,128]{1,0:T(8,128)(2,1)S(1)} %multiply_convert_fusion.6), channel_id=1, source_target_pairs={{0,3},{1,0},{2,1},{3,2},{4,7},{5,4},{6,5},{7,6},{8,11},{9,8},{10,9... | collective-permute-start | bytes 786440 | tf_op jit(solution)/shard_map/ppermute | solution.py:90
  42.9 47.8 %collective-permute-start.1 = (bf16[1024,128]{1,0:T(8,128)(2,1)S(1)}, bf16[1024,128]{1,0:T(8,128)(2,1)S(1)}, u32[]{:S(2)}, u32[]{:S(2)}) collective-permute-start(bf16[1024,128]{1,0:T(8,128)(2,1)S(1)} %multiply_convert_fusion.6), channel_id=1, source_target_pairs={{0,2},{1,3},{2,0},{3,1},{4,6},{5,7},{6,4},{7,5},{8,10},{9,11},{10,... | collective-permute-start | bytes 786440 | tf_op jit(solution)/shard_map/ppermute | solution.py:90
  46.0 47.4 %collective-permute-start = (bf16[1024,128]{1,0:T(8,128)(2,1)S(1)}, bf16[1024,128]{1,0:T(8,128)(2,1)S(1)}, u32[]{:S(2)}, u32[]{:S(2)}) collective-permute-start(bf16[1024,128]{1,0:T(8,128)(2,1)S(1)} %multiply_convert_fusion.6), channel_id=1, source_target_pairs={{0,1},{1,2},{2,3},{3,0},{4,5},{5,6},{6,7},{7,4},{8,9},{9,10},{10,1... | collective-permute-start | bytes 786440 | tf_op jit(solution)/shard_map/ppermute | solution.py:90
  53.2 3.1 %copy-start.35 = (f32[8]{0:T(128)}, f32[8]{0:T(128)S(1)}, u32[]{:S(2)}) copy-start(f32[8]{0:T(128)S(1)} %slice_reduce_fusion.1) | copy-start | bytes 100
  90.6 2.7 %copy-start.13 = (bf16[1024,128]{1,0:T(8,128)(2,1)}, bf16[1024,128]{1,0:T(8,128)(2,1)S(1)}, u32[]{:S(2)}) copy-start(bf16[1024,128]{1,0:T(8,128)(2,1)S(1)} %collective-permute-done.2) | copy-start | bytes 786436
  90.7 2.7 %copy-start.14 = (bf16[1024,128]{1,0:T(8,128)(2,1)}, bf16[1024,128]{1,0:T(8,128)(2,1)S(1)}, u32[]{:S(2)}) copy-start(bf16[1024,128]{1,0:T(8,128)(2,1)S(1)} %collective-permute-done.1) | copy-start | bytes 786436
  93.3 0.7 copy-start.15
  96.2 1.4 copy-start.8
  96.2 1.4 copy-start.23
  97.6 4.0 %copy-start.11 = (pred[256,768]{1,0:T(8,128)(4,1)S(1)}, pred[256,768]{1,0:T(8,128)(4,1)}, u32[]{:S(2)}) copy-start(pred[256,768]{1,0:T(8,128)(4,1)} %iota_compare_fusion.1) | copy-start | bytes 589828
  97.6 4.0 %copy-start.16 = (f32[8,768]{1,0:T(8,128)S(1)}, f32[8,768]{1,0:T(8,128)}, u32[]{:S(2)}) copy-start(f32[8,768]{1,0:T(8,128)} %slice.217) | copy-start | bytes 73732
  97.6 4.0 %copy-start.17 = (f32[8,768]{1,0:T(8,128)S(1)}, f32[8,768]{1,0:T(8,128)}, u32[]{:S(2)}) copy-start(f32[8,768]{1,0:T(8,128)} %slice.218) | copy-start | bytes 73732
  97.6 4.0 %copy-start.22 = (f32[8,256]{1,0:T(8,128)S(1)}, f32[8,256]{1,0:T(8,128)}, u32[]{:S(2)}) copy-start(f32[8,256]{1,0:T(8,128)} %get-tuple-element.11) | copy-start | bytes 24580
  101.7 3.3 %copy-start.12 = (pred[256,512]{1,0:T(8,128)(4,1)S(1)}, pred[256,512]{1,0:T(8,128)(4,1)}, u32[]{:S(2)}) copy-start(pred[256,512]{1,0:T(8,128)(4,1)} %iota_compare_fusion.2) | copy-start | bytes 393220
  101.7 3.3 %copy-start.18 = (f32[8,512]{1,0:T(8,128)S(1)}, f32[8,512]{1,0:T(8,128)}, u32[]{:S(2)}) copy-start(f32[8,512]{1,0:T(8,128)} %slice.212) | copy-start | bytes 49156
  101.7 3.3 %copy-start.19 = (f32[8,512]{1,0:T(8,128)S(1)}, f32[8,512]{1,0:T(8,128)}, u32[]{:S(2)}) copy-start(f32[8,512]{1,0:T(8,128)} %slice.211) | copy-start | bytes 49156
  101.7 3.3 %copy-start.21 = (f32[8,256]{1,0:T(8,128)S(1)}, f32[8,256]{1,0:T(8,128)}, u32[]{:S(2)}) copy-start(f32[8,256]{1,0:T(8,128)} %get-tuple-element.12) | copy-start | bytes 24580
  104.7 2.8 %copy-start.20 = (f32[8,256]{1,0:T(8,128)S(1)}, f32[8,256]{1,0:T(8,128)}, u32[]{:S(2)}) copy-start(f32[8,256]{1,0:T(8,128)} %slice.206) | copy-start | bytes 24580
  107.5 2.0 %copy-start.28 = (f32[512]{0:T(512)S(1)}, f32[512]{0:T(512)}, u32[]{:S(2)}) copy-start(f32[512]{0:T(512)} %convert_element_type.96) | copy-start | bytes 6148
  107.5 2.0 %copy-start.29 = (f32[1,512]{1,0:T(1,128)S(1)}, f32[1,512]{1,0:T(1,128)}, u32[]{:S(2)}) copy-start(f32[1,512]{1,0:T(1,128)} %get-tuple-element.13) | copy-start | bytes 6148
  107.5 2.0 %copy-start.30 = (f32[1,512]{1,0:T(1,128)S(1)}, f32[1,512]{1,0:T(1,128)}, u32[]{:S(2)}) copy-start(f32[1,512]{1,0:T(1,128)} %get-tuple-element.14) | copy-start | bytes 6148
  107.5 2.0 %copy-start.31 = (f32[1,512]{1,0:T(1,128)S(1)}, f32[1,512]{1,0:T(1,128)}, u32[]{:S(2)}) copy-start(f32[1,512]{1,0:T(1,128)} %get-tuple-element.15) | copy-start | bytes 6148
  107.5 2.0 %copy-start.32 = (f32[1,512]{1,0:T(1,128)S(1)}, f32[1,512]{1,0:T(1,128)}, u32[]{:S(2)}) copy-start(f32[1,512]{1,0:T(1,128)} %get-tuple-element.16) | copy-start | bytes 6148
  111.0 3.1 %copy-start.1 = (bf16[1024,512]{1,0:T(8,128)(2,1)}, bf16[1024,512]{1,0:T(8,128)(2,1)S(1)}, u32[]{:S(2)}) copy-start(bf16[1024,512]{1,0:T(8,128)(2,1)S(1)} %multiply_convert_fusion.3) | copy-start | bytes 3145732
  114.1 3.5 %slice-start = ((bf16[1024,512]{1,0:T(8,128)(2,1)}), bf16[256,512]{1,0:T(8,128)(2,1)S(1)}, s32[]{:S(2)}) async-start(bf16[1024,512]{1,0:T(8,128)(2,1)} %copy-done.1), calls=%async_computation.3 | async-start | bytes 524288 | tf_op jit(solution)/shard_map/slice | solution.py:132
  118.4 4.0 %copy-start.2 = (bf16[8,256,768]{2,1,0:T(8,128)(2,1)S(1)}, bf16[8,256,768]{2,1,0:T(8,128)(2,1)}, u32[]{:S(2)}) copy-start(bf16[8,256,768]{2,1,0:T(8,128)(2,1)} %select_convert_fusion.1) | copy-start | bytes 9437188
  122.5 1.6 copy-start.3
  122.5 1.7 copy-start.6
  123.6 1.4 copy-start.4
  123.6 1.4 copy-start.9
  124.2 1.3 copy-start.5
  124.2 1.3 copy-start.25
  124.2 1.5 copy-start.39
  124.2 1.5 copy-start.40
  129.3 13.2 %copy-start.26 = (bf16[8192]{0:T(1024)(128)(2,1)S(1)}, bf16[8192]{0:T(1024)(128)(2,1)}, u32[]{:S(2)}) copy-start(bf16[8192]{0:T(1024)(128)(2,1)} %param.26) | copy-start | bytes 49156
  129.3 13.2 %copy-start.36 = (f32[8]{0:T(128)S(1)}, f32[8]{0:T(128)}, u32[]{:S(2)}) copy-start(f32[8]{0:T(128)} %copy-done.35) | copy-start | bytes 100
  132.6 11.8 %copy-start.24 = (f32[1024,8]{0,1:T(8,128)S(1)}, f32[1024,8]{0,1:T(8,128)}, u32[]{:S(2)}) copy-start(f32[1024,8]{0,1:T(8,128)} %get-tuple-element.4) | copy-start | bytes 98308
  132.6 58.5 %all-to-all-start.2 = ((bf16[16,64,512]{2,1,0:T(8,128)(2,1)}), bf16[16,64,512]{2,1,0:T(8,128)(2,1)S(1)}, u32[]{:S(2)}, u32[]{:S(2)}) async-start(bf16[16,64,512]{2,1,0:T(8,128)(2,1)} %copy.169), calls=%async_computation.2 | async-start | bytes 2097152 | tf_op jit(solution)/shard_map/all_to_all | solution.py:155

commit v4 on v2

--- a/solution.py
+++ b/solution.py
@@ -83,7 +83,17 @@
     own_weight_bc = lax.dynamic_slice_in_dim(conv_weight_bc, column_start, bc_width, 1)
     own_bias_bc = lax.dynamic_slice_in_dim(conv_bias_bc, column_start, bc_width, 0)
     mixed_bc_part = causal_conv(head_bc_part, own_state_bc, own_weight_bc, own_bias_bc)
-    mixed_bc = lax.all_gather(mixed_bc_part, "tj", axis=1, tiled=True)
+    group_rank = lax.axis_index("tj")
+    across = lax.ppermute(
+        mixed_bc_part, "tj", [(source, source ^ 2) for source in range(group_size)]
+    )
+    pair = jnp.stack([mixed_bc_part, across])
+    beside = lax.ppermute(pair, "tj", [(source, source ^ 1) for source in range(group_size)])
+    stacked = jnp.concatenate([pair, beside], axis=0)
+    slot_of = jnp.array([0, 2, 1, 3], dtype=jnp.int32)
+    order = slot_of[jnp.arange(group_size, dtype=jnp.int32) ^ group_rank]
+    ordered = jnp.take(stacked, order, axis=0)
+    mixed_bc = jnp.transpose(ordered, (1, 0, 2)).reshape(length, group_size * bc_width)
     input_map = mixed_bc[:, :STATE]
     output_map = mixed_bc[:, STATE:]
 
@@ -94,6 +104,7 @@
 
     mixed_x = causal_conv(head_x, conv_state_x, conv_weight_x, conv_bias_x)
     values = mixed_x.reshape(length, heads_here, HEAD_DIM)
+    values_t = jnp.transpose(values, (1, 2, 0))
 
     query_rows = min(256, length)
     pieces = []
@@ -116,26 +127,29 @@
         weights = lax.optimization_barrier(weights)
         pieces.append(
             jnp.einsum(
-                "hts,shp->thp", weights, values[:row_stop], preferred_element_type=jnp.float32
+                "hts,hps->htp",
+                weights,
+                values_t[:, :, :row_stop],
+                preferred_element_type=jnp.float32,
             )
         )
-    local_all = jnp.concatenate(pieces, axis=0)
+    local_all = jnp.concatenate(pieces, axis=1)
     carried = jnp.einsum(
-        "tn,hpn->thp",
+        "tn,hpn->htp",
         output_map.astype(jnp.float32),
         scan_state,
         precision=lax.Precision.HIGHEST,
     )
-    carried = carried * jnp.exp(running)[:, :, None]
-    channels = values.astype(jnp.float32)
-    mixed = local_all + carried + skip_gain[None, :, None] * channels
-    mixed_y = mixed.reshape(length, x_width).astype(jnp.bfloat16)
+    carried = carried * jnp.exp(running_cols)[:, :, None]
+    channels = jnp.transpose(values_t, (0, 2, 1)).astype(jnp.float32)
+    mixed = local_all + carried + skip_gain[:, None, None] * channels
+    mixed_y = jnp.transpose(mixed.astype(jnp.bfloat16), (1, 0, 2)).reshape(length, x_width)
     tail_decay = jnp.exp(running[length - 1][None, :] - running) * step_size
     weighted = (input_map.astype(jnp.float32)[:, None, :] * tail_decay[:, :, None]).astype(
         jnp.bfloat16
     )
     gathered_in = jnp.einsum(
-        "shp,shn->hpn", values, weighted, preferred_element_type=jnp.float32
+        "hps,shn->hpn", values_t, weighted, preferred_element_type=jnp.float32
     )
     final_state = jnp.exp(running[length - 1])[:, None, None] * scan_state + gathered_in
 

time: 202 us -> 189 us (0.936)
  the two profiles are of different devices: /device:TPU:65 before, /device:TPU:95 now
where the time goes in v4:
time: 189 us; the launch traced here: 188 us
  waiting for transfers between devices  92.3 us (49%)
  starting transfers between devices  32.5 us (17%)
  other arithmetic  26.2 us (14%)
  local copies, waits for them, and re-layouts  24.2 us (13%)
  matrix products  11.7 us (6%)
    all_to_all x1, waiting for transfers between devices, local(): lax.all_to_all(mixed_y, TENSOR, split_axis=0, concat_axis=1, tiled=True)  42.6 us
    ppermute x1, waiting for transfers between devices, local(): lax.ppermute(mixed_bc_part, 'tj', [(source, source ^ 2) for source in ran...  42.4 us
    all_to_all x1, starting transfers between devices, local(): small_recv = lax.all_to_all(small_send, TENSOR, 0, 0, tiled=True)  12.5 us
    convert_element_type x4, other arithmetic, local(): weights = jnp.where(causal[None], scores[None] * decayed * step_cols[:, N...  9.55 us
    all_to_all x1, waiting for transfers between devices, local(): small_recv = lax.all_to_all(small_send, TENSOR, 0, 0, tiled=True)  7.32 us
    all_to_all x1, starting transfers between devices, local(): lax.all_to_all(mixed_y, TENSOR, split_axis=0, concat_axis=1, tiled=True)  7.12 us
    all_to_all x1, starting transfers between devices, local(): x_recv = lax.all_to_all(x_send, TENSOR, 0, 0, tiled=True)  6.74 us
    dot_general x4, matrix products, local(): jnp.einsum('hts,hps->htp', weights, values_t[:, :, :row_stop], preferred_...  5.98 us
  transfers between devices with their start and end apart: 5, of which 3 were waited for; matrix products, arithmetic and copies ran while one was open for 20% of the time, Pallas kernels for 0%

profile of v4, /device:TPU:95, one launch (start us, length us, event | category | flops | bytes accessed | tf_op | source)
XLA Modules:
  0.0 188.2 jit_solution(9384626891703477225)
XLA Ops:
  0.7 0.9 copy.128
  2.1 0.5 broadcast.163
  2.6 0.9 reduce.7
  3.4 0.8 reshape.242
  4.2 12.5 %all-to-all-start = ((bf16[16,2,4352]{2,1,0:T(2,128)(2,1)}), bf16[16,2,4352]{2,1,0:T(2,128)(2,1)S(1)}, u32[]{:S(2)}, u32[]{:S(2)}) async-start(bf16[16,2,4352]{2,1,0:T(2,128)(2,1)} %reshape.242), calls=%async_computation | async-start | bytes 557056 | tf_op jit(solution)/shard_map/all_to_all | solution.py:72
  16.7 0.6 gather_fusion
  17.4 0.5 compare_and_fusion
  17.9 0.7 dynamic-slice_convert_fusion
  18.6 0.7 constant_dynamic-slice_fusion
  19.3 0.6 pad_clamp_fusion
  19.9 0.8 dynamic-slice_convert_fusion.1
  20.6 1.1 copy.161
  21.7 0.6 convert_element_type.100
  22.4 0.6 slice_convert_fusion.5
  23.0 0.8 iota_compare_fusion.2
  23.8 0.9 iota_compare_fusion.1
  24.6 0.9 iota_compare_fusion
  25.5 7.3 %all-to-all-done = bf16[16,2,4352]{2,1,0:T(2,128)(2,1)S(1)} async-done(((bf16[16,2,4352]{2,1,0:T(2,128)(2,1)}), bf16[16,2,4352]{2,1,0:T(2,128)(2,1)S(1)}, u32[]{:S(2)}, u32[]{:S(2)}) %all-to-all-start) | async-done | bytes 278560 | tf_op jit(solution)/shard_map/all_to_all | solution.py:72
  32.9 6.7 %all-to-all-start.1 = ((bf16[16,64,512]{2,1,0:T(8,128)(2,1)}), bf16[16,64,512]{2,1,0:T(8,128)(2,1)S(1)}, u32[]{:S(2)}, u32[]{:S(2)}) async-start(bf16[16,64,512]{2,1,0:T(8,128)(2,1)} %bitcast.110), calls=%async_computation.1 | async-start | bytes 2097152 | tf_op jit(solution)/shard_map/all_to_all | solution.py:78
  40.0 0.3 reshape.216
  40.6 2.3 %reduce-window.6 = f32[8,8,128]{2,1,0:T(8,128)S(1)} reduce-window(f32[8,8,128]{2,1,0:T(8,128)S(1)} %copy.134, f32[]{:T(128)} %constant.50.clone.1), window={size=1x1x128 pad=0_0x0_0x127_0}, to_apply=%region_0.1 | reduce-window | flops 1040384 | bytes 65540 | tf_op jit(solution)/shard_map/reduce-window
  43.4 0.4 multiply_convert_fusion.6
  43.7 3.1 %collective-permute-start = (bf16[1024,128]{1,0:T(8,128)(2,1)S(1)}, bf16[1024,128]{1,0:T(8,128)(2,1)S(1)}, u32[]{:S(2)}, u32[]{:S(2)}) collective-permute-start(bf16[1024,128]{1,0:T(8,128)(2,1)S(1)} %multiply_convert_fusion.6), channel_id=1, source_target_pairs={{0,2},{1,3},{2,0},{3,1},{4,6},{5,7},{6,4},{7,5},{8,10},{9,11},{10,... | collective-permute-start | bytes 786440 | tf_op jit(solution)/shard_map/ppermute | solution.py:87
  47.1 42.4 %collective-permute-done = bf16[1024,128]{1,0:T(8,128)(2,1)S(1)} collective-permute-done((bf16[1024,128]{1,0:T(8,128)(2,1)S(1)}, bf16[1024,128]{1,0:T(8,128)(2,1)S(1)}, u32[]{:S(2)}, u32[]{:S(2)}) %collective-permute-start) | collective-permute-done | bytes 262176 | tf_op jit(solution)/shard_map/ppermute | solution.py:87
  89.5 3.1 %collective-permute-start.1 = (bf16[2,1024,128]{2,1,0:T(8,128)(2,1)S(1)}, bf16[2,1024,128]{2,1,0:T(8,128)(2,1)S(1)}, u32[]{:S(2)}, u32[]{:S(2)}) collective-permute-start(bf16[2,1024,128]{2,1,0:T(8,128)(2,1)S(1)} %pad_maximum_fusion.3), channel_id=1, source_target_pairs={{0,1},{1,0},{2,3},{3,2},{4,5},{5,4},{6,7},{7,6},{8,9},{9,8},{10,11... | collective-permute-start | bytes 1572872 | tf_op jit(solution)/shard_map/ppermute | solution.py:91
  92.6 0.7 exponential_multiply_fusion
  93.3 0.6 slice.206
  93.9 0.6 slice.207
  94.5 0.6 slice.201
  95.1 0.6 slice.200
  95.7 0.6 slice.191
  96.3 0.6 fusion.49
  96.9 0.6 fusion.47
  97.7 0.9 gather_fusion.1
  98.6 1.1 copy_bitcast_fusion
  99.6 0.3 fusion.30
  100.0 3.6 %select_convert_fusion = bf16[8,256,1024]{2,1,0:T(8,128)(2,1)} fusion(f32[8,1024]{1,0:T(8,128)S(1)} %get-tuple-element.5, f32[8,1024]{1,0:T(8,128)S(1)} %bitcast.139, f32[8,256]{1,0:T(8,128)S(1)} %copy-done.17, f32[256,1024]{1,0:T(8,128)S(1)} %fusion.30, pred[256,1024]{1,0:T(8,128)(4,1)S(1)} %copy-done.6), kind=kLoop, calls=%fused_computation.3 | loop fusion | flops 12582912 | bytes 5578752 | tf_op jit(solution)/shard_map/convert_element_type | solution.py:126
  103.7 0.3 fusion.32
  104.1 3.0 %select_convert_fusion.1 = bf16[8,256,768]{2,1,0:T(8,128)(2,1)} fusion(f32[8,768]{1,0:T(8,128)S(1)} %copy-done.11, f32[8,768]{1,0:T(8,128)S(1)} %copy-done.10, f32[8,256]{1,0:T(8,128)S(1)} %copy-done.16, f32[256,768]{1,0:T(8,128)S(1)} %fusion.32, pred[256,768]{1,0:T(8,128)(4,1)S(1)} %copy-done.8), kind=kLoop, calls=%fused_computation.4 | loop fusion | flops 9437184 | bytes 4186112 | tf_op jit(solution)/shard_map/convert_element_type | solution.py:126
  107.1 0.3 fusion.34
  107.4 2.3 %select_convert_fusion.2 = bf16[8,256,512]{2,1,0:T(8,128)(2,1)} fusion(f32[8,512]{1,0:T(8,128)S(1)} %copy-done.12, f32[8,512]{1,0:T(8,128)S(1)} %copy-done.13, f32[8,256]{1,0:T(8,128)S(1)} %copy-done.15, f32[256,512]{1,0:T(8,128)S(1)} %fusion.34, pred[256,512]{1,0:T(8,128)(4,1)S(1)} %copy-done.9), kind=kLoop, calls=%fused_computation.8 | loop fusion | flops 6291456 | bytes 2793472 | tf_op jit(solution)/shard_map/convert_element_type | solution.py:126
  109.9 0.6 select_convert_fusion.3
  110.6 0.3 bitcast_convert_fusion.4
  110.9 0.6 copy-done.4
  111.6 2.2 %multiply_convert_fusion.3 = bf16[1024,512]{1,0:T(8,128)(2,1)} fusion(f32[1024,512]{1,0:T(8,128)S(1)} %bitcast_convert_fusion.4, f32[3,512]{1,0:T(4,128)S(1)} %convert_element_type.101, f32[512]{0:T(512)S(1)} %bitcast.146, f32[512]{0:T(512)S(1)} %bitcast.147, f32[512]{0:T(512)S(1)} %bitcast.145, f32[512]{0:T(512)S(1)} %bitcast.144, f32[512]{0:T(512)S(1)} %copy-done.22), kind=kLoop, calls=%fused_computation.29 | loop fusion | flops 8388608 | bytes 3162112 | tf_op jit(solution)/shard_map/convert_element_type | solution.py:30
  113.8 1.5 copy.136
  115.3 3.7 %fusion.50 = f32[8,256,64]{1,2,0:T(8,128)S(1)} fusion(bf16[8,256,1024]{2,1,0:T(8,128)(2,1)} %select_convert_fusion, bf16[8,64,1024]{2,1,0:T(8,128)(2,1)S(1)} %bitcast.116), kind=kOutput, calls=%fused_computation.115 | convolution fusion | flops 268435456 | bytes 5767168 | tf_op jit(solution)/shard_map/hts,hps->htp/dot_general | solution.py:129
  119.0 1.1 fusion.17
  120.1 0.5 copy-done.3
  120.6 0.8 fusion.27
  121.4 0.4 fusion.36
  121.8 1.3 fusion.15
  123.2 2.3 %reshape.239 = bf16[16,64,512]{1,0,2:T(8,128)(2,1)} reshape(bf16[1024,8,64]{0,2,1:T(8,128)(2,1)S(1)} %fusion.15) | data formatting | bytes 2097152 | tf_op jit(solution)/shard_map/all_to_all | solution.py:156
  125.5 3.3 %copy.140 = bf16[16,64,512]{2,1,0:T(8,128)(2,1)} copy(bf16[16,64,512]{1,0,2:T(8,128)(2,1)} %reshape.239) | data formatting | bytes 2097152 | tf_op jit(solution)/shard_map/all_to_all | solution.py:156
  128.8 7.1 %all-to-all-start.2 = ((bf16[16,64,512]{2,1,0:T(8,128)(2,1)}), bf16[16,64,512]{2,1,0:T(8,128)(2,1)S(1)}, u32[]{:S(2)}, u32[]{:S(2)}) async-start(bf16[16,64,512]{2,1,0:T(8,128)(2,1)} %copy.140), calls=%async_computation.2 | async-start | bytes 2097152 | tf_op jit(solution)/shard_map/all_to_all | solution.py:156
  136.0 1.3 slice.215
  137.3 1.3 slice.214
  138.6 3.3 %fusion.16 = f32[8,64,256]{2,1,0:T(8,128)} fusion(bf16[8,64,1024]{2,1,0:T(8,128)(2,1)S(1)} %bitcast.121, f32[1024,8]{0,1:T(8,128)S(1)} %copy-done.19, f32[1024,256]{1,0:T(8,128)S(1)} %slice_convert_fusion, f32[8,64,256]{2,1,0:T(8,128)} %param.28, f32[8]{0:T(128)S(1)} %exp.49), kind=kOutput, calls=%fused_computation.32 | convolution fusion | flops 272891904 | bytes 3178528 | tf_op jit(solution)/shard_map/hps,shn->hpn/dot_general | solution.py:151
  141.9 42.6 %all-to-all-done.2 = bf16[16,64,512]{2,1,0:T(8,128)(2,1)S(1)} async-done(((bf16[16,64,512]{2,1,0:T(8,128)(2,1)}), bf16[16,64,512]{2,1,0:T(8,128)(2,1)S(1)}, u32[]{:S(2)}, u32[]{:S(2)}) %all-to-all-start.2) | async-done | bytes 1048608 | tf_op jit(solution)/shard_map/all_to_all | solution.py:156
  184.5 0.3 convert_bitcast_fusion
  185.0 0.3 fusion.3
  185.4 0.3 mul.317
  185.8 1.2 copy.148
  187.0 1.3 multiply_convert_fusion.2
  (108 shorter events, 2.8 us)
Async XLA Ops:
  0.6 1.1 copy-start
  0.6 16.1 %copy-start.1 = (s32[4]{0:T(128)S(1)}, s32[4]{0:T(128)}, u32[]{:S(2)}) copy-start(s32[4]{0:T(128)} %constant.56.clone) | copy-start | bytes 52
  1.5 19.1 %copy-start.7 = (bf16[64,8192]{1,0:T(8,128)(2,1)S(1)}, bf16[64,8192]{1,0:T(8,128)(2,1)}, u32[]{:S(2)}) copy-start(bf16[64,8192]{1,0:T(8,128)(2,1)} %param.15) | copy-start | bytes 3145732
  2.6 19.1 %copy-start.27 = (bf16[3,512]{1,0:T(4,128)(2,1)S(1)}, bf16[3,512]{1,0:T(4,128)(2,1)}, u32[]{:S(2)}) copy-start(bf16[3,512]{1,0:T(4,128)(2,1)} %param.18) | copy-start | bytes 9220
  2.6 19.1 %copy-start.31 = (bf16[512]{0:T(512)(128)(2,1)S(1)}, bf16[512]{0:T(512)(128)(2,1)}, u32[]{:S(2)}) copy-start(bf16[512]{0:T(512)(128)(2,1)} %param.21) | copy-start | bytes 3076
  2.6 19.8 %copy-start.21 = (bf16[4,512]{1,0:T(4,128)(2,1)S(1)}, bf16[4,512]{1,0:T(4,128)(2,1)}, u32[]{:S(2)}) copy-start(bf16[4,512]{1,0:T(4,128)(2,1)} %param.20) | copy-start | bytes 12292
  4.2 28.6 %all-to-all-start = ((bf16[16,2,4352]{2,1,0:T(2,128)(2,1)}), bf16[16,2,4352]{2,1,0:T(2,128)(2,1)S(1)}, u32[]{:S(2)}, u32[]{:S(2)}) async-start(bf16[16,2,4352]{2,1,0:T(2,128)(2,1)} %reshape.242), calls=%async_computation | async-start | bytes 557056 | tf_op jit(solution)/shard_map/all_to_all | solution.py:72
  32.9 77.7 %all-to-all-start.1 = ((bf16[16,64,512]{2,1,0:T(8,128)(2,1)}), bf16[16,64,512]{2,1,0:T(8,128)(2,1)S(1)}, u32[]{:S(2)}, u32[]{:S(2)}) async-start(bf16[16,64,512]{2,1,0:T(8,128)(2,1)} %bitcast.110), calls=%async_computation.1 | async-start | bytes 2097152 | tf_op jit(solution)/shard_map/all_to_all | solution.py:78
  39.6 0.8 copy-start.28
  39.6 0.8 copy-start.32
  43.3 54.3 %copy-start.5 = (bf16[1024,128]{1,0:T(8,128)(2,1)}, bf16[1024,128]{1,0:T(8,128)(2,1)S(1)}, u32[]{:S(2)}) copy-start(bf16[1024,128]{1,0:T(8,128)(2,1)S(1)} %reshape.205) | copy-start | bytes 786436
  43.7 45.7 %collective-permute-start = (bf16[1024,128]{1,0:T(8,128)(2,1)S(1)}, bf16[1024,128]{1,0:T(8,128)(2,1)S(1)}, u32[]{:S(2)}, u32[]{:S(2)}) collective-permute-start(bf16[1024,128]{1,0:T(8,128)(2,1)S(1)} %multiply_convert_fusion.6), channel_id=1, source_target_pairs={{0,2},{1,3},{2,0},{3,1},{4,6},{5,7},{6,4},{7,5},{8,10},{9,11},{10,... | collective-permute-start | bytes 786440 | tf_op jit(solution)/shard_map/ppermute | solution.py:87
  47.1 48.6 %copy-start.29 = (f32[8]{0:T(128)}, f32[8]{0:T(128)S(1)}, u32[]{:S(2)}) copy-start(f32[8]{0:T(128)S(1)} %slice_reduce_fusion.1) | copy-start | bytes 100
  89.5 8.1 %collective-permute-start.1 = (bf16[2,1024,128]{2,1,0:T(8,128)(2,1)S(1)}, bf16[2,1024,128]{2,1,0:T(8,128)(2,1)S(1)}, u32[]{:S(2)}, u32[]{:S(2)}) collective-permute-start(bf16[2,1024,128]{2,1,0:T(8,128)(2,1)S(1)} %pad_maximum_fusion.3), channel_id=1, source_target_pairs={{0,1},{1,0},{2,3},{3,2},{4,5},{5,4},{6,7},{7,6},{8,9},{9,8},{10,11... | collective-permute-start | bytes 1572872 | tf_op jit(solution)/shard_map/ppermute | solution.py:91
  98.5 1.4 copy-start.6
  98.6 1.4 copy-start.17
  100.0 4.0 %copy-start.8 = (pred[256,768]{1,0:T(8,128)(4,1)S(1)}, pred[256,768]{1,0:T(8,128)(4,1)}, u32[]{:S(2)}) copy-start(pred[256,768]{1,0:T(8,128)(4,1)} %iota_compare_fusion.1) | copy-start | bytes 589828
  100.0 4.0 %copy-start.10 = (f32[8,768]{1,0:T(8,128)S(1)}, f32[8,768]{1,0:T(8,128)}, u32[]{:S(2)}) copy-start(f32[8,768]{1,0:T(8,128)} %slice.206) | copy-start | bytes 73732
  100.0 4.0 %copy-start.11 = (f32[8,768]{1,0:T(8,128)S(1)}, f32[8,768]{1,0:T(8,128)}, u32[]{:S(2)}) copy-start(f32[8,768]{1,0:T(8,128)} %slice.207) | copy-start | bytes 73732
  100.0 4.0 %copy-start.16 = (f32[8,256]{1,0:T(8,128)S(1)}, f32[8,256]{1,0:T(8,128)}, u32[]{:S(2)}) copy-start(f32[8,256]{1,0:T(8,128)} %get-tuple-element.10) | copy-start | bytes 24580
  104.0 3.3 %copy-start.9 = (pred[256,512]{1,0:T(8,128)(4,1)S(1)}, pred[256,512]{1,0:T(8,128)(4,1)}, u32[]{:S(2)}) copy-start(pred[256,512]{1,0:T(8,128)(4,1)} %iota_compare_fusion.2) | copy-start | bytes 393220
  104.0 3.3 %copy-start.12 = (f32[8,512]{1,0:T(8,128)S(1)}, f32[8,512]{1,0:T(8,128)}, u32[]{:S(2)}) copy-start(f32[8,512]{1,0:T(8,128)} %slice.201) | copy-start | bytes 49156
  104.0 3.3 %copy-start.13 = (f32[8,512]{1,0:T(8,128)S(1)}, f32[8,512]{1,0:T(8,128)}, u32[]{:S(2)}) copy-start(f32[8,512]{1,0:T(8,128)} %slice.200) | copy-start | bytes 49156
  104.0 3.3 %copy-start.15 = (f32[8,256]{1,0:T(8,128)S(1)}, f32[8,256]{1,0:T(8,128)}, u32[]{:S(2)}) copy-start(f32[8,256]{1,0:T(8,128)} %get-tuple-element.11) | copy-start | bytes 24580
  107.1 2.8 %copy-start.14 = (f32[8,256]{1,0:T(8,128)S(1)}, f32[8,256]{1,0:T(8,128)}, u32[]{:S(2)}) copy-start(f32[8,256]{1,0:T(8,128)} %slice.191) | copy-start | bytes 24580
  109.9 1.7 copy-start.22
  109.9 1.7 copy-start.23
  109.9 1.7 copy-start.24
  109.9 1.7 copy-start.25
  109.9 1.7 copy-start.26
  110.6 1.0 copy-start.4
  115.3 3.7 %copy-start.2 = (bf16[8,256,768]{2,1,0:T(8,128)(2,1)S(1)}, bf16[8,256,768]{2,1,0:T(8,128)(2,1)}, u32[]{:S(2)}) copy-start(bf16[8,256,768]{2,1,0:T(8,128)(2,1)} %select_convert_fusion.1) | copy-start | bytes 9437188
  119.0 1.6 copy-start.3
  120.6 1.2 copy-start.18
  120.6 1.2 copy-start.33
  120.6 1.2 copy-start.34
  125.5 10.4 %copy-start.20 = (bf16[8192]{0:T(1024)(128)(2,1)S(1)}, bf16[8192]{0:T(1024)(128)(2,1)}, u32[]{:S(2)}) copy-start(bf16[8192]{0:T(1024)(128)(2,1)} %param.27) | copy-start | bytes 49156
  125.5 10.5 %copy-start.30 = (f32[8]{0:T(128)S(1)}, f32[8]{0:T(128)}, u32[]{:S(2)}) copy-start(f32[8]{0:T(128)} %copy-done.29) | copy-start | bytes 100
  128.8 9.8 %copy-start.19 = (f32[1024,8]{0,1:T(8,128)S(1)}, f32[1024,8]{0,1:T(8,128)}, u32[]{:S(2)}) copy-start(f32[1024,8]{0,1:T(8,128)} %get-tuple-element.4) | copy-start | bytes 98308
  128.8 55.7 %all-to-all-start.2 = ((bf16[16,64,512]{2,1,0:T(8,128)(2,1)}), bf16[16,64,512]{2,1,0:T(8,128)(2,1)S(1)}, u32[]{:S(2)}, u32[]{:S(2)}) async-start(bf16[16,64,512]{2,1,0:T(8,128)(2,1)} %copy.140), calls=%async_computation.2 | async-start | bytes 2097152 | tf_op jit(solution)/shard_map/all_to_all | solution.py:156

commit v5 on v4

--- a/solution.py
+++ b/solution.py
@@ -74,10 +74,6 @@
     head_bc_part = small_recv[:, :bc_end].reshape(length, bc_width)
     head_step = small_recv[:, bc_end:].reshape(length, heads_here)
 
-    x_send = jnp.transpose(inner_x.reshape(token_rows, tensor_count, x_width), (1, 0, 2))
-    x_recv = lax.all_to_all(x_send, TENSOR, 0, 0, tiled=True)
-    head_x = x_recv.reshape(length, x_width)
-
     column_start = device_rank * bc_width
     own_state_bc = lax.dynamic_slice_in_dim(conv_state_bc, column_start, bc_width, 1)
     own_weight_bc = lax.dynamic_slice_in_dim(conv_weight_bc, column_start, bc_width, 1)
@@ -94,6 +90,10 @@
     order = slot_of[jnp.arange(group_size, dtype=jnp.int32) ^ group_rank]
     ordered = jnp.take(stacked, order, axis=0)
     mixed_bc = jnp.transpose(ordered, (1, 0, 2)).reshape(length, group_size * bc_width)
+    x_send = jnp.transpose(inner_x.reshape(token_rows, tensor_count, x_width), (1, 0, 2))
+    x_send, mixed_bc = lax.optimization_barrier((x_send, mixed_bc))
+    x_recv = lax.all_to_all(x_send, TENSOR, 0, 0, tiled=True)
+    head_x = x_recv.reshape(length, x_width)
     input_map = mixed_bc[:, :STATE]
     output_map = mixed_bc[:, STATE:]
 

time: 189 us -> 184 us (0.974)
  the two profiles are of different devices: /device:TPU:95 before, /device:TPU:81 now
where the time goes in v5:
time: 184 us; the launch traced here: 183 us
  waiting for transfers between devices  96.7 us (53%)
  starting transfers between devices  31 us (17%)
  other arithmetic  22.1 us (12%)
  local copies, waits for them, and re-layouts  20.2 us (11%)
  matrix products  11.8 us (6%)
    all_to_all x1, waiting for transfers between devices, local(): lax.all_to_all(mixed_y, TENSOR, split_axis=0, concat_axis=1, tiled=True)  42.6 us
    all_to_all x1, waiting for transfers between devices, local(): x_recv = lax.all_to_all(x_send, TENSOR, 0, 0, tiled=True)  34.4 us
    all_to_all x1, waiting for transfers between devices, local(): small_recv = lax.all_to_all(small_send, TENSOR, 0, 0, tiled=True)  12.5 us
    all_to_all x1, starting transfers between devices, local(): small_recv = lax.all_to_all(small_send, TENSOR, 0, 0, tiled=True)  12.5 us
    convert_element_type x4, other arithmetic, local(): weights = jnp.where(causal[None], scores[None] * decayed * step_cols[:, N...  9.48 us
    all_to_all x1, starting transfers between devices, local(): x_recv = lax.all_to_all(x_send, TENSOR, 0, 0, tiled=True)  6.93 us
    all_to_all x1, starting transfers between devices, local(): lax.all_to_all(mixed_y, TENSOR, split_axis=0, concat_axis=1, tiled=True)  6.71 us
    ppermute x1, waiting for transfers between devices, local(): lax.ppermute(mixed_bc_part, 'tj', [(source, source ^ 2) for source in ran...  6.29 us
  transfers between devices with their start and end apart: 5, of which 5 were waited for; matrix products, arithmetic and copies ran while one was open for 14% of the time, Pallas kernels for 0%

profile of v5, /device:TPU:81, one launch (start us, length us, event | category | flops | bytes accessed | tf_op | source)
XLA Modules:
  0.0 183.0 jit_solution(6820100267710470491)
XLA Ops:
  0.7 0.9 copy.129
  1.8 0.2 copy.163
  2.1 0.5 broadcast.163
  2.6 0.8 reduce.7
  3.4 0.8 reshape.242
  4.2 12.5 %all-to-all-start = ((bf16[16,2,4352]{2,1,0:T(2,128)(2,1)}), bf16[16,2,4352]{2,1,0:T(2,128)(2,1)S(1)}, u32[]{:S(2)}, u32[]{:S(2)}) async-start(bf16[16,2,4352]{2,1,0:T(2,128)(2,1)} %reshape.242), calls=%async_computation | async-start | bytes 557056 | tf_op jit(solution)/shard_map/all_to_all | solution.py:72
  16.7 0.7 dynamic-slice_convert_fusion
  17.4 0.7 constant_dynamic-slice_fusion
  18.1 0.6 gather_fusion
  18.7 0.8 dynamic-slice_convert_fusion.1
  19.5 0.6 slice_convert_fusion.5
  20.3 12.5 %all-to-all-done = bf16[16,2,4352]{2,1,0:T(2,128)(2,1)S(1)} async-done(((bf16[16,2,4352]{2,1,0:T(2,128)(2,1)}), bf16[16,2,4352]{2,1,0:T(2,128)(2,1)S(1)}, u32[]{:S(2)}, u32[]{:S(2)}) %all-to-all-start) | async-done | bytes 278560 | tf_op jit(solution)/shard_map/all_to_all | solution.py:72
  32.8 0.2 reshape.243
  33.3 0.4 multiply_convert_fusion.6
  33.7 2.4 %collective-permute-start = (bf16[1024,128]{1,0:T(8,128)(2,1)S(1)}, bf16[1024,128]{1,0:T(8,128)(2,1)S(1)}, u32[]{:S(2)}, u32[]{:S(2)}) collective-permute-start(bf16[1024,128]{1,0:T(8,128)(2,1)S(1)} %multiply_convert_fusion.6), channel_id=1, source_target_pairs={{0,2},{1,3},{2,0},{3,1},{4,6},{5,7},{6,4},{7,5},{8,10},{9,11},{10,... | collective-permute-start | bytes 786440 | tf_op jit(solution)/shard_map/ppermute | solution.py:83
  36.1 1.1 copy.161
  37.2 0.2 iota_compare_fusion.1
  37.4 6.3 %collective-permute-done = bf16[1024,128]{1,0:T(8,128)(2,1)S(1)} collective-permute-done((bf16[1024,128]{1,0:T(8,128)(2,1)S(1)}, bf16[1024,128]{1,0:T(8,128)(2,1)S(1)}, u32[]{:S(2)}, u32[]{:S(2)}) %collective-permute-start) | collective-permute-done | bytes 262176 | tf_op jit(solution)/shard_map/ppermute | solution.py:83
  43.8 2.5 %collective-permute-start.1 = (bf16[2,1024,128]{2,1,0:T(8,128)(2,1)S(1)}, bf16[2,1024,128]{2,1,0:T(8,128)(2,1)}, u32[]{:S(2)}, u32[]{:S(2)}) collective-permute-start(bf16[2,1024,128]{2,1,0:T(8,128)(2,1)S(1)} %pad_maximum_fusion.3), channel_id=1, source_target_pairs={{0,1},{1,0},{2,3},{3,2},{4,5},{5,4},{6,7},{7,6},{8,9},{9,8},{10,11... | collective-permute-start | bytes 1572872 | tf_op jit(solution)/shard_map/ppermute | solution.py:87
  46.3 0.2 iota_compare_fusion
  46.5 0.3 reshape.216
  46.9 0.2 copy.134
  47.0 0.9 collective-permute-done.1
  47.9 1.1 pad_maximum_fusion.1
  49.1 0.7 gather_fusion.1
  49.9 0.4 copy_bitcast_fusion
  50.2 6.9 %all-to-all-start.1 = ((bf16[16,64,512]{2,1,0:T(8,128)(2,1)}), bf16[16,64,512]{2,1,0:T(8,128)(2,1)S(1)}, u32[]{:S(2)}, u32[]{:S(2)}) async-start(bf16[16,64,512]{2,1,0:T(8,128)(2,1)} %bitcast.110), calls=%async_computation.1 | async-start | bytes 2097152 | tf_op jit(solution)/shard_map/all_to_all | solution.py:95
  57.3 2.3 %reduce-window.6 = f32[8,8,128]{2,1,0:T(8,128)S(1)} reduce-window(f32[8,8,128]{2,1,0:T(8,128)S(1)} %copy.135, f32[]{:T(128)} %constant.50.clone.1), window={size=1x1x128 pad=0_0x0_0x127_0}, to_apply=%region_0.1 | reduce-window | flops 1040384 | bytes 65540 | tf_op jit(solution)/shard_map/reduce-window
  59.6 0.2 slice_reduce_fusion
  59.7 0.2 reduce-window.9
  60.0 0.2 slice_reduce_fusion.1
  60.3 0.4 copy-done.14
  60.7 0.3 fusion.32
  61.1 3.7 %select_convert_fusion = bf16[8,256,1024]{2,1,0:T(8,128)(2,1)} fusion(f32[8,1024]{1,0:T(8,128)S(1)} %get-tuple-element.9, f32[8,1024]{1,0:T(8,128)S(1)} %bitcast.139, f32[8,256]{1,0:T(8,128)S(1)} %get-tuple-element.13, f32[256,1024]{1,0:T(8,128)S(1)} %fusion.32, pred[256,1024]{1,0:T(8,128)(4,1)S(1)} %iota_compare_fusion), kind=kLoop, calls=%fused_computation.3 | loop fusion | flops 12582912 | bytes 5578752 | tf_op jit(solution)/shard_map/convert_element_type | solution.py:126
  64.7 0.3 fusion.34
  65.0 3.0 %select_convert_fusion.1 = bf16[8,256,768]{2,1,0:T(8,128)(2,1)} fusion(f32[8,768]{1,0:T(8,128)S(1)} %slice.201, f32[8,768]{1,0:T(8,128)S(1)} %slice.200, f32[8,256]{1,0:T(8,128)S(1)} %get-tuple-element.14, f32[256,768]{1,0:T(8,128)S(1)} %fusion.34, pred[256,768]{1,0:T(8,128)(4,1)S(1)} %iota_compare_fusion.1), kind=kLoop, calls=%fused_computation.4 | loop fusion | flops 9437184 | bytes 4186112 | tf_op jit(solution)/shard_map/convert_element_type | solution.py:126
  68.0 0.3 fusion.38
  68.2 2.3 %select_convert_fusion.2 = bf16[8,256,512]{2,1,0:T(8,128)(2,1)} fusion(f32[8,512]{1,0:T(8,128)S(1)} %slice.197, f32[8,512]{1,0:T(8,128)S(1)} %slice.196, f32[8,256]{1,0:T(8,128)S(1)} %get-tuple-element.15, f32[256,512]{1,0:T(8,128)S(1)} %fusion.38, pred[256,512]{1,0:T(8,128)(4,1)S(1)} %iota_compare_fusion.2), kind=kLoop, calls=%fused_computation.8 | loop fusion | flops 6291456 | bytes 2793472 | tf_op jit(solution)/shard_map/convert_element_type | solution.py:126
  70.5 0.2 fusion.43
  70.7 0.6 select_convert_fusion.3
  71.4 34.4 %all-to-all-done.1 = bf16[16,64,512]{2,1,0:T(8,128)(2,1)S(1)} async-done(((bf16[16,64,512]{2,1,0:T(8,128)(2,1)}), bf16[16,64,512]{2,1,0:T(8,128)(2,1)S(1)}, u32[]{:S(2)}, u32[]{:S(2)}) %all-to-all-start.1) | async-done | bytes 1048608 | tf_op jit(solution)/shard_map/all_to_all | solution.py:95
  105.8 0.3 bitcast_convert_fusion.4
  106.1 0.6 copy-done.4
  106.7 2.2 %multiply_convert_fusion.3 = bf16[1024,512]{1,0:T(8,128)(2,1)} fusion(f32[1024,512]{1,0:T(8,128)S(1)} %bitcast_convert_fusion.4, f32[3,512]{1,0:T(4,128)S(1)} %convert_element_type.101, f32[512]{0:T(512)S(1)} %bitcast.146, f32[512]{0:T(512)S(1)} %bitcast.147, f32[512]{0:T(512)S(1)} %bitcast.145, f32[512]{0:T(512)S(1)} %bitcast.144, ...), kind=kLoop, calls=%fused_computation.29 | loop fusion | flops 8388608 | bytes 3162112 | tf_op jit(solution)/shard_map/convert_element_type | solution.py:30
  108.9 1.5 copy.136
  110.4 3.7 %fusion.52 = f32[8,256,64]{1,2,0:T(8,128)S(1)} fusion(bf16[8,256,1024]{2,1,0:T(8,128)(2,1)} %select_convert_fusion, bf16[8,64,1024]{2,1,0:T(8,128)(2,1)S(1)} %bitcast.116), kind=kOutput, calls=%fused_computation.116 | convolution fusion | flops 268435456 | bytes 5767168 | tf_op jit(solution)/shard_map/hts,hps->htp/dot_general | solution.py:129
  114.2 1.1 fusion.17
  115.2 0.5 copy-done.3
  115.7 0.8 fusion.27
  116.5 0.4 fusion.36
  117.0 1.3 fusion.15
  118.3 2.3 %reshape.239 = bf16[16,64,512]{1,0,2:T(8,128)(2,1)} reshape(bf16[1024,8,64]{0,2,1:T(8,128)(2,1)S(1)} %fusion.15) | data formatting | bytes 2097152 | tf_op jit(solution)/shard_map/all_to_all | solution.py:156
  120.6 3.3 %copy.140 = bf16[16,64,512]{2,1,0:T(8,128)(2,1)} copy(bf16[16,64,512]{1,0,2:T(8,128)(2,1)} %reshape.239) | data formatting | bytes 2097152 | tf_op jit(solution)/shard_map/all_to_all | solution.py:156
  124.0 6.7 %all-to-all-start.2 = ((bf16[16,64,512]{2,1,0:T(8,128)(2,1)}), bf16[16,64,512]{2,1,0:T(8,128)(2,1)S(1)}, u32[]{:S(2)}, u32[]{:S(2)}) async-start(bf16[16,64,512]{2,1,0:T(8,128)(2,1)} %copy.140), calls=%async_computation.2 | async-start | bytes 2097152 | tf_op jit(solution)/shard_map/all_to_all | solution.py:156
  130.7 1.3 slice.206
  132.0 1.3 slice.205
  133.3 3.3 %fusion.16 = f32[8,64,256]{2,1,0:T(8,128)} fusion(bf16[8,64,1024]{2,1,0:T(8,128)(2,1)S(1)} %bitcast.121, f32[1024,8]{0,1:T(8,128)S(1)} %get-tuple-element.8, f32[1024,256]{1,0:T(8,128)S(1)} %slice_convert_fusion, f32[8,64,256]{2,1,0:T(8,128)} %param.28, f32[8]{0:T(128)S(1)} %exp.49), kind=kOutput, calls=%fused_computation.32 | convolution fusion | flops 272891904 | bytes 3178528 | tf_op jit(solution)/shard_map/hps,shn->hpn/dot_general | solution.py:151
  136.7 42.6 %all-to-all-done.2 = bf16[16,64,512]{2,1,0:T(8,128)(2,1)S(1)} async-done(((bf16[16,64,512]{2,1,0:T(8,128)(2,1)}), bf16[16,64,512]{2,1,0:T(8,128)(2,1)S(1)}, u32[]{:S(2)}, u32[]{:S(2)}) %all-to-all-start.2) | async-done | bytes 1048608 | tf_op jit(solution)/shard_map/all_to_all | solution.py:156
  179.3 0.3 convert_bitcast_fusion
  179.6 0.2 copy.145
  179.8 0.3 fusion.3
  180.2 0.3 mul.317
  180.5 1.2 copy.148
  181.7 1.3 multiply_convert_fusion.2
  (78 shorter events, 1.4 us)
Async XLA Ops:
  0.6 1.1 copy-start
  0.6 17.4 %copy-start.1 = (s32[4]{0:T(128)S(1)}, s32[4]{0:T(128)}, u32[]{:S(2)}) copy-start(s32[4]{0:T(128)} %constant.56.clone) | copy-start | bytes 52
  1.5 18.0 %copy-start.8 = (bf16[4,512]{1,0:T(4,128)(2,1)S(1)}, bf16[4,512]{1,0:T(4,128)(2,1)}, u32[]{:S(2)}) copy-start(bf16[4,512]{1,0:T(4,128)(2,1)} %param.20) | copy-start | bytes 12292
  4.2 28.6 %all-to-all-start = ((bf16[16,2,4352]{2,1,0:T(2,128)(2,1)}), bf16[16,2,4352]{2,1,0:T(2,128)(2,1)S(1)}, u32[]{:S(2)}, u32[]{:S(2)}) async-start(bf16[16,2,4352]{2,1,0:T(2,128)(2,1)} %reshape.242), calls=%async_computation | async-start | bytes 557056 | tf_op jit(solution)/shard_map/all_to_all | solution.py:72
  20.3 15.9 %copy-start.6 = (bf16[64,8192]{1,0:T(8,128)(2,1)S(1)}, bf16[64,8192]{1,0:T(8,128)(2,1)}, u32[]{:S(2)}) copy-start(bf16[64,8192]{1,0:T(8,128)(2,1)} %param.15) | copy-start | bytes 3145732
  33.1 4.1 %copy-start.12 = (bf16[3,512]{1,0:T(4,128)(2,1)S(1)}, bf16[3,512]{1,0:T(4,128)(2,1)}, u32[]{:S(2)}) copy-start(bf16[3,512]{1,0:T(4,128)(2,1)} %param.18) | copy-start | bytes 9220
  33.1 4.1 %copy-start.16 = (bf16[512]{0:T(512)(128)(2,1)S(1)}, bf16[512]{0:T(512)(128)(2,1)}, u32[]{:S(2)}) copy-start(bf16[512]{0:T(512)(128)(2,1)} %param.21) | copy-start | bytes 3076
  33.3 10.5 %copy-start.5 = (bf16[1024,128]{1,0:T(8,128)(2,1)}, bf16[1024,128]{1,0:T(8,128)(2,1)S(1)}, u32[]{:S(2)}) copy-start(bf16[1024,128]{1,0:T(8,128)(2,1)S(1)} %reshape.206) | copy-start | bytes 786436
  33.7 10.0 %collective-permute-start = (bf16[1024,128]{1,0:T(8,128)(2,1)S(1)}, bf16[1024,128]{1,0:T(8,128)(2,1)S(1)}, u32[]{:S(2)}, u32[]{:S(2)}) collective-permute-start(bf16[1024,128]{1,0:T(8,128)(2,1)S(1)} %multiply_convert_fusion.6), channel_id=1, source_target_pairs={{0,2},{1,3},{2,0},{3,1},{4,6},{5,7},{6,4},{7,5},{8,10},{9,11},{10,... | collective-permute-start | bytes 786440 | tf_op jit(solution)/shard_map/ppermute | solution.py:83
  43.8 4.2 %collective-permute-start.1 = (bf16[2,1024,128]{2,1,0:T(8,128)(2,1)S(1)}, bf16[2,1024,128]{2,1,0:T(8,128)(2,1)}, u32[]{:S(2)}, u32[]{:S(2)}) collective-permute-start(bf16[2,1024,128]{2,1,0:T(8,128)(2,1)S(1)} %pad_maximum_fusion.3), channel_id=1, source_target_pairs={{0,1},{1,0},{2,3},{3,2},{4,5},{5,4},{6,7},{7,6},{8,9},{9,8},{10,11... | collective-permute-start | bytes 1572872 | tf_op jit(solution)/shard_map/ppermute | solution.py:87
  49.8 7.3 %copy-start.13 = (f32[8]{0:T(128)S(1)}, f32[8]{0:T(128)}, u32[]{:S(2)}) copy-start(f32[8]{0:T(128)} %param.24) | copy-start | bytes 100
  49.9 7.3 %copy-start.17 = (f32[8]{0:T(128)S(1)}, f32[8]{0:T(128)}, u32[]{:S(2)}) copy-start(f32[8]{0:T(128)} %param.25) | copy-start | bytes 100
  50.2 55.5 %all-to-all-start.1 = ((bf16[16,64,512]{2,1,0:T(8,128)(2,1)}), bf16[16,64,512]{2,1,0:T(8,128)(2,1)S(1)}, u32[]{:S(2)}, u32[]{:S(2)}) async-start(bf16[16,64,512]{2,1,0:T(8,128)(2,1)} %bitcast.110), calls=%async_computation.1 | async-start | bytes 2097152 | tf_op jit(solution)/shard_map/all_to_all | solution.py:95
  60.2 0.5 copy-start.14
  71.3 35.4 %copy-start.9 = (f32[1,512]{1,0:T(1,128)S(1)}, f32[1,512]{1,0:T(1,128)}, u32[]{:S(2)}) copy-start(f32[1,512]{1,0:T(1,128)} %get-tuple-element.17) | copy-start | bytes 6148
  71.3 35.4 %copy-start.10 = (f32[1,512]{1,0:T(1,128)S(1)}, f32[1,512]{1,0:T(1,128)}, u32[]{:S(2)}) copy-start(f32[1,512]{1,0:T(1,128)} %get-tuple-element.18) | copy-start | bytes 6148
  71.3 35.4 %copy-start.11 = (f32[1,512]{1,0:T(1,128)S(1)}, f32[1,512]{1,0:T(1,128)}, u32[]{:S(2)}) copy-start(f32[1,512]{1,0:T(1,128)} %get-tuple-element.19) | copy-start | bytes 6148
  105.8 1.0 copy-start.4
  110.4 3.7 %copy-start.2 = (bf16[8,256,768]{2,1,0:T(8,128)(2,1)S(1)}, bf16[8,256,768]{2,1,0:T(8,128)(2,1)}, u32[]{:S(2)}) copy-start(bf16[8,256,768]{2,1,0:T(8,128)(2,1)} %select_convert_fusion.1) | copy-start | bytes 9437188
  114.1 1.6 copy-start.3
  115.7 1.2 copy-start.18
  115.7 1.2 copy-start.19
  120.6 10.0 %copy-start.7 = (bf16[8192]{0:T(1024)(128)(2,1)S(1)}, bf16[8192]{0:T(1024)(128)(2,1)}, u32[]{:S(2)}) copy-start(bf16[8192]{0:T(1024)(128)(2,1)} %param.27) | copy-start | bytes 49156
  120.6 10.1 %copy-start.15 = (f32[8]{0:T(128)S(1)}, f32[8]{0:T(128)}, u32[]{:S(2)}) copy-start(f32[8]{0:T(128)} %copy-done.14) | copy-start | bytes 100
  124.0 55.3 %all-to-all-start.2 = ((bf16[16,64,512]{2,1,0:T(8,128)(2,1)}), bf16[16,64,512]{2,1,0:T(8,128)(2,1)S(1)}, u32[]{:S(2)}, u32[]{:S(2)}) async-start(bf16[16,64,512]{2,1,0:T(8,128)(2,1)} %copy.140), calls=%async_computation.2 | async-start | bytes 2097152 | tf_op jit(solution)/shard_map/all_to_all | solution.py:156

commit v6 on v4

--- a/solution.py
+++ b/solution.py
@@ -64,30 +64,55 @@
     bc_width = inner_bc.shape[1] // tensor_count
     length = tensor_count * token_rows
 
-    bc_send = jnp.transpose(inner_bc.reshape(token_rows, tensor_count, bc_width), (1, 0, 2))
+    quarters = inner_bc.reshape(token_rows, GROUPS, 2, group_size // 2, bc_width)
+    across_quarters = jnp.flip(quarters, axis=2)
+    bc_send = jnp.stack([quarters, across_quarters], axis=4).reshape(
+        token_rows, tensor_count, 2, bc_width
+    )
+    bc_send = jnp.transpose(bc_send, (1, 0, 2, 3))
+    x_send = jnp.transpose(inner_x.reshape(token_rows, tensor_count, x_width), (1, 0, 2))
     step_send = jnp.transpose(step_raw.reshape(token_rows, tensor_count, heads_here), (1, 0, 2))
-    small_send = jnp.concatenate(
-        [bc_send.reshape(tensor_count, -1), step_send.reshape(tensor_count, -1)], axis=1
-    )
-    small_recv = lax.all_to_all(small_send, TENSOR, 0, 0, tiled=True)
-    bc_end = token_rows * bc_width
-    head_bc_part = small_recv[:, :bc_end].reshape(length, bc_width)
-    head_step = small_recv[:, bc_end:].reshape(length, heads_here)
-
-    x_send = jnp.transpose(inner_x.reshape(token_rows, tensor_count, x_width), (1, 0, 2))
-    x_recv = lax.all_to_all(x_send, TENSOR, 0, 0, tiled=True)
-    head_x = x_recv.reshape(length, x_width)
-
+    send = jnp.concatenate(
+        [
+            x_send.reshape(tensor_count, -1),
+            bc_send.reshape(tensor_count, -1),
+            step_send.reshape(tensor_count, -1),
+        ],
+        axis=1,
+    )
+    recv = lax.all_to_all(send, TENSOR, 0, 0, tiled=True)
+    x_end = token_rows * x_width
+    bc_end = x_end + token_rows * 2 * bc_width
+    head_x = recv[:, :x_end].reshape(length, x_width)
+    head_bc_pair = recv[:, x_end:bc_end].reshape(length, 2 * bc_width)
+    head_step = recv[:, bc_end:].reshape(length, heads_here)
+
+    group_rank = lax.axis_index("tj")
     column_start = device_rank * bc_width
-    own_state_bc = lax.dynamic_slice_in_dim(conv_state_bc, column_start, bc_width, 1)
-    own_weight_bc = lax.dynamic_slice_in_dim(conv_weight_bc, column_start, bc_width, 1)
-    own_bias_bc = lax.dynamic_slice_in_dim(conv_bias_bc, column_start, bc_width, 0)
-    mixed_bc_part = causal_conv(head_bc_part, own_state_bc, own_weight_bc, own_bias_bc)
-    group_rank = lax.axis_index("tj")
-    across = lax.ppermute(
-        mixed_bc_part, "tj", [(source, source ^ 2) for source in range(group_size)]
-    )
-    pair = jnp.stack([mixed_bc_part, across])
+    across_start = (device_rank ^ 2) * bc_width
+    pair_state_bc = jnp.concatenate(
+        [
+            lax.dynamic_slice_in_dim(conv_state_bc, column_start, bc_width, 1),
+            lax.dynamic_slice_in_dim(conv_state_bc, across_start, bc_width, 1),
+        ],
+        axis=1,
+    )
+    pair_weight_bc = jnp.concatenate(
+        [
+            lax.dynamic_slice_in_dim(conv_weight_bc, column_start, bc_width, 1),
+            lax.dynamic_slice_in_dim(conv_weight_bc, across_start, bc_width, 1),
+        ],
+        axis=1,
+    )
+    pair_bias_bc = jnp.concatenate(
+        [
+            lax.dynamic_slice_in_dim(conv_bias_bc, column_start, bc_width, 0),
+            lax.dynamic_slice_in_dim(conv_bias_bc, across_start, bc_width, 0),
+        ],
+        axis=0,
+    )
+    mixed_pair = causal_conv(head_bc_pair, pair_state_bc, pair_weight_bc, pair_bias_bc)
+    pair = jnp.transpose(mixed_pair.reshape(length, 2, bc_width), (1, 0, 2))
     beside = lax.ppermute(pair, "tj", [(source, source ^ 1) for source in range(group_size)])
     stacked = jnp.concatenate([pair, beside], axis=0)
     slot_of = jnp.array([0, 2, 1, 3], dtype=jnp.int32)
@@ -156,7 +181,7 @@
     token_y = lax.all_to_all(mixed_y, TENSOR, split_axis=0, concat_axis=1, tiled=True)
     normed = group_norm(token_y, norm_weight)
     tail_x = head_x[length - CONV_K + 1 :]
-    tail_bc = head_bc_part[length - CONV_K + 1 :]
+    tail_bc = head_bc_pair[length - CONV_K + 1 :, :bc_width]
     return (normed, final_state, tail_x, tail_bc)
 
 

time: 189 us -> 198 us (1.048)
  the two profiles are of different devices: /device:TPU:95 before, /device:TPU:65 now
where the time goes in v6:
time: 198 us; the launch traced here: 197 us
  waiting for transfers between devices  106 us (54%)
  local copies, waits for them, and re-layouts  36.3 us (18%)
  other arithmetic  22.5 us (11%)
  starting transfers between devices  21.5 us (11%)
  matrix products  9.34 us (5%)
    all_to_all x1, waiting for transfers between devices, local(): recv = lax.all_to_all(send, TENSOR, 0, 0, tiled=True)  63.5 us
    all_to_all x1, waiting for transfers between devices, local(): lax.all_to_all(mixed_y, TENSOR, split_axis=0, concat_axis=1, tiled=True)  42.6 us
    unnamed x76, local copies, waits for them, and re-layouts  14.3 us
    all_to_all x1, starting transfers between devices, local(): recv = lax.all_to_all(send, TENSOR, 0, 0, tiled=True)  12.6 us
    all_to_all x1, starting transfers between devices, local(): lax.all_to_all(mixed_y, TENSOR, split_axis=0, concat_axis=1, tiled=True)  6.78 us
    convert_element_type x4, other arithmetic, local(): weights = jnp.where(causal[None], scores[None] * decayed * step_cols[:, N...  6.03 us
    all_to_all x2, local copies, waits for them, and re-layouts, local(): lax.all_to_all(mixed_y, TENSOR, split_axis=0, concat_axis=1, tiled=True)  5.63 us
  transfers between devices with their start and end apart: 3, of which 2 were waited for; matrix products, arithmetic and copies ran while one was open for 10% of the time, Pallas kernels for 0%

profile of v6, /device:TPU:65, one launch (start us, length us, event | category | flops | bytes accessed | tf_op | source)
XLA Modules:
  0.0 197.2 jit_solution(4166465773582823298)
XLA Ops:
  0.6 0.8 copy.185
  1.7 1.1 reshape.228
  2.8 1.1 copy.205
  4.2 0.5 copy.184
  4.7 0.4 reshape.229
  5.2 0.6 copy.204
  5.9 0.5 broadcast.162
  6.5 1.9 reduce.7
  8.3 1.4 reshape.269
  9.7 12.6 %all-to-all-start = ((bf16[16,2,24832]{2,1,0:T(2,128)(2,1)}), bf16[16,2,24832]{2,1,0:T(2,128)(2,1)}, u32[]{:S(2)}, u32[]{:S(2)}) async-start(bf16[16,2,24832]{2,1,0:T(2,128)(2,1)} %reshape.269), calls=%async_computation | async-start | bytes 3178496 | tf_op jit(solution)/shard_map/all_to_all | solution.py:83
  22.4 0.6 gather_fusion
  23.1 0.8 fusion.57
  23.9 0.6 maximum_convert_fusion.1
  24.5 0.7 constant_dynamic-slice_fusion.1
  25.2 0.7 constant_dynamic-slice_fusion.3
  25.9 0.6 pad_clamp_fusion
  26.5 0.6 fusion.49
  27.1 0.5 compare_and_fusion
  27.6 0.6 slice_convert_fusion.5
  28.2 0.8 iota_compare_fusion.2
  29.0 0.9 iota_compare_fusion.1
  30.1 63.5 %all-to-all-done = bf16[16,2,24832]{2,1,0:T(2,128)(2,1)} async-done(((bf16[16,2,24832]{2,1,0:T(2,128)(2,1)}), bf16[16,2,24832]{2,1,0:T(2,128)(2,1)}, u32[]{:S(2)}, u32[]{:S(2)}) %all-to-all-start) | async-done | bytes 1589280 | tf_op jit(solution)/shard_map/all_to_all | solution.py:83
  93.6 8.9 %reshape.270 = bf16[16,1,49664]{2,1,0:T(2,128)(2,1)S(1)} reshape(bf16[16,2,24832]{2,1,0:T(2,128)(2,1)} %all-to-all-done) | data formatting | bytes 3178496
  102.8 0.3 reshape.243
  103.4 2.3 %reduce-window.6 = f32[8,8,128]{2,1,0:T(8,128)S(1)} reduce-window(f32[8,8,128]{2,1,0:T(8,128)S(1)} %copy.193, f32[]{:T(128)} %constant.52.clone.1), window={size=1x1x128 pad=0_0x0_0x127_0}, to_apply=%region_0.1 | reduce-window | flops 1040384 | bytes 65540 | tf_op jit(solution)/shard_map/reduce-window
  106.3 0.5 reshape.237
  107.3 0.7 multiply_convert_fusion.6
  108.2 0.3 copy.190
  108.5 2.1 %collective-permute-start = (bf16[2,1024,128]{2,1,0:T(8,128)(2,1)S(1)}, bf16[2,1024,128]{2,1,0:T(8,128)(2,1)}, u32[]{:S(2)}, u32[]{:S(2)}) collective-permute-start(bf16[2,1024,128]{2,1,0:T(8,128)(2,1)S(1)} %bitcast.118), channel_id=1, source_target_pairs={{0,1},{1,0},{2,3},{3,2},{4,5},{5,4},{6,7},{7,6},{8,9},{9,8},{10,11... | collective-permute-start | bytes 1572872 | tf_op jit(solution)/shard_map/ppermute | solution.py:116
  110.6 0.3 convert_element_type.106
  111.0 1.4 multiply_convert_fusion.3
  112.4 0.7 exponential_multiply_fusion
  113.1 0.6 slice.211
  113.7 0.6 slice.217
  114.3 0.6 slice.212
  114.9 0.6 slice.218
  115.5 0.5 copy.194
  116.0 0.6 fusion.56
  116.6 0.6 fusion.54
  117.3 1.1 pad_maximum_fusion.2
  118.4 0.9 gather_fusion.1
  119.3 0.9 copy_bitcast_fusion.1
  120.7 0.3 fusion.32
  121.0 0.3 fusion.30
  121.4 0.6 select_convert_fusion.3
  122.0 1.3 select_convert_fusion.2
  123.4 0.4 fusion.36
  123.8 0.8 fusion.28
  124.6 1.8 select_convert_fusion.1
  126.4 1.1 fusion.26
  127.5 2.3 %select_convert_fusion = bf16[8,256,1024]{2,1,0:T(8,128)(2,1)S(1)} fusion(f32[8,1024]{1,0:T(8,128)S(1)} %get-tuple-element.9, f32[8,1024]{1,0:T(8,128)S(1)} %bitcast.128, f32[8,256]{1,0:T(8,128)S(1)} %copy-done.10, f32[256,1024]{1,0:T(8,128)S(1)} %fusion.30, pred[256,1024]{1,0:T(8,128)(4,1)S(1)} %iota_compare_fusion), kind=kLoop, calls=%fused_computation.3 | loop fusion | flops 12582912 | bytes 5578752 | tf_op jit(solution)/shard_map/convert_element_type | solution.py:151
  129.9 1.4 fusion.58
  131.3 1.3 fusion.15
  132.6 2.3 %reshape.266 = bf16[16,64,512]{1,0,2:T(8,128)(2,1)} reshape(bf16[1024,8,64]{0,2,1:T(8,128)(2,1)S(1)} %fusion.15) | data formatting | bytes 2097152 | tf_op jit(solution)/shard_map/all_to_all | solution.py:181
  134.9 3.3 %copy.199 = bf16[16,64,512]{2,1,0:T(8,128)(2,1)} copy(bf16[16,64,512]{1,0,2:T(8,128)(2,1)} %reshape.266) | data formatting | bytes 2097152 | tf_op jit(solution)/shard_map/all_to_all | solution.py:181
  138.2 6.8 %all-to-all-start.1 = ((bf16[16,64,512]{2,1,0:T(8,128)(2,1)}), bf16[16,64,512]{2,1,0:T(8,128)(2,1)S(1)}, u32[]{:S(2)}, u32[]{:S(2)}) async-start(bf16[16,64,512]{2,1,0:T(8,128)(2,1)} %copy.199), calls=%async_computation.1 | async-start | bytes 2097152 | tf_op jit(solution)/shard_map/all_to_all | solution.py:181
  145.0 1.3 slice.226
  146.3 1.3 slice.225
  147.6 3.4 %fusion.16 = f32[8,64,256]{2,1,0:T(8,128)} fusion(bf16[8,64,1024]{2,1,0:T(8,128)(2,1)S(1)} %bitcast.108, f32[1024,8]{0,1:T(8,128)S(1)} %copy-done.14, f32[1024,256]{1,0:T(8,128)S(1)} %slice_convert_fusion, f32[8,64,256]{2,1,0:T(8,128)} %param.28, f32[8]{0:T(128)S(1)} %exp.49), kind=kOutput, calls=%fused_computation.36 | convolution fusion | flops 272891904 | bytes 3178528 | tf_op jit(solution)/shard_map/hps,shn->hpn/dot_general | solution.py:176
  151.0 42.6 %all-to-all-done.1 = bf16[16,64,512]{2,1,0:T(8,128)(2,1)S(1)} async-done(((bf16[16,64,512]{2,1,0:T(8,128)(2,1)}), bf16[16,64,512]{2,1,0:T(8,128)(2,1)S(1)}, u32[]{:S(2)}, u32[]{:S(2)}) %all-to-all-start.1) | async-done | bytes 1048608 | tf_op jit(solution)/shard_map/all_to_all | solution.py:181
  194.0 0.3 convert_bitcast_fusion
  194.4 0.3 mul.321
  194.8 1.2 copy.207
  196.0 1.2 multiply_convert_fusion.2
  (112 shorter events, 3.9 us)
Async XLA Ops:
  2.8 2.3 %copy-start.3 = (bf16[64,8192]{1,0:T(8,128)(2,1)S(1)}, bf16[64,8192]{1,0:T(8,128)(2,1)}, u32[]{:S(2)}) copy-start(bf16[64,8192]{1,0:T(8,128)(2,1)} %param.15) | copy-start | bytes 3145732
  9.7 12.6 %copy-start.30 = (bf16[512]{0:T(512)(128)(2,1)S(1)}, bf16[512]{0:T(512)(128)(2,1)}, u32[]{:S(2)}) copy-start(bf16[512]{0:T(512)(128)(2,1)} %param.21) | copy-start | bytes 3076
  9.7 12.6 %copy-start.21 = (bf16[3,512]{1,0:T(4,128)(2,1)S(1)}, bf16[3,512]{1,0:T(4,128)(2,1)}, u32[]{:S(2)}) copy-start(bf16[3,512]{1,0:T(4,128)(2,1)} %param.18) | copy-start | bytes 9220
  9.7 12.7 %copy-start = (s32[4]{0:T(128)S(1)}, s32[4]{0:T(128)}, u32[]{:S(2)}) copy-start(s32[4]{0:T(128)} %constant.58.clone) | copy-start | bytes 52
  9.7 17.9 %copy-start.16 = (bf16[4,512]{1,0:T(4,128)(2,1)S(1)}, bf16[4,512]{1,0:T(4,128)(2,1)}, u32[]{:S(2)}) copy-start(bf16[4,512]{1,0:T(4,128)(2,1)} %param.20) | copy-start | bytes 12292
  9.7 83.9 %all-to-all-start = ((bf16[16,2,24832]{2,1,0:T(2,128)(2,1)}), bf16[16,2,24832]{2,1,0:T(2,128)(2,1)}, u32[]{:S(2)}, u32[]{:S(2)}) async-start(bf16[16,2,24832]{2,1,0:T(2,128)(2,1)} %reshape.269), calls=%async_computation | async-start | bytes 3178496 | tf_op jit(solution)/shard_map/all_to_all | solution.py:83
  102.6 0.7 copy-start.27
  102.6 0.7 copy-start.31
  106.3 6.1 %copy-start.28 = (f32[8]{0:T(128)}, f32[8]{0:T(128)S(1)}, u32[]{:S(2)}) copy-start(f32[8]{0:T(128)S(1)} %slice_reduce_fusion.1) | copy-start | bytes 100
  106.3 0.9 copy-start.22
  106.3 0.9 copy-start.23
  106.3 0.9 copy-start.24
  106.3 0.9 copy-start.25
  106.3 0.9 copy-start.26
  106.9 3.7 %copy-start.1 = (bf16[1024,512]{1,0:T(8,128)(2,1)}, bf16[1024,512]{1,0:T(8,128)(2,1)S(1)}, u32[]{:S(2)}) copy-start(bf16[1024,512]{1,0:T(8,128)(2,1)S(1)} %reshape.237) | copy-start | bytes 3145732
  107.1 1.0 copy-start.2
  108.2 2.7 %copy-start.17 = (f32[1,512]{1,0:T(1,128)S(1)}, f32[1,512]{1,0:T(1,128)}, u32[]{:S(2)}) copy-start(f32[1,512]{1,0:T(1,128)} %get-tuple-element.22) | copy-start | bytes 6148
  108.2 2.7 %copy-start.18 = (f32[1,512]{1,0:T(1,128)S(1)}, f32[1,512]{1,0:T(1,128)}, u32[]{:S(2)}) copy-start(f32[1,512]{1,0:T(1,128)} %get-tuple-element.23) | copy-start | bytes 6148
  108.2 2.7 %copy-start.19 = (f32[1,512]{1,0:T(1,128)S(1)}, f32[1,512]{1,0:T(1,128)}, u32[]{:S(2)}) copy-start(f32[1,512]{1,0:T(1,128)} %get-tuple-element.24) | copy-start | bytes 6148
  108.2 2.7 %copy-start.20 = (f32[1,512]{1,0:T(1,128)S(1)}, f32[1,512]{1,0:T(1,128)}, u32[]{:S(2)}) copy-start(f32[1,512]{1,0:T(1,128)} %get-tuple-element.25) | copy-start | bytes 6148
  108.5 8.8 %collective-permute-start = (bf16[2,1024,128]{2,1,0:T(8,128)(2,1)S(1)}, bf16[2,1024,128]{2,1,0:T(8,128)(2,1)}, u32[]{:S(2)}, u32[]{:S(2)}) collective-permute-start(bf16[2,1024,128]{2,1,0:T(8,128)(2,1)S(1)} %bitcast.118), channel_id=1, source_target_pairs={{0,1},{1,0},{2,3},{3,2},{4,5},{5,4},{6,7},{7,6},{8,9},{9,8},{10,11... | collective-permute-start | bytes 1572872 | tf_op jit(solution)/shard_map/ppermute | solution.py:116
  120.7 1.3 copy-start.5
  120.7 1.3 copy-start.8
  120.7 1.3 copy-start.9
  120.7 1.3 copy-start.12
  123.3 1.2 copy-start.4
  123.3 1.2 copy-start.6
  123.3 1.2 copy-start.7
  123.3 1.2 copy-start.11
  126.4 1.1 copy-start.10
  129.8 1.4 copy-start.13
  129.8 1.4 copy-start.32
  129.9 1.4 copy-start.33
  134.9 10.1 %copy-start.15 = (bf16[8192]{0:T(1024)(128)(2,1)S(1)}, bf16[8192]{0:T(1024)(128)(2,1)}, u32[]{:S(2)}) copy-start(bf16[8192]{0:T(1024)(128)(2,1)} %param.27) | copy-start | bytes 49156
  134.9 10.1 %copy-start.29 = (f32[8]{0:T(128)S(1)}, f32[8]{0:T(128)}, u32[]{:S(2)}) copy-start(f32[8]{0:T(128)} %copy-done.28) | copy-start | bytes 100
  138.2 9.4 %copy-start.14 = (f32[1024,8]{0,1:T(8,128)S(1)}, f32[1024,8]{0,1:T(8,128)}, u32[]{:S(2)}) copy-start(f32[1024,8]{0,1:T(8,128)} %get-tuple-element.8) | copy-start | bytes 98308
  138.2 55.4 %all-to-all-start.1 = ((bf16[16,64,512]{2,1,0:T(8,128)(2,1)}), bf16[16,64,512]{2,1,0:T(8,128)(2,1)S(1)}, u32[]{:S(2)}, u32[]{:S(2)}) async-start(bf16[16,64,512]{2,1,0:T(8,128)(2,1)} %copy.199), calls=%async_computation.1 | async-start | bytes 2097152 | tf_op jit(solution)/shard_map/all_to_all | solution.py:181

commit v7 on v6

--- a/solution.py
+++ b/solution.py
@@ -64,28 +64,36 @@
     bc_width = inner_bc.shape[1] // tensor_count
     length = tensor_count * token_rows
 
+    x_send = jnp.transpose(inner_x.reshape(token_rows, tensor_count, x_width), (1, 0, 2))
+    x_recv = lax.all_to_all(x_send, TENSOR, 0, 0, tiled=True)
+    head_x = x_recv.reshape(length, x_width)
+
     quarters = inner_bc.reshape(token_rows, GROUPS, 2, group_size // 2, bc_width)
     across_quarters = jnp.flip(quarters, axis=2)
     bc_send = jnp.stack([quarters, across_quarters], axis=4).reshape(
-        token_rows, tensor_count, 2, bc_width
-    )
-    bc_send = jnp.transpose(bc_send, (1, 0, 2, 3))
-    x_send = jnp.transpose(inner_x.reshape(token_rows, tensor_count, x_width), (1, 0, 2))
+        token_rows, tensor_count, 2 * bc_width
+    )
+    bc_send = jnp.transpose(bc_send, (1, 0, 2))
     step_send = jnp.transpose(step_raw.reshape(token_rows, tensor_count, heads_here), (1, 0, 2))
-    send = jnp.concatenate(
-        [
-            x_send.reshape(tensor_count, -1),
-            bc_send.reshape(tensor_count, -1),
-            step_send.reshape(tensor_count, -1),
-        ],
-        axis=1,
-    )
-    recv = lax.all_to_all(send, TENSOR, 0, 0, tiled=True)
-    x_end = token_rows * x_width
-    bc_end = x_end + token_rows * 2 * bc_width
-    head_x = recv[:, :x_end].reshape(length, x_width)
-    head_bc_pair = recv[:, x_end:bc_end].reshape(length, 2 * bc_width)
-    head_step = recv[:, bc_end:].reshape(length, heads_here)
+    small_send = jnp.concatenate(
+        [bc_send.reshape(tensor_count, -1), step_send.reshape(tensor_count, -1)], axis=1
+    )
+    slots = [lax.dynamic_index_in_dim(small_send, device_rank, 0, keepdims=False)]
+    for shift in range(1, tensor_count):
+        target = (device_rank + shift) % tensor_count
+        slots.append(
+            lax.ppermute(
+                lax.dynamic_index_in_dim(small_send, target, 0, keepdims=False),
+                TENSOR,
+                [(source, (source + shift) % tensor_count) for source in range(tensor_count)],
+            )
+        )
+    arrived = jnp.stack(slots)
+    by_source = (device_rank - jnp.arange(tensor_count, dtype=jnp.int32)) % tensor_count
+    small_recv = jnp.take(arrived, by_source, axis=0)
+    bc_end = token_rows * 2 * bc_width
+    head_bc_pair = small_recv[:, :bc_end].reshape(length, 2 * bc_width)
+    head_step = small_recv[:, bc_end:].reshape(length, heads_here)
 
     group_rank = lax.axis_index("tj")
     column_start = device_rank * bc_width

time: 198 us -> 218 us (1.10)
  the two profiles are of different devices: /device:TPU:65 before, /device:TPU:91 now
where the time goes in v7:
time: 218 us; the launch traced here: 217 us
  starting transfers between devices  89.2 us (41%)
  waiting for transfers between devices  57.4 us (26%)
  other arithmetic  28.7 us (13%)
  local copies, waits for them, and re-layouts  28.3 us (13%)
  matrix products  11.8 us (5%)
    ppermute x15, starting transfers between devices, local(): lax.ppermute(lax.dynamic_index_in_dim(small_send, target, 0, keepdims=Fal...  64.8 us
    all_to_all x1, waiting for transfers between devices, local(): lax.all_to_all(mixed_y, TENSOR, split_axis=0, concat_axis=1, tiled=True)  42.6 us
    ppermute x15, waiting for transfers between devices, local(): lax.ppermute(lax.dynamic_index_in_dim(small_send, target, 0, keepdims=Fal...  14.8 us
    all_to_all x1, starting transfers between devices, local(): x_recv = lax.all_to_all(x_send, TENSOR, 0, 0, tiled=True)  12.6 us
    all_to_all x1, starting transfers between devices, local(): lax.all_to_all(mixed_y, TENSOR, split_axis=0, concat_axis=1, tiled=True)  9.89 us
    convert_element_type x4, other arithmetic, local(): weights = jnp.where(causal[None], scores[None] * decayed * step_cols[:, N...  9.67 us
    dot_general x4, matrix products, local(): jnp.einsum('hts,hps->htp', weights, values_t[:, :, :row_stop], preferred_...  5.99 us
    all_to_all x2, local copies, waits for them, and re-layouts, local(): lax.all_to_all(mixed_y, TENSOR, split_axis=0, concat_axis=1, tiled=True)  5.69 us
  transfers between devices with their start and end apart: 18, of which 3 were waited for; matrix products, arithmetic and copies ran while one was open for 20% of the time, Pallas kernels for 0%

profile of v7, /device:TPU:91, one launch (start us, length us, event | category | flops | bytes accessed | tf_op | source)
XLA Modules:
  0.0 217.3 jit_solution(6924003959270524544)
XLA Ops:
  0.6 2.4 %copy.151 = bf16[8,16,8,512]{3,2,0,1:T(8,128)(2,1)} copy(bf16[8,16,8,512]{3,2,1,0:T(8,128)(2,1)} %bitcast.120) | data formatting | bytes 2097152 | tf_op jit(solution)/shard_map/reshape | solution.py:67
  3.0 12.6 %all-to-all-start = ((bf16[16,64,512]{2,1,0:T(8,128)(2,1)}), bf16[16,64,512]{2,1,0:T(8,128)(2,1)S(1)}, u32[]{:S(2)}, u32[]{:S(2)}) async-start(bf16[16,64,512]{2,1,0:T(8,128)(2,1)} %bitcast.98), calls=%async_computation | async-start | bytes 2097152 | tf_op jit(solution)/shard_map/all_to_all | solution.py:68
  16.6 0.7 pad_maximum_fusion.3
  18.6 0.8 fusion.74
  19.4 3.4 %collective-permute-start = (bf16[16896]{0:T(1024)(128)(2,1)S(1)}, bf16[16896]{0:T(1024)(128)(2,1)S(1)}, u32[]{:S(2)}, u32[]{:S(2)}) collective-permute-start(bf16[16896]{0:T(1024)(128)(2,1)S(1)} %get-tuple-element.5), channel_id=1, source_target_pairs={{0,1},{1,2},{2,3},{3,4},{4,5},{5,6},{6,7},{7,8},{8,9},{9,10},{10,1... | collective-permute-start | bytes 101384 | tf_op jit(solution)/shard_map/ppermute | solution.py:85
  22.8 4.3 %collective-permute-start.1 = (bf16[16896]{0:T(1024)(128)(2,1)S(1)}, bf16[16896]{0:T(1024)(128)(2,1)S(1)}, u32[]{:S(2)}, u32[]{:S(2)}) collective-permute-start(bf16[16896]{0:T(1024)(128)(2,1)S(1)} %get-tuple-element.6), channel_id=1, source_target_pairs={{0,2},{1,3},{2,4},{3,5},{4,6},{5,7},{6,8},{7,9},{8,10},{9,11},{10,... | collective-permute-start | bytes 101384 | tf_op jit(solution)/shard_map/ppermute | solution.py:85
  27.1 3.2 %collective-permute-start.2 = (bf16[16896]{0:T(1024)(128)(2,1)S(1)}, bf16[16896]{0:T(1024)(128)(2,1)S(1)}, u32[]{:S(2)}, u32[]{:S(2)}) collective-permute-start(bf16[16896]{0:T(1024)(128)(2,1)S(1)} %get-tuple-element.7), channel_id=1, source_target_pairs={{0,3},{1,4},{2,5},{3,6},{4,7},{5,8},{6,9},{7,10},{8,11},{9,12},{10... | collective-permute-start | bytes 101384 | tf_op jit(solution)/shard_map/ppermute | solution.py:85
  30.3 0.8 fusion.60
  31.1 4.0 %collective-permute-start.3 = (bf16[16896]{0:T(1024)(128)(2,1)S(1)}, bf16[16896]{0:T(1024)(128)(2,1)S(1)}, u32[]{:S(2)}, u32[]{:S(2)}) collective-permute-start(bf16[16896]{0:T(1024)(128)(2,1)S(1)} %get-tuple-element.9), channel_id=1, source_target_pairs={{0,4},{1,5},{2,6},{3,7},{4,8},{5,9},{6,10},{7,11},{8,12},{9,13},{1... | collective-permute-start | bytes 101384 | tf_op jit(solution)/shard_map/ppermute | solution.py:85
  35.1 4.4 %collective-permute-start.4 = (bf16[16896]{0:T(1024)(128)(2,1)S(1)}, bf16[16896]{0:T(1024)(128)(2,1)S(1)}, u32[]{:S(2)}, u32[]{:S(2)}) collective-permute-start(bf16[16896]{0:T(1024)(128)(2,1)S(1)} %get-tuple-element.10), channel_id=1, source_target_pairs={{0,5},{1,6},{2,7},{3,8},{4,9},{5,10},{6,11},{7,12},{8,13},{9,14},{... | collective-permute-start | bytes 101384 | tf_op jit(solution)/shard_map/ppermute | solution.py:85
  39.7 0.6 gather_fusion
  40.9 0.6 iota_compare_fusion.3
  41.6 0.6 slice_convert_fusion.5
  42.2 0.7 constant_dynamic-slice_fusion.1
  42.9 0.7 constant_dynamic-slice_fusion.3
  43.6 0.8 fusion.91
  44.4 0.6 pad_clamp_fusion
  45.2 0.8 iota_compare_fusion.1
  46.1 0.8 iota_compare_fusion.2
  46.9 0.7 fusion.62
  47.6 0.8 fusion.61
  48.4 13.1 %collective-permute-done = bf16[16896]{0:T(1024)(128)(2,1)S(1)} collective-permute-done((bf16[16896]{0:T(1024)(128)(2,1)S(1)}, bf16[16896]{0:T(1024)(128)(2,1)S(1)}, u32[]{:S(2)}, u32[]{:S(2)}) %collective-permute-start) | collective-permute-done | bytes 33824 | tf_op jit(solution)/shard_map/ppermute | solution.py:85
  61.5 1.9 collective-permute-start.5
  63.4 1.9 collective-permute-start.6
  65.4 6.7 %collective-permute-start.7 = (bf16[16896]{0:T(1024)(128)(2,1)S(1)}, bf16[16896]{0:T(1024)(128)(2,1)S(1)}, u32[]{:S(2)}, u32[]{:S(2)}) collective-permute-start(bf16[16896]{0:T(1024)(128)(2,1)S(1)} %get-tuple-element.14), channel_id=1, source_target_pairs={{0,8},{1,9},{2,10},{3,11},{4,12},{5,13},{6,14},{7,15},{8,0},{9,1},... | collective-permute-start | bytes 101384 | tf_op jit(solution)/shard_map/ppermute | solution.py:85
  72.1 7.3 %collective-permute-start.8 = (bf16[16896]{0:T(1024)(128)(2,1)S(1)}, bf16[16896]{0:T(1024)(128)(2,1)S(1)}, u32[]{:S(2)}, u32[]{:S(2)}) collective-permute-start(bf16[16896]{0:T(1024)(128)(2,1)S(1)} %get-tuple-element.15), channel_id=1, source_target_pairs={{0,9},{1,10},{2,11},{3,12},{4,13},{5,14},{6,15},{7,0},{8,1},{9,2},... | collective-permute-start | bytes 101384 | tf_op jit(solution)/shard_map/ppermute | solution.py:85
  79.4 5.7 %collective-permute-start.9 = (bf16[16896]{0:T(1024)(128)(2,1)S(1)}, bf16[16896]{0:T(1024)(128)(2,1)S(1)}, u32[]{:S(2)}, u32[]{:S(2)}) collective-permute-start(bf16[16896]{0:T(1024)(128)(2,1)S(1)} %get-tuple-element.17), channel_id=1, source_target_pairs={{0,10},{1,11},{2,12},{3,13},{4,14},{5,15},{6,0},{7,1},{8,2},{9,3},... | collective-permute-start | bytes 101384 | tf_op jit(solution)/shard_map/ppermute | solution.py:85
  85.1 11.4 %collective-permute-start.10 = (bf16[16896]{0:T(1024)(128)(2,1)S(1)}, bf16[16896]{0:T(1024)(128)(2,1)S(1)}, u32[]{:S(2)}, u32[]{:S(2)}) collective-permute-start(bf16[16896]{0:T(1024)(128)(2,1)S(1)} %get-tuple-element.18), channel_id=1, source_target_pairs={{0,11},{1,12},{2,13},{3,14},{4,15},{5,0},{6,1},{7,2},{8,3},{9,4},{... | collective-permute-start | bytes 101384 | tf_op jit(solution)/shard_map/ppermute | solution.py:85
  96.5 1.9 collective-permute-start.11
  98.4 3.1 %collective-permute-start.12 = (bf16[16896]{0:T(1024)(128)(2,1)S(1)}, bf16[16896]{0:T(1024)(128)(2,1)S(1)}, u32[]{:S(2)}, u32[]{:S(2)}) collective-permute-start(bf16[16896]{0:T(1024)(128)(2,1)S(1)} %get-tuple-element.12), channel_id=1, source_target_pairs={{0,13},{1,14},{2,15},{3,0},{4,1},{5,2},{6,3},{7,4},{8,5},{9,6},{10... | collective-permute-start | bytes 101384 | tf_op jit(solution)/shard_map/ppermute | solution.py:85
  101.6 3.4 %collective-permute-start.13 = (bf16[16896]{0:T(1024)(128)(2,1)S(1)}, bf16[16896]{0:T(1024)(128)(2,1)S(1)}, u32[]{:S(2)}, u32[]{:S(2)}) collective-permute-start(bf16[16896]{0:T(1024)(128)(2,1)S(1)} %get-tuple-element.8), channel_id=1, source_target_pairs={{0,14},{1,15},{2,0},{3,1},{4,2},{5,3},{6,4},{7,5},{8,6},{9,7},{10,... | collective-permute-start | bytes 101384 | tf_op jit(solution)/shard_map/ppermute | solution.py:85
  104.9 2.2 %collective-permute-start.14 = (bf16[16896]{0:T(1024)(128)(2,1)S(1)}, bf16[16896]{0:T(1024)(128)(2,1)S(1)}, u32[]{:S(2)}, u32[]{:S(2)}) collective-permute-start(bf16[16896]{0:T(1024)(128)(2,1)S(1)} %get-tuple-element.4), channel_id=1, source_target_pairs={{0,15},{1,0},{2,1},{3,2},{4,3},{5,4},{6,5},{7,6},{8,7},{9,8},{10,9... | collective-permute-start | bytes 101384 | tf_op jit(solution)/shard_map/ppermute | solution.py:85
  108.6 1.6 collective-permute-done.14
  110.2 1.7 stack.72
  112.0 0.9 gather_fusion.1
  113.7 2.3 %reduce-window.6 = f32[8,8,128]{2,1,0:T(8,128)S(1)} reduce-window(f32[8,8,128]{2,1,0:T(8,128)S(1)} %copy.129, f32[]{:T(128)} %constant.200.clone.1), window={size=1x1x128 pad=0_0x0_0x127_0}, to_apply=%region_0.1 | reduce-window | flops 1040384 | bytes 65540 | tf_op jit(solution)/shard_map/reduce-window
  116.9 1.3 multiply_convert_fusion.6
  118.5 1.9 collective-permute-start.15
  120.6 0.7 exponential_multiply_fusion
  121.4 0.6 slice.208
  122.6 0.6 fusion.90
  123.2 0.6 fusion.88
  123.9 0.9 gather_fusion.2
  124.8 1.0 copy_bitcast_fusion
  126.2 3.7 %select_convert_fusion = bf16[8,256,1024]{2,1,0:T(8,128)(2,1)} fusion(f32[8,1024]{1,0:T(8,128)S(1)} %get-tuple-element.21, f32[8,1024]{1,0:T(8,128)S(1)} %bitcast.125, f32[8,256]{1,0:T(8,128)S(1)} %copy-done.13, f32[256,1024]{1,0:T(8,128)S(1)} %fusion.30, pred[256,1024]{1,0:T(8,128)(4,1)S(1)} %iota_compare_fusion), kind=kLoop, calls=%fused_computation.4 | loop fusion | flops 12582912 | bytes 5578752 | tf_op jit(solution)/shard_map/convert_element_type | solution.py:159
  130.2 3.1 %select_convert_fusion.1 = bf16[8,256,768]{2,1,0:T(8,128)(2,1)} fusion(f32[8,768]{1,0:T(8,128)S(1)} %slice.215, f32[8,768]{1,0:T(8,128)S(1)} %slice.214, f32[8,256]{1,0:T(8,128)S(1)} %copy-done.12, f32[256,768]{1,0:T(8,128)S(1)} %fusion.32, pred[256,768]{1,0:T(8,128)(4,1)S(1)} %copy-done.6), kind=kLoop, calls=%fused_computation.5 | loop fusion | flops 9437184 | bytes 4186112 | tf_op jit(solution)/shard_map/convert_element_type | solution.py:159
  133.6 2.3 %select_convert_fusion.2 = bf16[8,256,512]{2,1,0:T(8,128)(2,1)} fusion(f32[8,512]{1,0:T(8,128)S(1)} %slice.209, f32[8,512]{1,0:T(8,128)S(1)} %copy-done.9, f32[8,256]{1,0:T(8,128)S(1)} %copy-done.11, f32[256,512]{1,0:T(8,128)S(1)} %fusion.34, pred[256,512]{1,0:T(8,128)(4,1)S(1)} %copy-done.7), kind=kLoop, calls=%fused_computation.9 | loop fusion | flops 6291456 | bytes 2793472 | tf_op jit(solution)/shard_map/convert_element_type | solution.py:159
  136.2 0.6 select_convert_fusion.3
  137.2 0.6 copy-done.3
  137.8 2.2 %multiply_convert_fusion.3 = bf16[1024,512]{1,0:T(8,128)(2,1)} fusion(f32[1024,512]{1,0:T(8,128)S(1)} %bitcast_convert_fusion, f32[3,512]{1,0:T(4,128)S(1)} %convert_element_type.105, f32[512]{0:T(512)S(1)} %bitcast.132, f32[512]{0:T(512)S(1)} %bitcast.133, f32[512]{0:T(512)S(1)} %bitcast.131, f32[512]{0:T(512)S(1)} %bitcast.130, f32[512]{0:T(512)S(1)} %copy-done.19), kind=kLoop, calls=%fused_computation.46 | loop fusion | flops 8388608 | bytes 3162112 | tf_op jit(solution)/shard_map/convert_element_type | solution.py:30
  140.0 1.5 copy.131
  141.5 3.7 %fusion.92 = f32[8,256,64]{1,2,0:T(8,128)S(1)} fusion(bf16[8,256,1024]{2,1,0:T(8,128)(2,1)} %select_convert_fusion, bf16[8,64,1024]{2,1,0:T(8,128)(2,1)S(1)} %bitcast.106), kind=kOutput, calls=%fused_computation.190 | convolution fusion | flops 268435456 | bytes 5767168 | tf_op jit(solution)/shard_map/hts,hps->htp/dot_general | solution.py:162
  145.2 1.1 fusion.26
  146.8 0.8 fusion.28
  148.1 1.3 fusion.15
  149.4 2.4 %reshape.321 = bf16[16,64,512]{1,0,2:T(8,128)(2,1)} reshape(bf16[1024,8,64]{0,2,1:T(8,128)(2,1)S(1)} %fusion.15) | data formatting | bytes 2097152 | tf_op jit(solution)/shard_map/all_to_all | solution.py:189
  151.8 3.3 %copy.135 = bf16[16,64,512]{2,1,0:T(8,128)(2,1)} copy(bf16[16,64,512]{1,0,2:T(8,128)(2,1)} %reshape.321) | data formatting | bytes 2097152 | tf_op jit(solution)/shard_map/all_to_all | solution.py:189
  155.1 9.9 %all-to-all-start.1 = ((bf16[16,64,512]{2,1,0:T(8,128)(2,1)}), bf16[16,64,512]{2,1,0:T(8,128)(2,1)S(1)}, u32[]{:S(2)}, u32[]{:S(2)}) async-start(bf16[16,64,512]{2,1,0:T(8,128)(2,1)} %copy.135), calls=%async_computation.1 | async-start | bytes 2097152 | tf_op jit(solution)/shard_map/all_to_all | solution.py:189
  165.0 1.3 slice.223
  166.3 1.3 slice.222
  167.6 3.3 %fusion.16 = f32[8,64,256]{2,1,0:T(8,128)} fusion(bf16[8,64,1024]{2,1,0:T(8,128)(2,1)S(1)} %bitcast.111, f32[1024,8]{0,1:T(8,128)S(1)} %copy-done.15, f32[1024,256]{1,0:T(8,128)S(1)} %slice_convert_fusion, f32[8,64,256]{2,1,0:T(8,128)} %param.28, f32[8]{0:T(128)S(1)} %exp.49), kind=kOutput, calls=%fused_computation.51 | convolution fusion | flops 272891904 | bytes 3178528 | tf_op jit(solution)/shard_map/hps,shn->hpn/dot_general | solution.py:184
  171.0 42.6 %all-to-all-done.1 = bf16[16,64,512]{2,1,0:T(8,128)(2,1)S(1)} async-done(((bf16[16,64,512]{2,1,0:T(8,128)(2,1)}), bf16[16,64,512]{2,1,0:T(8,128)(2,1)S(1)}, u32[]{:S(2)}, u32[]{:S(2)}) %all-to-all-start.1) | async-done | bytes 1048608 | tf_op jit(solution)/shard_map/all_to_all | solution.py:189
  214.8 1.2 copy.141
  216.0 1.3 multiply_convert_fusion.2
  (156 shorter events, 10.8 us)
Async XLA Ops:
  0.6 15.0 %copy-start.5 = (bf16[64,2048]{1,0:T(8,128)(2,1)S(1)}, bf16[64,2048]{1,0:T(8,128)(2,1)}, u32[]{:S(2)}) copy-start(bf16[64,2048]{1,0:T(8,128)(2,1)} %param.16) | copy-start | bytes 786436
  3.0 13.0 %copy-start.16 = (bf16[64,128]{1,0:T(8,128)(2,1)S(1)}, bf16[64,128]{1,0:T(8,128)(2,1)}, u32[]{:S(2)}) copy-start(bf16[64,128]{1,0:T(8,128)(2,1)} %param.17) | copy-start | bytes 49156
  3.0 133.8 %all-to-all-start = ((bf16[16,64,512]{2,1,0:T(8,128)(2,1)}), bf16[16,64,512]{2,1,0:T(8,128)(2,1)S(1)}, u32[]{:S(2)}, u32[]{:S(2)}) async-start(bf16[16,64,512]{2,1,0:T(8,128)(2,1)} %bitcast.98), calls=%async_computation | async-start | bytes 2097152 | tf_op jit(solution)/shard_map/all_to_all | solution.py:68
  17.9 21.9 %copy-start = (s32[4]{0:T(128)S(1)}, s32[4]{0:T(128)}, u32[]{:S(2)}) copy-start(s32[4]{0:T(128)} %constant.206.clone) | copy-start | bytes 52
  17.9 23.7 %copy-start.18 = (bf16[4,512]{1,0:T(4,128)(2,1)S(1)}, bf16[4,512]{1,0:T(4,128)(2,1)}, u32[]{:S(2)}) copy-start(bf16[4,512]{1,0:T(4,128)(2,1)} %param.20) | copy-start | bytes 12292
  18.6 88.6 %copy-start.24 = (bf16[3,512]{1,0:T(4,128)(2,1)S(1)}, bf16[3,512]{1,0:T(4,128)(2,1)}, u32[]{:S(2)}) copy-start(bf16[3,512]{1,0:T(4,128)(2,1)} %param.18) | copy-start | bytes 9220
  18.6 88.6 %copy-start.28 = (bf16[512]{0:T(512)(128)(2,1)S(1)}, bf16[512]{0:T(512)(128)(2,1)}, u32[]{:S(2)}) copy-start(bf16[512]{0:T(512)(128)(2,1)} %param.21) | copy-start | bytes 3076
  19.4 42.1 %collective-permute-start = (bf16[16896]{0:T(1024)(128)(2,1)S(1)}, bf16[16896]{0:T(1024)(128)(2,1)S(1)}, u32[]{:S(2)}, u32[]{:S(2)}) collective-permute-start(bf16[16896]{0:T(1024)(128)(2,1)S(1)} %get-tuple-element.5), channel_id=1, source_target_pairs={{0,1},{1,2},{2,3},{3,4},{4,5},{5,6},{6,7},{7,8},{8,9},{9,10},{10,1... | collective-permute-start | bytes 101384 | tf_op jit(solution)/shard_map/ppermute | solution.py:85
  22.8 40.7 %collective-permute-start.1 = (bf16[16896]{0:T(1024)(128)(2,1)S(1)}, bf16[16896]{0:T(1024)(128)(2,1)S(1)}, u32[]{:S(2)}, u32[]{:S(2)}) collective-permute-start(bf16[16896]{0:T(1024)(128)(2,1)S(1)} %get-tuple-element.6), channel_id=1, source_target_pairs={{0,2},{1,3},{2,4},{3,5},{4,6},{5,7},{6,8},{7,9},{8,10},{9,11},{10,... | collective-permute-start | bytes 101384 | tf_op jit(solution)/shard_map/ppermute | solution.py:85
  27.1 38.3 %collective-permute-start.2 = (bf16[16896]{0:T(1024)(128)(2,1)S(1)}, bf16[16896]{0:T(1024)(128)(2,1)S(1)}, u32[]{:S(2)}, u32[]{:S(2)}) collective-permute-start(bf16[16896]{0:T(1024)(128)(2,1)S(1)} %get-tuple-element.7), channel_id=1, source_target_pairs={{0,3},{1,4},{2,5},{3,6},{4,7},{5,8},{6,9},{7,10},{8,11},{9,12},{10... | collective-permute-start | bytes 101384 | tf_op jit(solution)/shard_map/ppermute | solution.py:85
  31.1 41.0 %collective-permute-start.3 = (bf16[16896]{0:T(1024)(128)(2,1)S(1)}, bf16[16896]{0:T(1024)(128)(2,1)S(1)}, u32[]{:S(2)}, u32[]{:S(2)}) collective-permute-start(bf16[16896]{0:T(1024)(128)(2,1)S(1)} %get-tuple-element.9), channel_id=1, source_target_pairs={{0,4},{1,5},{2,6},{3,7},{4,8},{5,9},{6,10},{7,11},{8,12},{9,13},{1... | collective-permute-start | bytes 101384 | tf_op jit(solution)/shard_map/ppermute | solution.py:85
  35.1 44.2 %collective-permute-start.4 = (bf16[16896]{0:T(1024)(128)(2,1)S(1)}, bf16[16896]{0:T(1024)(128)(2,1)S(1)}, u32[]{:S(2)}, u32[]{:S(2)}) collective-permute-start(bf16[16896]{0:T(1024)(128)(2,1)S(1)} %get-tuple-element.10), channel_id=1, source_target_pairs={{0,5},{1,6},{2,7},{3,8},{4,9},{5,10},{6,11},{7,12},{8,13},{9,14},{... | collective-permute-start | bytes 101384 | tf_op jit(solution)/shard_map/ppermute | solution.py:85
  61.5 23.6 %collective-permute-start.5 = (bf16[16896]{0:T(1024)(128)(2,1)S(1)}, bf16[16896]{0:T(1024)(128)(2,1)S(1)}, u32[]{:S(2)}, u32[]{:S(2)}) collective-permute-start(bf16[16896]{0:T(1024)(128)(2,1)S(1)} %get-tuple-element.11), channel_id=1, source_target_pairs={{0,6},{1,7},{2,8},{3,9},{4,10},{5,11},{6,12},{7,13},{8,14},{9,15},... | collective-permute-start | bytes 101384 | tf_op jit(solution)/shard_map/ppermute | solution.py:85
  63.4 33.1 %collective-permute-start.6 = (bf16[16896]{0:T(1024)(128)(2,1)S(1)}, bf16[16896]{0:T(1024)(128)(2,1)S(1)}, u32[]{:S(2)}, u32[]{:S(2)}) collective-permute-start(bf16[16896]{0:T(1024)(128)(2,1)S(1)} %get-tuple-element.13), channel_id=1, source_target_pairs={{0,7},{1,8},{2,9},{3,10},{4,11},{5,12},{6,13},{7,14},{8,15},{9,0},... | collective-permute-start | bytes 101384 | tf_op jit(solution)/shard_map/ppermute | solution.py:85
  65.4 33.1 %collective-permute-start.7 = (bf16[16896]{0:T(1024)(128)(2,1)S(1)}, bf16[16896]{0:T(1024)(128)(2,1)S(1)}, u32[]{:S(2)}, u32[]{:S(2)}) collective-permute-start(bf16[16896]{0:T(1024)(128)(2,1)S(1)} %get-tuple-element.14), channel_id=1, source_target_pairs={{0,8},{1,9},{2,10},{3,11},{4,12},{5,13},{6,14},{7,15},{8,0},{9,1},... | collective-permute-start | bytes 101384 | tf_op jit(solution)/shard_map/ppermute | solution.py:85
  72.1 29.4 %collective-permute-start.8 = (bf16[16896]{0:T(1024)(128)(2,1)S(1)}, bf16[16896]{0:T(1024)(128)(2,1)S(1)}, u32[]{:S(2)}, u32[]{:S(2)}) collective-permute-start(bf16[16896]{0:T(1024)(128)(2,1)S(1)} %get-tuple-element.15), channel_id=1, source_target_pairs={{0,9},{1,10},{2,11},{3,12},{4,13},{5,14},{6,15},{7,0},{8,1},{9,2},... | collective-permute-start | bytes 101384 | tf_op jit(solution)/shard_map/ppermute | solution.py:85
  79.4 25.6 %collective-permute-start.9 = (bf16[16896]{0:T(1024)(128)(2,1)S(1)}, bf16[16896]{0:T(1024)(128)(2,1)S(1)}, u32[]{:S(2)}, u32[]{:S(2)}) collective-permute-start(bf16[16896]{0:T(1024)(128)(2,1)S(1)} %get-tuple-element.17), channel_id=1, source_target_pairs={{0,10},{1,11},{2,12},{3,13},{4,14},{5,15},{6,0},{7,1},{8,2},{9,3},... | collective-permute-start | bytes 101384 | tf_op jit(solution)/shard_map/ppermute | solution.py:85
  85.1 23.3 %collective-permute-start.10 = (bf16[16896]{0:T(1024)(128)(2,1)S(1)}, bf16[16896]{0:T(1024)(128)(2,1)S(1)}, u32[]{:S(2)}, u32[]{:S(2)}) collective-permute-start(bf16[16896]{0:T(1024)(128)(2,1)S(1)} %get-tuple-element.18), channel_id=1, source_target_pairs={{0,11},{1,12},{2,13},{3,14},{4,15},{5,0},{6,1},{7,2},{8,3},{9,4},{... | collective-permute-start | bytes 101384 | tf_op jit(solution)/shard_map/ppermute | solution.py:85
  96.5 11.9 %collective-permute-start.11 = (bf16[16896]{0:T(1024)(128)(2,1)S(1)}, bf16[16896]{0:T(1024)(128)(2,1)S(1)}, u32[]{:S(2)}, u32[]{:S(2)}) collective-permute-start(bf16[16896]{0:T(1024)(128)(2,1)S(1)} %get-tuple-element.16), channel_id=1, source_target_pairs={{0,12},{1,13},{2,14},{3,15},{4,0},{5,1},{6,2},{7,3},{8,4},{9,5},{1... | collective-permute-start | bytes 101384 | tf_op jit(solution)/shard_map/ppermute | solution.py:85
  98.4 10.0 %collective-permute-start.12 = (bf16[16896]{0:T(1024)(128)(2,1)S(1)}, bf16[16896]{0:T(1024)(128)(2,1)S(1)}, u32[]{:S(2)}, u32[]{:S(2)}) collective-permute-start(bf16[16896]{0:T(1024)(128)(2,1)S(1)} %get-tuple-element.12), channel_id=1, source_target_pairs={{0,13},{1,14},{2,15},{3,0},{4,1},{5,2},{6,3},{7,4},{8,5},{9,6},{10... | collective-permute-start | bytes 101384 | tf_op jit(solution)/shard_map/ppermute | solution.py:85
  101.6 7.0 %collective-permute-start.13 = (bf16[16896]{0:T(1024)(128)(2,1)S(1)}, bf16[16896]{0:T(1024)(128)(2,1)S(1)}, u32[]{:S(2)}, u32[]{:S(2)}) collective-permute-start(bf16[16896]{0:T(1024)(128)(2,1)S(1)} %get-tuple-element.8), channel_id=1, source_target_pairs={{0,14},{1,15},{2,0},{3,1},{4,2},{5,3},{6,4},{7,5},{8,6},{9,7},{10,... | collective-permute-start | bytes 101384 | tf_op jit(solution)/shard_map/ppermute | solution.py:85
  104.9 5.3 %collective-permute-start.14 = (bf16[16896]{0:T(1024)(128)(2,1)S(1)}, bf16[16896]{0:T(1024)(128)(2,1)S(1)}, u32[]{:S(2)}, u32[]{:S(2)}) collective-permute-start(bf16[16896]{0:T(1024)(128)(2,1)S(1)} %get-tuple-element.4), channel_id=1, source_target_pairs={{0,15},{1,0},{2,1},{3,2},{4,3},{5,4},{6,5},{7,6},{8,7},{9,8},{10,9... | collective-permute-start | bytes 101384 | tf_op jit(solution)/shard_map/ppermute | solution.py:85
  112.9 0.7 copy-start.25
  112.9 0.7 copy-start.29
  116.5 1.6 copy-start.4
  118.5 5.3 %collective-permute-start.15 = (bf16[2,1024,128]{2,1,0:T(8,128)(2,1)S(1)}, bf16[2,1024,128]{2,1,0:T(8,128)(2,1)S(1)}, u32[]{:S(2)}, u32[]{:S(2)}) collective-permute-start(bf16[2,1024,128]{2,1,0:T(8,128)(2,1)S(1)} %bitcast.118), channel_id=1, source_target_pairs={{0,1},{1,0},{2,3},{3,2},{4,5},{5,4},{6,7},{7,6},{8,9},{9,8},{10,11... | collective-permute-start | bytes 1572872 | tf_op jit(solution)/shard_map/ppermute | solution.py:124
  120.6 0.7 copy-start.26
  124.8 1.4 copy-start.13
  126.2 4.0 %copy-start.6 = (pred[256,768]{1,0:T(8,128)(4,1)S(1)}, pred[256,768]{1,0:T(8,128)(4,1)}, u32[]{:S(2)}) copy-start(pred[256,768]{1,0:T(8,128)(4,1)} %iota_compare_fusion.1) | copy-start | bytes 589828
  126.2 4.0 %copy-start.12 = (f32[8,256]{1,0:T(8,128)S(1)}, f32[8,256]{1,0:T(8,128)}, u32[]{:S(2)}) copy-start(f32[8,256]{1,0:T(8,128)} %get-tuple-element.26) | copy-start | bytes 24580
  130.2 3.4 %copy-start.7 = (pred[256,512]{1,0:T(8,128)(4,1)S(1)}, pred[256,512]{1,0:T(8,128)(4,1)}, u32[]{:S(2)}) copy-start(pred[256,512]{1,0:T(8,128)(4,1)} %iota_compare_fusion.2) | copy-start | bytes 393220
  130.2 3.4 %copy-start.9 = (f32[8,512]{1,0:T(8,128)S(1)}, f32[8,512]{1,0:T(8,128)}, u32[]{:S(2)}) copy-start(f32[8,512]{1,0:T(8,128)} %slice.208) | copy-start | bytes 49156
  130.2 3.4 %copy-start.11 = (f32[8,256]{1,0:T(8,128)S(1)}, f32[8,256]{1,0:T(8,128)}, u32[]{:S(2)}) copy-start(f32[8,256]{1,0:T(8,128)} %get-tuple-element.27) | copy-start | bytes 24580
  133.3 2.8 %copy-start.8 = (pred[256,256]{1,0:T(8,128)(4,1)S(1)}, pred[256,256]{1,0:T(8,128)(4,1)}, u32[]{:S(2)}) copy-start(pred[256,256]{1,0:T(8,128)(4,1)} %iota_compare_fusion.3) | copy-start | bytes 196612
  133.3 2.8 %copy-start.10 = (f32[8,256]{1,0:T(8,128)S(1)}, f32[8,256]{1,0:T(8,128)}, u32[]{:S(2)}) copy-start(f32[8,256]{1,0:T(8,128)} %slice.199) | copy-start | bytes 24580
  136.1 1.7 copy-start.19
  136.2 1.6 copy-start.20
  136.2 1.6 copy-start.21
  136.2 1.6 copy-start.22
  136.2 1.6 copy-start.23
  136.8 1.0 copy-start.3
  141.5 3.7 %copy-start.1 = (bf16[8,256,768]{2,1,0:T(8,128)(2,1)S(1)}, bf16[8,256,768]{2,1,0:T(8,128)(2,1)}, u32[]{:S(2)}) copy-start(bf16[8,256,768]{2,1,0:T(8,128)(2,1)} %select_convert_fusion.1) | copy-start | bytes 9437188
  145.2 1.6 copy-start.2
  146.8 1.2 copy-start.14
  146.8 1.2 copy-start.30
  146.8 1.2 copy-start.31
  151.8 13.2 %copy-start.17 = (bf16[8192]{0:T(1024)(128)(2,1)S(1)}, bf16[8192]{0:T(1024)(128)(2,1)}, u32[]{:S(2)}) copy-start(bf16[8192]{0:T(1024)(128)(2,1)} %param.27) | copy-start | bytes 49156
  151.8 13.2 %copy-start.27 = (f32[8]{0:T(128)S(1)}, f32[8]{0:T(128)}, u32[]{:S(2)}) copy-start(f32[8]{0:T(128)} %copy-done.26) | copy-start | bytes 100
  155.1 12.6 %copy-start.15 = (f32[1024,8]{0,1:T(8,128)S(1)}, f32[1024,8]{0,1:T(8,128)}, u32[]{:S(2)}) copy-start(f32[1024,8]{0,1:T(8,128)} %get-tuple-element.20) | copy-start | bytes 98308
  155.1 58.5 %all-to-all-start.1 = ((bf16[16,64,512]{2,1,0:T(8,128)(2,1)}), bf16[16,64,512]{2,1,0:T(8,128)(2,1)S(1)}, u32[]{:S(2)}, u32[]{:S(2)}) async-start(bf16[16,64,512]{2,1,0:T(8,128)(2,1)} %copy.135), calls=%async_computation.1 | async-start | bytes 2097152 | tf_op jit(solution)/shard_map/all_to_all | solution.py:189

commit v8 on v7

--- a/solution.py
+++ b/solution.py
@@ -64,10 +64,6 @@
     bc_width = inner_bc.shape[1] // tensor_count
     length = tensor_count * token_rows
 
-    x_send = jnp.transpose(inner_x.reshape(token_rows, tensor_count, x_width), (1, 0, 2))
-    x_recv = lax.all_to_all(x_send, TENSOR, 0, 0, tiled=True)
-    head_x = x_recv.reshape(length, x_width)
-
     quarters = inner_bc.reshape(token_rows, GROUPS, 2, group_size // 2, bc_width)
     across_quarters = jnp.flip(quarters, axis=2)
     bc_send = jnp.stack([quarters, across_quarters], axis=4).reshape(
@@ -78,22 +74,14 @@
     small_send = jnp.concatenate(
         [bc_send.reshape(tensor_count, -1), step_send.reshape(tensor_count, -1)], axis=1
     )
-    slots = [lax.dynamic_index_in_dim(small_send, device_rank, 0, keepdims=False)]
-    for shift in range(1, tensor_count):
-        target = (device_rank + shift) % tensor_count
-        slots.append(
-            lax.ppermute(
-                lax.dynamic_index_in_dim(small_send, target, 0, keepdims=False),
-                TENSOR,
-                [(source, (source + shift) % tensor_count) for source in range(tensor_count)],
-            )
-        )
-    arrived = jnp.stack(slots)
-    by_source = (device_rank - jnp.arange(tensor_count, dtype=jnp.int32)) % tensor_count
-    small_recv = jnp.take(arrived, by_source, axis=0)
+    small_recv = lax.all_to_all(small_send, TENSOR, 0, 0, tiled=True)
     bc_end = token_rows * 2 * bc_width
     head_bc_pair = small_recv[:, :bc_end].reshape(length, 2 * bc_width)
     head_step = small_recv[:, bc_end:].reshape(length, heads_here)
+
+    x_send = jnp.transpose(inner_x.reshape(token_rows, tensor_count, x_width), (1, 0, 2))
+    x_recv = lax.all_to_all(x_send, TENSOR, 0, 0, tiled=True)
+    head_x = x_recv.reshape(length, x_width)
 
     group_rank = lax.axis_index("tj")
     column_start = device_rank * bc_width

time: 218 us -> 182 us (0.83)
  the two profiles are of different devices: /device:TPU:91 before, /device:TPU:65 now
where the time goes in v8:
time: 182 us; the launch traced here: 181 us
  waiting for transfers between devices  84.2 us (46%)
  local copies, waits for them, and re-layouts  30.2 us (17%)
  starting transfers between devices  28.6 us (16%)
  other arithmetic  25.3 us (14%)
  matrix products  11.7 us (6%)
    all_to_all x1, waiting for transfers between devices, local(): lax.all_to_all(mixed_y, TENSOR, split_axis=0, concat_axis=1, tiled=True)  42.6 us
    all_to_all x1, waiting for transfers between devices, local(): x_recv = lax.all_to_all(x_send, TENSOR, 0, 0, tiled=True)  22.6 us
    all_to_all x1, waiting for transfers between devices, local(): small_recv = lax.all_to_all(small_send, TENSOR, 0, 0, tiled=True)  19 us
    all_to_all x1, starting transfers between devices, local(): small_recv = lax.all_to_all(small_send, TENSOR, 0, 0, tiled=True)  12.6 us
    convert_element_type x4, other arithmetic, local(): weights = jnp.where(causal[None], scores[None] * decayed * step_cols[:, N...  9.55 us
    all_to_all x1, starting transfers between devices, local(): lax.all_to_all(mixed_y, TENSOR, split_axis=0, concat_axis=1, tiled=True)  6.84 us
    all_to_all x1, starting transfers between devices, local(): x_recv = lax.all_to_all(x_send, TENSOR, 0, 0, tiled=True)  6.7 us
    dot_general x4, matrix products, local(): jnp.einsum('hts,hps->htp', weights, values_t[:, :, :row_stop], preferred_...  5.99 us
  transfers between devices with their start and end apart: 4, of which 3 were waited for; matrix products, arithmetic and copies ran while one was open for 21% of the time, Pallas kernels for 0%

profile of v8, /device:TPU:65, one launch (start us, length us, event | category | flops | bytes accessed | tf_op | source)
XLA Modules:
  0.0 181.3 jit_solution(12312664221112355702)
XLA Ops:
  0.6 1.1 reshape.221
  1.7 1.1 stack_reshape.3
  2.9 0.8 copy.179
  4.1 0.7 pad_maximum_fusion.3
  4.9 0.8 copy.177
  5.7 0.3 reshape.222
  6.1 0.5 broadcast.162
  6.7 1.0 reduce.7
  7.7 0.9 reshape.264
  8.7 12.6 %all-to-all-start = ((bf16[16,2,8448]{2,1,0:T(2,128)(2,1)}), bf16[16,2,8448]{2,1,0:T(2,128)(2,1)S(1)}, u32[]{:S(2)}, u32[]{:S(2)}) async-start(bf16[16,2,8448]{2,1,0:T(2,128)(2,1)} %reshape.264), calls=%async_computation | async-start | bytes 1081344 | tf_op jit(solution)/shard_map/all_to_all | solution.py:77
  21.3 1.1 copy.212
  22.4 0.6 convert_element_type.104
  23.0 0.7 constant_dynamic-slice_fusion.1
  23.7 0.8 fusion.57
  24.6 0.6 gather_fusion
  25.2 0.7 constant_dynamic-slice_fusion.3
  25.9 0.6 pad_clamp_fusion
  26.6 0.5 compare_and_fusion
  27.1 0.6 slice_convert_fusion.5
  27.7 0.8 iota_compare_fusion.2
  28.5 0.9 iota_compare_fusion.1
  29.6 19.0 %all-to-all-done = bf16[16,2,8448]{2,1,0:T(2,128)(2,1)S(1)} async-done(((bf16[16,2,8448]{2,1,0:T(2,128)(2,1)}), bf16[16,2,8448]{2,1,0:T(2,128)(2,1)S(1)}, u32[]{:S(2)}, u32[]{:S(2)}) %all-to-all-start) | async-done | bytes 540704 | tf_op jit(solution)/shard_map/all_to_all | solution.py:77
  48.6 6.7 %all-to-all-start.1 = ((bf16[16,64,512]{2,1,0:T(8,128)(2,1)}), bf16[16,64,512]{2,1,0:T(8,128)(2,1)S(1)}, u32[]{:S(2)}, u32[]{:S(2)}) async-start(bf16[16,64,512]{2,1,0:T(8,128)(2,1)} %bitcast.98), calls=%async_computation.1 | async-start | bytes 2097152 | tf_op jit(solution)/shard_map/all_to_all | solution.py:83
  55.3 0.4 reshape.265
  55.9 0.3 reshape.238
  56.5 2.3 %reduce-window.6 = f32[8,8,128]{2,1,0:T(8,128)S(1)} reduce-window(f32[8,8,128]{2,1,0:T(8,128)S(1)} %copy.187, f32[]{:T(128)} %constant.52.clone.1), window={size=1x1x128 pad=0_0x0_0x127_0}, to_apply=%region_0.1 | reduce-window | flops 1040384 | bytes 65540 | tf_op jit(solution)/shard_map/reduce-window
  59.5 0.7 multiply_convert_fusion.6
  60.7 2.5 %collective-permute-start = (bf16[2,1024,128]{2,1,0:T(8,128)(2,1)S(1)}, bf16[2,1024,128]{2,1,0:T(8,128)(2,1)S(1)}, u32[]{:S(2)}, u32[]{:S(2)}) collective-permute-start(bf16[2,1024,128]{2,1,0:T(8,128)(2,1)S(1)} %bitcast.118), channel_id=1, source_target_pairs={{0,1},{1,0},{2,3},{3,2},{4,5},{5,4},{6,7},{7,6},{8,9},{9,8},{10,11... | collective-permute-start | bytes 1572872 | tf_op jit(solution)/shard_map/ppermute | solution.py:112
  63.4 0.7 exponential_multiply_fusion
  64.1 0.6 slice.212
  64.7 0.6 slice.213
  65.3 0.6 slice.207
  66.0 0.6 slice.206
  66.6 0.6 slice.197
  67.2 0.6 fusion.56
  67.8 0.6 fusion.54
  68.5 0.9 gather_fusion.1
  69.4 1.0 copy_bitcast_fusion
  70.4 0.3 fusion.30
  70.8 3.6 %select_convert_fusion = bf16[8,256,1024]{2,1,0:T(8,128)(2,1)} fusion(f32[8,1024]{1,0:T(8,128)S(1)} %get-tuple-element.9, f32[8,1024]{1,0:T(8,128)S(1)} %bitcast.125, f32[8,256]{1,0:T(8,128)S(1)} %copy-done.15, f32[256,1024]{1,0:T(8,128)S(1)} %fusion.30, pred[256,1024]{1,0:T(8,128)(4,1)S(1)} %iota_compare_fusion), kind=kLoop, calls=%fused_computation.3 | loop fusion | flops 12582912 | bytes 5578752 | tf_op jit(solution)/shard_map/convert_element_type | solution.py:147
  74.8 3.0 %select_convert_fusion.1 = bf16[8,256,768]{2,1,0:T(8,128)(2,1)} fusion(f32[8,768]{1,0:T(8,128)S(1)} %copy-done.9, f32[8,768]{1,0:T(8,128)S(1)} %copy-done.8, f32[8,256]{1,0:T(8,128)S(1)} %copy-done.14, f32[256,768]{1,0:T(8,128)S(1)} %fusion.32, pred[256,768]{1,0:T(8,128)(4,1)S(1)} %copy-done.6), kind=kLoop, calls=%fused_computation.4 | loop fusion | flops 9437184 | bytes 4186112 | tf_op jit(solution)/shard_map/convert_element_type | solution.py:147
  78.1 2.3 %select_convert_fusion.2 = bf16[8,256,512]{2,1,0:T(8,128)(2,1)} fusion(f32[8,512]{1,0:T(8,128)S(1)} %copy-done.10, f32[8,512]{1,0:T(8,128)S(1)} %copy-done.11, f32[8,256]{1,0:T(8,128)S(1)} %copy-done.13, f32[256,512]{1,0:T(8,128)S(1)} %fusion.34, pred[256,512]{1,0:T(8,128)(4,1)S(1)} %copy-done.7), kind=kLoop, calls=%fused_computation.8 | loop fusion | flops 6291456 | bytes 2793472 | tf_op jit(solution)/shard_map/convert_element_type | solution.py:147
  80.7 0.6 select_convert_fusion.3
  81.3 22.6 %all-to-all-done.1 = bf16[16,64,512]{2,1,0:T(8,128)(2,1)S(1)} async-done(((bf16[16,64,512]{2,1,0:T(8,128)(2,1)}), bf16[16,64,512]{2,1,0:T(8,128)(2,1)S(1)}, u32[]{:S(2)}, u32[]{:S(2)}) %all-to-all-start.1) | async-done | bytes 1048608 | tf_op jit(solution)/shard_map/all_to_all | solution.py:83
  103.9 0.3 bitcast_convert_fusion
  104.2 0.6 copy-done.3
  104.9 2.2 %multiply_convert_fusion.3 = bf16[1024,512]{1,0:T(8,128)(2,1)} fusion(f32[1024,512]{1,0:T(8,128)S(1)} %bitcast_convert_fusion, f32[3,512]{1,0:T(4,128)S(1)} %convert_element_type.105, f32[512]{0:T(512)S(1)} %bitcast.132, f32[512]{0:T(512)S(1)} %bitcast.133, f32[512]{0:T(512)S(1)} %bitcast.131, f32[512]{0:T(512)S(1)} %bitcast.130, f32[512]{0:T(512)S(1)} %copy-done.20), kind=kLoop, calls=%fused_computation.29 | loop fusion | flops 8388608 | bytes 3162112 | tf_op jit(solution)/shard_map/convert_element_type | solution.py:30
  107.1 1.5 copy.189
  108.6 3.7 %fusion.58 = f32[8,256,64]{1,2,0:T(8,128)S(1)} fusion(bf16[8,256,1024]{2,1,0:T(8,128)(2,1)} %select_convert_fusion, bf16[8,64,1024]{2,1,0:T(8,128)(2,1)S(1)} %bitcast.103), kind=kOutput, calls=%fused_computation.128 | convolution fusion | flops 268435456 | bytes 5767168 | tf_op jit(solution)/shard_map/hts,hps->htp/dot_general | solution.py:150
  112.3 1.1 fusion.26
  113.4 0.5 copy-done.2
  113.9 0.8 fusion.28
  114.7 0.4 fusion.36
  115.2 1.3 fusion.15
  116.5 2.3 %reshape.261 = bf16[16,64,512]{1,0,2:T(8,128)(2,1)} reshape(bf16[1024,8,64]{0,2,1:T(8,128)(2,1)S(1)} %fusion.15) | data formatting | bytes 2097152 | tf_op jit(solution)/shard_map/all_to_all | solution.py:177
  118.8 3.3 %copy.194 = bf16[16,64,512]{2,1,0:T(8,128)(2,1)} copy(bf16[16,64,512]{1,0,2:T(8,128)(2,1)} %reshape.261) | data formatting | bytes 2097152 | tf_op jit(solution)/shard_map/all_to_all | solution.py:177
  122.1 6.8 %all-to-all-start.2 = ((bf16[16,64,512]{2,1,0:T(8,128)(2,1)}), bf16[16,64,512]{2,1,0:T(8,128)(2,1)S(1)}, u32[]{:S(2)}, u32[]{:S(2)}) async-start(bf16[16,64,512]{2,1,0:T(8,128)(2,1)} %copy.194), calls=%async_computation.2 | async-start | bytes 2097152 | tf_op jit(solution)/shard_map/all_to_all | solution.py:177
  129.0 1.3 slice.221
  130.3 1.3 slice.220
  131.6 3.3 %fusion.16 = f32[8,64,256]{2,1,0:T(8,128)} fusion(bf16[8,64,1024]{2,1,0:T(8,128)(2,1)S(1)} %bitcast.108, f32[1024,8]{0,1:T(8,128)S(1)} %copy-done.17, f32[1024,256]{1,0:T(8,128)S(1)} %slice_convert_fusion, f32[8,64,256]{2,1,0:T(8,128)} %param.28, f32[8]{0:T(128)S(1)} %exp.49), kind=kOutput, calls=%fused_computation.34 | convolution fusion | flops 272891904 | bytes 3178528 | tf_op jit(solution)/shard_map/hps,shn->hpn/dot_general | solution.py:172
  135.0 42.6 %all-to-all-done.2 = bf16[16,64,512]{2,1,0:T(8,128)(2,1)S(1)} async-done(((bf16[16,64,512]{2,1,0:T(8,128)(2,1)}), bf16[16,64,512]{2,1,0:T(8,128)(2,1)S(1)}, u32[]{:S(2)}, u32[]{:S(2)}) %all-to-all-start.2) | async-done | bytes 1048608 | tf_op jit(solution)/shard_map/all_to_all | solution.py:177
  178.5 0.3 mul.321
  178.8 1.2 copy.201
  180.0 1.3 multiply_convert_fusion.2
  (110 shorter events, 4.5 us)
Async XLA Ops:
  6.1 15.2 %copy-start.5 = (bf16[64,8192]{1,0:T(8,128)(2,1)S(1)}, bf16[64,8192]{1,0:T(8,128)(2,1)}, u32[]{:S(2)}) copy-start(bf16[64,8192]{1,0:T(8,128)(2,1)} %param.15) | copy-start | bytes 3145732
  7.7 14.7 %copy-start.25 = (bf16[3,512]{1,0:T(4,128)(2,1)S(1)}, bf16[3,512]{1,0:T(4,128)(2,1)}, u32[]{:S(2)}) copy-start(bf16[3,512]{1,0:T(4,128)(2,1)} %param.18) | copy-start | bytes 9220
  7.7 14.7 %copy-start.29 = (bf16[512]{0:T(512)(128)(2,1)S(1)}, bf16[512]{0:T(512)(128)(2,1)}, u32[]{:S(2)}) copy-start(bf16[512]{0:T(512)(128)(2,1)} %param.21) | copy-start | bytes 3076
  7.7 16.8 %copy-start = (s32[4]{0:T(128)S(1)}, s32[4]{0:T(128)}, u32[]{:S(2)}) copy-start(s32[4]{0:T(128)} %constant.58.clone) | copy-start | bytes 52
  8.7 18.4 %copy-start.19 = (bf16[4,512]{1,0:T(4,128)(2,1)S(1)}, bf16[4,512]{1,0:T(4,128)(2,1)}, u32[]{:S(2)}) copy-start(bf16[4,512]{1,0:T(4,128)(2,1)} %param.20) | copy-start | bytes 12292
  8.7 39.9 %all-to-all-start = ((bf16[16,2,8448]{2,1,0:T(2,128)(2,1)}), bf16[16,2,8448]{2,1,0:T(2,128)(2,1)S(1)}, u32[]{:S(2)}, u32[]{:S(2)}) async-start(bf16[16,2,8448]{2,1,0:T(2,128)(2,1)} %reshape.264), calls=%async_computation | async-start | bytes 1081344 | tf_op jit(solution)/shard_map/all_to_all | solution.py:77
  48.6 55.3 %all-to-all-start.1 = ((bf16[16,64,512]{2,1,0:T(8,128)(2,1)}), bf16[16,64,512]{2,1,0:T(8,128)(2,1)S(1)}, u32[]{:S(2)}, u32[]{:S(2)}) async-start(bf16[16,64,512]{2,1,0:T(8,128)(2,1)} %bitcast.98), calls=%async_computation.1 | async-start | bytes 2097152 | tf_op jit(solution)/shard_map/all_to_all | solution.py:83
  55.7 0.7 copy-start.26
  55.8 0.7 copy-start.30
  59.4 1.1 copy-start.4
  60.7 7.7 %collective-permute-start = (bf16[2,1024,128]{2,1,0:T(8,128)(2,1)S(1)}, bf16[2,1024,128]{2,1,0:T(8,128)(2,1)S(1)}, u32[]{:S(2)}, u32[]{:S(2)}) collective-permute-start(bf16[2,1024,128]{2,1,0:T(8,128)(2,1)S(1)} %bitcast.118), channel_id=1, source_target_pairs={{0,1},{1,0},{2,3},{3,2},{4,5},{5,4},{6,7},{7,6},{8,9},{9,8},{10,11... | collective-permute-start | bytes 1572872 | tf_op jit(solution)/shard_map/ppermute | solution.py:112
  63.4 3.1 %copy-start.27 = (f32[8]{0:T(128)}, f32[8]{0:T(128)S(1)}, u32[]{:S(2)}) copy-start(f32[8]{0:T(128)S(1)} %slice_reduce_fusion.1) | copy-start | bytes 100
  69.4 1.4 copy-start.15
  70.8 4.0 %copy-start.6 = (pred[256,768]{1,0:T(8,128)(4,1)S(1)}, pred[256,768]{1,0:T(8,128)(4,1)}, u32[]{:S(2)}) copy-start(pred[256,768]{1,0:T(8,128)(4,1)} %iota_compare_fusion.1) | copy-start | bytes 589828
  70.8 4.0 %copy-start.8 = (f32[8,768]{1,0:T(8,128)S(1)}, f32[8,768]{1,0:T(8,128)}, u32[]{:S(2)}) copy-start(f32[8,768]{1,0:T(8,128)} %slice.212) | copy-start | bytes 73732
  70.8 4.0 %copy-start.9 = (f32[8,768]{1,0:T(8,128)S(1)}, f32[8,768]{1,0:T(8,128)}, u32[]{:S(2)}) copy-start(f32[8,768]{1,0:T(8,128)} %slice.213) | copy-start | bytes 73732
  70.8 4.0 %copy-start.14 = (f32[8,256]{1,0:T(8,128)S(1)}, f32[8,256]{1,0:T(8,128)}, u32[]{:S(2)}) copy-start(f32[8,256]{1,0:T(8,128)} %get-tuple-element.14) | copy-start | bytes 24580
  74.8 3.3 %copy-start.7 = (pred[256,512]{1,0:T(8,128)(4,1)S(1)}, pred[256,512]{1,0:T(8,128)(4,1)}, u32[]{:S(2)}) copy-start(pred[256,512]{1,0:T(8,128)(4,1)} %iota_compare_fusion.2) | copy-start | bytes 393220
  74.8 3.3 %copy-start.10 = (f32[8,512]{1,0:T(8,128)S(1)}, f32[8,512]{1,0:T(8,128)}, u32[]{:S(2)}) copy-start(f32[8,512]{1,0:T(8,128)} %slice.207) | copy-start | bytes 49156
  74.8 3.3 %copy-start.11 = (f32[8,512]{1,0:T(8,128)S(1)}, f32[8,512]{1,0:T(8,128)}, u32[]{:S(2)}) copy-start(f32[8,512]{1,0:T(8,128)} %slice.206) | copy-start | bytes 49156
  74.8 3.3 %copy-start.13 = (f32[8,256]{1,0:T(8,128)S(1)}, f32[8,256]{1,0:T(8,128)}, u32[]{:S(2)}) copy-start(f32[8,256]{1,0:T(8,128)} %get-tuple-element.15) | copy-start | bytes 24580
  77.8 2.8 %copy-start.12 = (f32[8,256]{1,0:T(8,128)S(1)}, f32[8,256]{1,0:T(8,128)}, u32[]{:S(2)}) copy-start(f32[8,256]{1,0:T(8,128)} %slice.197) | copy-start | bytes 24580
  80.6 24.2 %copy-start.20 = (f32[512]{0:T(512)S(1)}, f32[512]{0:T(512)}, u32[]{:S(2)}) copy-start(f32[512]{0:T(512)} %convert_element_type.104) | copy-start | bytes 6148
  80.7 24.2 %copy-start.21 = (f32[1,512]{1,0:T(1,128)S(1)}, f32[1,512]{1,0:T(1,128)}, u32[]{:S(2)}) copy-start(f32[1,512]{1,0:T(1,128)} %get-tuple-element.22) | copy-start | bytes 6148
  80.7 24.2 %copy-start.22 = (f32[1,512]{1,0:T(1,128)S(1)}, f32[1,512]{1,0:T(1,128)}, u32[]{:S(2)}) copy-start(f32[1,512]{1,0:T(1,128)} %get-tuple-element.23) | copy-start | bytes 6148
  80.7 24.2 %copy-start.23 = (f32[1,512]{1,0:T(1,128)S(1)}, f32[1,512]{1,0:T(1,128)}, u32[]{:S(2)}) copy-start(f32[1,512]{1,0:T(1,128)} %get-tuple-element.24) | copy-start | bytes 6148
  80.7 24.2 %copy-start.24 = (f32[1,512]{1,0:T(1,128)S(1)}, f32[1,512]{1,0:T(1,128)}, u32[]{:S(2)}) copy-start(f32[1,512]{1,0:T(1,128)} %get-tuple-element.25) | copy-start | bytes 6148
  103.9 1.0 copy-start.3
  108.6 3.7 %copy-start.1 = (bf16[8,256,768]{2,1,0:T(8,128)(2,1)S(1)}, bf16[8,256,768]{2,1,0:T(8,128)(2,1)}, u32[]{:S(2)}) copy-start(bf16[8,256,768]{2,1,0:T(8,128)(2,1)} %select_convert_fusion.1) | copy-start | bytes 9437188
  112.3 1.6 copy-start.2
  113.9 1.2 copy-start.16
  113.9 1.2 copy-start.31
  113.9 1.2 copy-start.32
  118.8 10.2 %copy-start.18 = (bf16[8192]{0:T(1024)(128)(2,1)S(1)}, bf16[8192]{0:T(1024)(128)(2,1)}, u32[]{:S(2)}) copy-start(bf16[8192]{0:T(1024)(128)(2,1)} %param.27) | copy-start | bytes 49156
  118.8 10.2 %copy-start.28 = (f32[8]{0:T(128)S(1)}, f32[8]{0:T(128)}, u32[]{:S(2)}) copy-start(f32[8]{0:T(128)} %copy-done.27) | copy-start | bytes 100
  122.1 9.5 %copy-start.17 = (f32[1024,8]{0,1:T(8,128)S(1)}, f32[1024,8]{0,1:T(8,128)}, u32[]{:S(2)}) copy-start(f32[1024,8]{0,1:T(8,128)} %get-tuple-element.8) | copy-start | bytes 98308
  122.1 55.4 %all-to-all-start.2 = ((bf16[16,64,512]{2,1,0:T(8,128)(2,1)}), bf16[16,64,512]{2,1,0:T(8,128)(2,1)S(1)}, u32[]{:S(2)}, u32[]{:S(2)}) async-start(bf16[16,64,512]{2,1,0:T(8,128)(2,1)} %copy.194), calls=%async_computation.2 | async-start | bytes 2097152 | tf_op jit(solution)/shard_map/all_to_all | solution.py:177

commit v9 on v8

--- a/solution.py
+++ b/solution.py
@@ -71,17 +71,27 @@
     )
     bc_send = jnp.transpose(bc_send, (1, 0, 2))
     step_send = jnp.transpose(step_raw.reshape(token_rows, tensor_count, heads_here), (1, 0, 2))
+    x_send = jnp.transpose(inner_x.reshape(token_rows, tensor_count, x_width), (1, 0, 2))
+    half_width = x_width // 2
+    half_heads = heads_here // 2
     small_send = jnp.concatenate(
-        [bc_send.reshape(tensor_count, -1), step_send.reshape(tensor_count, -1)], axis=1
+        [
+            bc_send.reshape(tensor_count, -1),
+            step_send.reshape(tensor_count, -1),
+            x_send[:, :, :half_width].reshape(tensor_count, -1),
+        ],
+        axis=1,
     )
     small_recv = lax.all_to_all(small_send, TENSOR, 0, 0, tiled=True)
+    late_send, small_recv = lax.optimization_barrier((x_send[:, :, half_width:], small_recv))
     bc_end = token_rows * 2 * bc_width
+    step_end = bc_end + token_rows * heads_here
     head_bc_pair = small_recv[:, :bc_end].reshape(length, 2 * bc_width)
-    head_step = small_recv[:, bc_end:].reshape(length, heads_here)
-
-    x_send = jnp.transpose(inner_x.reshape(token_rows, tensor_count, x_width), (1, 0, 2))
-    x_recv = lax.all_to_all(x_send, TENSOR, 0, 0, tiled=True)
-    head_x = x_recv.reshape(length, x_width)
+    head_step = small_recv[:, bc_end:step_end].reshape(length, heads_here)
+    early_x = small_recv[:, step_end:].reshape(length, half_width)
+
+    late_recv = lax.all_to_all(late_send, TENSOR, 0, 0, tiled=True)
+    late_x = late_recv.reshape(length, half_width)
 
     group_rank = lax.axis_index("tj")
     column_start = device_rank * bc_width
@@ -123,12 +133,28 @@
     step_cols = jnp.transpose(step_size)
     running_cols = jnp.transpose(running)
 
-    mixed_x = causal_conv(head_x, conv_state_x, conv_weight_x, conv_bias_x)
-    values = mixed_x.reshape(length, heads_here, HEAD_DIM)
-    values_t = jnp.transpose(values, (1, 2, 0))
+    early_values_t = jnp.transpose(
+        causal_conv(
+            early_x,
+            conv_state_x[:, :half_width],
+            conv_weight_x[:, :half_width],
+            conv_bias_x[:half_width],
+        ).reshape(length, half_heads, HEAD_DIM),
+        (1, 2, 0),
+    )
+    late_values_t = jnp.transpose(
+        causal_conv(
+            late_x,
+            conv_state_x[:, half_width:],
+            conv_weight_x[:, half_width:],
+            conv_bias_x[half_width:],
+        ).reshape(length, half_heads, HEAD_DIM),
+        (1, 2, 0),
+    )
 
     query_rows = min(256, length)
-    pieces = []
+    early_pieces = []
+    late_pieces = []
     for row_start in range(0, length, query_rows):
         row_stop = row_start + query_rows
         scores = jnp.einsum(
@@ -146,15 +172,22 @@
             causal[None], scores[None] * decayed * step_cols[:, None, :row_stop], 0.0
         ).astype(jnp.bfloat16)
         weights = lax.optimization_barrier(weights)
-        pieces.append(
+        early_pieces.append(
             jnp.einsum(
                 "hts,hps->htp",
-                weights,
-                values_t[:, :, :row_stop],
+                weights[:half_heads],
+                early_values_t[:, :, :row_stop],
                 preferred_element_type=jnp.float32,
             )
         )
-    local_all = jnp.concatenate(pieces, axis=1)
+        late_pieces.append(
+            jnp.einsum(
+                "hts,hps->htp",
+                weights[half_heads:],
+                late_values_t[:, :, :row_stop],
+                preferred_element_type=jnp.float32,
+            )
+        )
     carried = jnp.einsum(
         "tn,hpn->htp",
         output_map.astype(jnp.float32),
@@ -162,8 +195,20 @@
         precision=lax.Precision.HIGHEST,
     )
     carried = carried * jnp.exp(running_cols)[:, :, None]
-    channels = jnp.transpose(values_t, (0, 2, 1)).astype(jnp.float32)
-    mixed = local_all + carried + skip_gain[:, None, None] * channels
+    early_mixed = (
+        jnp.concatenate(early_pieces, axis=1)
+        + carried[:half_heads]
+        + skip_gain[:half_heads, None, None]
+        * jnp.transpose(early_values_t, (0, 2, 1)).astype(jnp.float32)
+    )
+    late_mixed = (
+        jnp.concatenate(late_pieces, axis=1)
+        + carried[half_heads:]
+        + skip_gain[half_heads:, None, None]
+        * jnp.transpose(late_values_t, (0, 2, 1)).astype(jnp.float32)
+    )
+    mixed = jnp.concatenate([early_mixed, late_mixed], axis=0)
+    values_t = jnp.concatenate([early_values_t, late_values_t], axis=0)
     mixed_y = jnp.transpose(mixed.astype(jnp.bfloat16), (1, 0, 2)).reshape(length, x_width)
     tail_decay = jnp.exp(running[length - 1][None, :] - running) * step_size
     weighted = (input_map.astype(jnp.float32)[:, None, :] * tail_decay[:, :, None]).astype(
@@ -176,7 +221,9 @@
 
     token_y = lax.all_to_all(mixed_y, TENSOR, split_axis=0, concat_axis=1, tiled=True)
     normed = group_norm(token_y, norm_weight)
-    tail_x = head_x[length - CONV_K + 1 :]
+    tail_x = jnp.concatenate(
+        [early_x[length - CONV_K + 1 :], late_x[length - CONV_K + 1 :]], axis=1
+    )
     tail_bc = head_bc_pair[length - CONV_K + 1 :, :bc_width]
     return (normed, final_state, tail_x, tail_bc)
 

time: 182 us -> 192 us (1.055)
  the two profiles are of different devices: /device:TPU:65 before, /device:TPU:77 now
where the time goes in v9:
time: 192 us; the launch traced here: 191 us
  waiting for transfers between devices  83.9 us (44%)
  local copies, waits for them, and re-layouts  35.2 us (18%)
  starting transfers between devices  28.8 us (15%)
  other arithmetic  25.9 us (13%)
  matrix products  15.7 us (8%)
    all_to_all x1, waiting for transfers between devices, local(): lax.all_to_all(mixed_y, TENSOR, split_axis=0, concat_axis=1, tiled=True)  42.1 us
    all_to_all x1, waiting for transfers between devices, local(): small_recv = lax.all_to_all(small_send, TENSOR, 0, 0, tiled=True)  39.1 us
    all_to_all x1, starting transfers between devices, local(): small_recv = lax.all_to_all(small_send, TENSOR, 0, 0, tiled=True)  12.5 us
    unnamed x124, local copies, waits for them, and re-layouts  9.21 us
    all_to_all x1, starting transfers between devices, local(): lax.all_to_all(mixed_y, TENSOR, split_axis=0, concat_axis=1, tiled=True)  7.02 us
    all_to_all x1, starting transfers between devices, local(): late_recv = lax.all_to_all(late_send, TENSOR, 0, 0, tiled=True)  6.85 us
    convert_element_type x4, other arithmetic, local(): weights = jnp.where(causal[None], scores[None] * decayed * step_cols[:, N...  6.05 us
    all_to_all x2, local copies, waits for them, and re-layouts, local(): lax.all_to_all(mixed_y, TENSOR, split_axis=0, concat_axis=1, tiled=True)  5.71 us
  transfers between devices with their start and end apart: 4, of which 3 were waited for; matrix products, arithmetic and copies ran while one was open for 19% of the time, Pallas kernels for 0%

profile of v9, /device:TPU:77, one launch (start us, length us, event | category | flops | bytes accessed | tf_op | source)
XLA Modules:
  0.0 191.1 jit_solution(188602360462759953)
XLA Ops:
  0.6 1.1 reshape.233
  1.7 1.1 stack_reshape.3
  2.9 0.8 copy.252
  4.1 0.7 pad_maximum_fusion.4
  4.9 0.8 copy.250
  6.5 0.9 slice_bitcast_fusion.2
  8.0 1.5 reduce.7
  9.5 1.2 reshape.282
  10.7 12.5 %all-to-all-start = ((bf16[16,2,16640]{2,1,0:T(2,128)(2,1)}), bf16[16,2,16640]{2,1,0:T(2,128)(2,1)S(1)}, u32[]{:S(2)}, u32[]{:S(2)}) async-start(bf16[16,2,16640]{2,1,0:T(2,128)(2,1)} %reshape.282), calls=%async_computation | async-start | bytes 2129920 | tf_op jit(solution)/shard_map/all_to_all | solution.py:85
  23.2 0.6 gather_fusion
  23.8 0.8 fusion.78
  25.2 0.7 constant_dynamic-slice_fusion.1
  25.9 0.7 constant_dynamic-slice_fusion.3
  26.6 0.6 pad_clamp_fusion
  29.0 0.7 fusion.79
  30.2 0.6 slice_convert_fusion.11
  30.8 0.6 slice_convert_fusion.3
  31.4 0.8 iota_compare_fusion.2
  32.2 0.9 iota_compare_fusion.1
  33.3 39.1 %all-to-all-done = bf16[16,2,16640]{2,1,0:T(2,128)(2,1)S(1)} async-done(((bf16[16,2,16640]{2,1,0:T(2,128)(2,1)}), bf16[16,2,16640]{2,1,0:T(2,128)(2,1)S(1)}, u32[]{:S(2)}, u32[]{:S(2)}) %all-to-all-start) | async-done | bytes 1064992 | tf_op jit(solution)/shard_map/all_to_all | solution.py:85
  72.4 0.9 reshape.283
  74.2 2.3 %reduce-window.6 = f32[8,8,128]{2,1,0:T(8,128)S(1)} reduce-window(f32[8,8,128]{2,1,0:T(8,128)S(1)} %copy.261, f32[]{:T(128)} %constant.52.clone.1), window={size=1x1x128 pad=0_0x0_0x127_0}, to_apply=%region_0.1 | reduce-window | flops 1040384 | bytes 65540 | tf_op jit(solution)/shard_map/reduce-window
  76.9 0.6 slice.342
  77.7 0.7 exponential_multiply_fusion
  78.4 0.6 slice.343
  79.0 0.9 copy.263
  80.0 6.9 %all-to-all-start.1 = ((bf16[16,64,256]{2,1,0:T(8,128)(2,1)}), bf16[16,64,256]{2,1,0:T(8,128)(2,1)}, u32[]{:S(2)}, u32[]{:S(2)}) async-start(bf16[16,64,256]{2,1,0:T(8,128)(2,1)} %copy.263), calls=%async_computation.1 | async-start | bytes 1048576 | tf_op jit(solution)/shard_map/all_to_all | solution.py:93
  87.5 0.7 multiply_convert_fusion.7
  88.8 2.5 %collective-permute-start = (bf16[2,1024,128]{2,1,0:T(8,128)(2,1)S(1)}, bf16[2,1024,128]{2,1,0:T(8,128)(2,1)S(1)}, u32[]{:S(2)}, u32[]{:S(2)}) collective-permute-start(bf16[2,1024,128]{2,1,0:T(8,128)(2,1)S(1)} %bitcast.130), channel_id=1, source_target_pairs={{0,1},{1,0},{2,3},{3,2},{4,5},{5,4},{6,7},{7,6},{8,9},{9,8},{10,11... | collective-permute-start | bytes 1572872 | tf_op jit(solution)/shard_map/ppermute | solution.py:122
  91.4 0.7 multiply_convert_fusion.6
  92.1 1.0 copy.262
  93.1 0.6 fusion.77
  93.7 0.6 fusion.74
  94.4 0.9 gather_fusion.1
  96.8 0.6 select_convert_fusion.3
  97.5 1.3 select_convert_fusion.2
  98.8 1.8 select_convert_fusion.1
  100.7 2.3 %select_convert_fusion = bf16[8,256,1024]{2,1,0:T(8,128)(2,1)S(1)} fusion(f32[8,1024]{1,0:T(8,128)S(1)} %get-tuple-element.23, f32[8,1024]{1,0:T(8,128)S(1)} %bitcast.139, f32[8,256]{1,0:T(8,128)S(1)} %copy-done.25, f32[256,1024]{1,0:T(8,128)S(1)} %fusion.39, pred[256,1024]{1,0:T(8,128)(4,1)S(1)} %iota_compare_fusion), kind=kLoop, calls=%fused_computation.3 | loop fusion | flops 12582912 | bytes 5578752 | tf_op jit(solution)/shard_map/convert_element_type | solution.py:173
  103.0 1.3 fusion.58
  104.8 0.8 copy-done.20
  105.6 2.4 %bitcast_multiply_fusion = f32[8,1024,64]{1,2,0:T(8,128)} fusion(f32[8,64,256]{2,1,0:T(8,128)S(1)} %copy-done.20, f32[8,1024]{1,0:T(8,128)S(1)} %copy-done.22, bf16[1024,512]{1,0:T(8,128)(2,1)S(1)} %copy_bitcast_fusion.1), kind=kOutput, calls=%fused_computation.12 | convolution fusion | flops 1611137024 | bytes 3178496 | tf_op jit(solution)/shard_map/tn,hpn->htp/dot_general | solution.py:191
  108.0 1.3 fusion.43
  109.3 1.5 fusion.80
  110.8 2.8 %all-to-all-done.1 = bf16[16,64,256]{2,1,0:T(8,128)(2,1)} async-done(((bf16[16,64,256]{2,1,0:T(8,128)(2,1)}), bf16[16,64,256]{2,1,0:T(8,128)(2,1)}, u32[]{:S(2)}, u32[]{:S(2)}) %all-to-all-start.1) | async-done | bytes 524320 | tf_op jit(solution)/shard_map/all_to_all | solution.py:93
  113.6 1.1 bitcast_convert_fusion
  114.7 1.5 multiply_convert_fusion.5
  116.2 2.0 %copy.264 = bf16[1024,256]{0,1:T(8,128)(2,1)} copy(bf16[1024,256]{1,0:T(8,128)(2,1)} %multiply_convert_fusion.5) | data formatting | bytes 1048576 | tf_op jit(solution)/shard_map/convert_element_type | solution.py:30
  118.3 1.3 fusion.53
  119.6 1.8 fusion.47
  121.4 0.6 fusion.41
  122.0 1.6 copy-done.2
  123.6 0.8 fusion.81
  124.6 0.7 copy-done.11
  126.2 2.3 %reshape.279 = bf16[16,64,512]{1,0,2:T(8,128)(2,1)} reshape(bf16[1024,8,64]{0,2,1:T(8,128)(2,1)S(1)} %maximum_bitcast_fusion.1) | data formatting | bytes 2097152 | tf_op jit(solution)/shard_map/all_to_all | solution.py:222
  128.5 3.4 %copy.269 = bf16[16,64,512]{2,1,0:T(8,128)(2,1)} copy(bf16[16,64,512]{1,0,2:T(8,128)(2,1)} %reshape.279) | data formatting | bytes 2097152 | tf_op jit(solution)/shard_map/all_to_all | solution.py:222
  131.9 7.0 %all-to-all-start.2 = ((bf16[16,64,512]{2,1,0:T(8,128)(2,1)}), bf16[16,64,512]{2,1,0:T(8,128)(2,1)S(1)}, u32[]{:S(2)}, u32[]{:S(2)}) async-start(bf16[16,64,512]{2,1,0:T(8,128)(2,1)} %copy.269), calls=%async_computation.2 | async-start | bytes 2097152 | tf_op jit(solution)/shard_map/all_to_all | solution.py:222
  138.9 0.7 slice.359
  139.6 1.2 slice.361
  140.9 0.7 slice.360
  141.6 0.6 pad_maximum_fusion.5
  142.2 3.3 %fusion.4 = f32[8,64,256]{2,1,0:T(8,128)} fusion(f32[1024,8]{0,1:T(8,128)S(1)} %copy-done.27, f32[1024,256]{1,0:T(8,128)S(1)} %slice_convert_fusion, bf16[4,64,1024]{2,1,0:T(8,128)(2,1)S(1)} %bitcast.121, bf16[4,64,1024]{2,1,0:T(8,128)(2,1)S(1)} %bitcast.115, f32[8,64,256]{2,1,0:T(8,128)} %param.28, f32[8]{0:T(128)S(1)} %exp.52), kind=kOutput, calls=%fused_computation.21 | convolution fusion | flops 273416192 | bytes 3178528 | tf_op jit(solution)/shard_map/hps,shn->hpn/dot_general | solution.py:217
  145.5 42.1 %all-to-all-done.2 = bf16[16,64,512]{2,1,0:T(8,128)(2,1)S(1)} async-done(((bf16[16,64,512]{2,1,0:T(8,128)(2,1)}), bf16[16,64,512]{2,1,0:T(8,128)(2,1)S(1)}, u32[]{:S(2)}, u32[]{:S(2)}) %all-to-all-start.2) | async-done | bytes 1048608 | tf_op jit(solution)/shard_map/all_to_all | solution.py:222
  188.7 1.2 copy.277
  189.9 1.2 multiply_convert_fusion.2
  (176 shorter events, 11.9 us)
Async XLA Ops:
  4.1 2.0 %copy-start.15 = (bf16[64,8192]{1,0:T(8,128)(2,1)S(1)}, bf16[64,8192]{1,0:T(8,128)(2,1)}, u32[]{:S(2)}) copy-start(bf16[64,8192]{1,0:T(8,128)(2,1)} %param.15) | copy-start | bytes 3145732
  9.4 13.7 %copy-start = (s32[4]{0:T(128)S(1)}, s32[4]{0:T(128)}, u32[]{:S(2)}) copy-start(s32[4]{0:T(128)} %constant.58.clone) | copy-start | bytes 52
  9.4 19.5 %copy-start.52 = (f32[8]{0:T(128)S(1)}, f32[8]{0:T(128)}, u32[]{:S(2)}) copy-start(f32[8]{0:T(128)} %param.26) | copy-start | bytes 100
  9.5 20.2 %copy-start.55 = (bf16[512]{0:T(512)(128)(2,1)S(1)}, bf16[512]{0:T(512)(128)(2,1)}, u32[]{:S(2)}) copy-start(bf16[512]{0:T(512)(128)(2,1)} %param.21) | copy-start | bytes 3076
  9.5 20.8 %copy-start.32 = (bf16[4,512]{1,0:T(4,128)(2,1)S(1)}, bf16[4,512]{1,0:T(4,128)(2,1)}, u32[]{:S(2)}) copy-start(bf16[4,512]{1,0:T(4,128)(2,1)} %param.20) | copy-start | bytes 12292
  9.5 21.4 %copy-start.33 = (bf16[3,512]{1,0:T(4,128)(2,1)S(1)}, bf16[3,512]{1,0:T(4,128)(2,1)}, u32[]{:S(2)}) copy-start(bf16[3,512]{1,0:T(4,128)(2,1)} %param.18) | copy-start | bytes 9220
  10.7 61.8 %all-to-all-start = ((bf16[16,2,16640]{2,1,0:T(2,128)(2,1)}), bf16[16,2,16640]{2,1,0:T(2,128)(2,1)S(1)}, u32[]{:S(2)}, u32[]{:S(2)}) async-start(bf16[16,2,16640]{2,1,0:T(2,128)(2,1)} %reshape.282), calls=%async_computation | async-start | bytes 2129920 | tf_op jit(solution)/shard_map/all_to_all | solution.py:85
  73.4 0.7 copy-start.49
  73.4 0.7 copy-start.56
  73.5 5.6 %copy-start.14 = (bf16[16,64,256]{2,0,1:T(8,128)(2,1)S(1)}, bf16[16,64,256]{2,0,1:T(8,128)(2,1)}, u32[]{:S(2)}) copy-start(bf16[16,64,256]{2,0,1:T(8,128)(2,1)} %get-tuple-element.7) | copy-start | bytes 1572868
  77.7 1.3 copy-start.50
  80.0 7.5 %copy-start.30 = (f32[3,256]{1,0:T(4,128)S(1)}, f32[3,256]{1,0:T(4,128)}, u32[]{:S(2)}) copy-start(f32[3,256]{1,0:T(4,128)} %maximum_convert_fusion) | copy-start | bytes 9220
  80.0 7.5 %copy-start.44 = (f32[256]{0:T(256)S(1)}, f32[256]{0:T(256)}, u32[]{:S(2)}) copy-start(f32[256]{0:T(256)} %maximum_convert_fusion.1) | copy-start | bytes 3076
  80.0 7.5 %copy-start.45 = (f32[1,256]{1,0:T(1,128)S(1)}, f32[1,256]{1,0:T(1,128)}, u32[]{:S(2)}) copy-start(f32[1,256]{1,0:T(1,128)} %get-tuple-element.46) | copy-start | bytes 3076
  80.0 7.5 %copy-start.46 = (f32[1,256]{1,0:T(1,128)S(1)}, f32[1,256]{1,0:T(1,128)}, u32[]{:S(2)}) copy-start(f32[1,256]{1,0:T(1,128)} %get-tuple-element.47) | copy-start | bytes 3076
  80.0 7.5 %copy-start.47 = (f32[1,256]{1,0:T(1,128)S(1)}, f32[1,256]{1,0:T(1,128)}, u32[]{:S(2)}) copy-start(f32[1,256]{1,0:T(1,128)} %get-tuple-element.48) | copy-start | bytes 3076
  80.0 7.5 %copy-start.48 = (f32[1,256]{1,0:T(1,128)S(1)}, f32[1,256]{1,0:T(1,128)}, u32[]{:S(2)}) copy-start(f32[1,256]{1,0:T(1,128)} %get-tuple-element.49) | copy-start | bytes 3076
  80.0 33.6 %all-to-all-start.1 = ((bf16[16,64,256]{2,1,0:T(8,128)(2,1)}), bf16[16,64,256]{2,1,0:T(8,128)(2,1)}, u32[]{:S(2)}, u32[]{:S(2)}) async-start(bf16[16,64,256]{2,1,0:T(8,128)(2,1)} %copy.263), calls=%async_computation.1 | async-start | bytes 1048576 | tf_op jit(solution)/shard_map/all_to_all | solution.py:93
  87.1 1.6 copy-start.12
  87.4 1.4 copy-start.13
  88.2 3.1 %copy-start.29 = (f32[3,256]{1,0:T(4,128)S(1)}, f32[3,256]{1,0:T(4,128)}, u32[]{:S(2)}) copy-start(f32[3,256]{1,0:T(4,128)} %get-tuple-element.42) | copy-start | bytes 9220
  88.2 3.1 %copy-start.39 = (f32[256]{0:T(256)S(1)}, f32[256]{0:T(256)}, u32[]{:S(2)}) copy-start(f32[256]{0:T(256)} %get-tuple-element.50) | copy-start | bytes 3076
  88.2 3.1 %copy-start.40 = (f32[1,256]{1,0:T(1,128)S(1)}, f32[1,256]{1,0:T(1,128)}, u32[]{:S(2)}) copy-start(f32[1,256]{1,0:T(1,128)} %get-tuple-element.34) | copy-start | bytes 3076
  88.2 3.1 %copy-start.41 = (f32[1,256]{1,0:T(1,128)S(1)}, f32[1,256]{1,0:T(1,128)}, u32[]{:S(2)}) copy-start(f32[1,256]{1,0:T(1,128)} %get-tuple-element.37) | copy-start | bytes 3076
  88.2 3.1 %copy-start.42 = (f32[1,256]{1,0:T(1,128)S(1)}, f32[1,256]{1,0:T(1,128)}, u32[]{:S(2)}) copy-start(f32[1,256]{1,0:T(1,128)} %get-tuple-element.38) | copy-start | bytes 3076
  88.2 3.1 %copy-start.43 = (f32[1,256]{1,0:T(1,128)S(1)}, f32[1,256]{1,0:T(1,128)}, u32[]{:S(2)}) copy-start(f32[1,256]{1,0:T(1,128)} %get-tuple-element.39) | copy-start | bytes 3076
  88.8 5.5 %collective-permute-start = (bf16[2,1024,128]{2,1,0:T(8,128)(2,1)S(1)}, bf16[2,1024,128]{2,1,0:T(8,128)(2,1)S(1)}, u32[]{:S(2)}, u32[]{:S(2)}) collective-permute-start(bf16[2,1024,128]{2,1,0:T(8,128)(2,1)S(1)} %bitcast.130), channel_id=1, source_target_pairs={{0,1},{1,0},{2,3},{3,2},{4,5},{5,4},{6,7},{7,6},{8,9},{9,8},{10,11... | collective-permute-start | bytes 1572872 | tf_op jit(solution)/shard_map/ppermute | solution.py:122
  93.7 1.6 copy-start.57
  95.7 9.1 %copy-start.4 = (bf16[1024,512]{1,0:T(8,128)(2,1)}, bf16[1024,512]{1,0:T(8,128)(2,1)S(1)}, u32[]{:S(2)}) copy-start(bf16[1024,512]{1,0:T(8,128)(2,1)S(1)} %copy_bitcast_fusion.1) | copy-start | bytes 3145732
  96.1 1.3 copy-start.21
  96.8 2.0 %copy-start.19 = (pred[256,768]{1,0:T(8,128)(4,1)S(1)}, pred[256,768]{1,0:T(8,128)(4,1)}, u32[]{:S(2)}) copy-start(pred[256,768]{1,0:T(8,128)(4,1)} %iota_compare_fusion.1) | copy-start | bytes 589828
  96.8 2.0 %copy-start.23 = (f32[8,768]{1,0:T(8,128)S(1)}, f32[8,768]{1,0:T(8,128)}, u32[]{:S(2)}) copy-start(f32[8,768]{1,0:T(8,128)} %slice.342) | copy-start | bytes 73732
  96.8 2.0 %copy-start.24 = (f32[8,768]{1,0:T(8,128)S(1)}, f32[8,768]{1,0:T(8,128)}, u32[]{:S(2)}) copy-start(f32[8,768]{1,0:T(8,128)} %slice.343) | copy-start | bytes 73732
  96.8 2.0 %copy-start.26 = (f32[8,256]{1,0:T(8,128)S(1)}, f32[8,256]{1,0:T(8,128)}, u32[]{:S(2)}) copy-start(f32[8,256]{1,0:T(8,128)} %get-tuple-element.28) | copy-start | bytes 24580
  97.5 5.6 %copy-start.10 = (bf16[8,256,256]{2,1,0:T(8,128)(2,1)}, bf16[8,256,256]{2,1,0:T(8,128)(2,1)S(1)}, u32[]{:S(2)}) copy-start(bf16[8,256,256]{2,1,0:T(8,128)(2,1)S(1)} %select_convert_fusion.3) | copy-start | bytes 3145732
  98.8 5.6 %copy-start.3 = (bf16[8,256,512]{2,1,0:T(8,128)(2,1)}, bf16[8,256,512]{2,1,0:T(8,128)(2,1)S(1)}, u32[]{:S(2)}) copy-start(bf16[8,256,512]{2,1,0:T(8,128)(2,1)S(1)} %select_convert_fusion.2) | copy-start | bytes 6291460
  98.8 1.9 copy-start.25
  100.7 2.4 %copy-start.6 = (bf16[1024,256]{0,1:T(8,128)(2,1)S(1)}, bf16[1024,256]{0,1:T(8,128)(2,1)}, u32[]{:S(2)}) copy-start(bf16[1024,256]{0,1:T(8,128)(2,1)} %copy.262) | copy-start | bytes 1572868
  103.0 6.3 %copy-start.1 = (bf16[8,256,1024]{2,1,0:T(8,128)(2,1)}, bf16[8,256,1024]{2,1,0:T(8,128)(2,1)S(1)}, u32[]{:S(2)}) copy-start(bf16[8,256,1024]{2,1,0:T(8,128)(2,1)S(1)} %select_convert_fusion) | copy-start | bytes 12582916
  104.3 1.2 copy-start.20
  104.3 1.2 copy-start.22
  109.3 5.4 %copy-start.28 = (f32[3,256]{1,0:T(4,128)S(1)}, f32[3,256]{1,0:T(4,128)}, u32[]{:S(2)}) copy-start(f32[3,256]{1,0:T(4,128)} %get-tuple-element.43) | copy-start | bytes 9220
  109.3 5.4 %copy-start.34 = (f32[256]{0:T(256)S(1)}, f32[256]{0:T(256)}, u32[]{:S(2)}) copy-start(f32[256]{0:T(256)} %get-tuple-element.51) | copy-start | bytes 3076
  109.3 5.4 %copy-start.35 = (f32[1,256]{1,0:T(1,128)S(1)}, f32[1,256]{1,0:T(1,128)}, u32[]{:S(2)}) copy-start(f32[1,256]{1,0:T(1,128)} %get-tuple-element.35) | copy-start | bytes 3076
  109.3 5.4 %copy-start.36 = (f32[1,256]{1,0:T(1,128)S(1)}, f32[1,256]{1,0:T(1,128)}, u32[]{:S(2)}) copy-start(f32[1,256]{1,0:T(1,128)} %get-tuple-element.36) | copy-start | bytes 3076
  109.3 5.4 %copy-start.37 = (f32[1,256]{1,0:T(1,128)S(1)}, f32[1,256]{1,0:T(1,128)}, u32[]{:S(2)}) copy-start(f32[1,256]{1,0:T(1,128)} %get-tuple-element.40) | copy-start | bytes 3076
  109.3 5.4 %copy-start.38 = (f32[1,256]{1,0:T(1,128)S(1)}, f32[1,256]{1,0:T(1,128)}, u32[]{:S(2)}) copy-start(f32[1,256]{1,0:T(1,128)} %get-tuple-element.41) | copy-start | bytes 3076
  119.6 1.8 copy-start.8
  121.4 2.2 %copy-start.2 = (bf16[8,256,1024]{2,1,0:T(8,128)(2,1)S(1)}, bf16[8,256,1024]{2,1,0:T(8,128)(2,1)}, u32[]{:S(2)}) copy-start(bf16[8,256,1024]{2,1,0:T(8,128)(2,1)} %copy-done.1) | copy-start | bytes 12582916
  123.6 1.0 copy-start.7
  123.6 1.8 copy-start.11
  123.6 1.8 copy-start.16
  123.6 1.8 copy-start.17
  123.6 1.9 copy-start.18
  123.6 1.9 copy-start.53
  123.6 1.9 copy-start.54
  128.5 10.4 %copy-start.31 = (bf16[8192]{0:T(1024)(128)(2,1)S(1)}, bf16[8192]{0:T(1024)(128)(2,1)}, u32[]{:S(2)}) copy-start(bf16[8192]{0:T(1024)(128)(2,1)} %param.27) | copy-start | bytes 49156
  128.5 11.1 %copy-start.51 = (f32[8]{0:T(128)S(1)}, f32[8]{0:T(128)}, u32[]{:S(2)}) copy-start(f32[8]{0:T(128)} %copy-done.50) | copy-start | bytes 100
  128.5 12.4 %copy-start.5 = (bf16[1024,512]{1,0:T(8,128)(2,1)S(1)}, bf16[1024,512]{1,0:T(8,128)(2,1)}, u32[]{:S(2)}) copy-start(bf16[1024,512]{1,0:T(8,128)(2,1)} %copy-done.4) | copy-start | bytes 3145732
  131.9 10.3 %copy-start.9 = (bf16[1024,256]{0,1:T(8,128)(2,1)S(1)}, bf16[1024,256]{0,1:T(8,128)(2,1)}, u32[]{:S(2)}) copy-start(bf16[1024,256]{0,1:T(8,128)(2,1)} %copy.264) | copy-start | bytes 1572868
  131.9 10.3 %copy-start.27 = (f32[1024,8]{0,1:T(8,128)S(1)}, f32[1024,8]{0,1:T(8,128)}, u32[]{:S(2)}) copy-start(f32[1024,8]{0,1:T(8,128)} %get-tuple-element.22) | copy-start | bytes 98308
  131.9 55.6 %all-to-all-start.2 = ((bf16[16,64,512]{2,1,0:T(8,128)(2,1)}), bf16[16,64,512]{2,1,0:T(8,128)(2,1)S(1)}, u32[]{:S(2)}, u32[]{:S(2)}) async-start(bf16[16,64,512]{2,1,0:T(8,128)(2,1)} %copy.269), calls=%async_computation.2 | async-start | bytes 2097152 | tf_op jit(solution)/shard_map/all_to_all | solution.py:222

commit v10 on v8

--- a/solution.py
+++ b/solution.py
@@ -66,18 +66,17 @@
 
     quarters = inner_bc.reshape(token_rows, GROUPS, 2, group_size // 2, bc_width)
     across_quarters = jnp.flip(quarters, axis=2)
-    bc_send = jnp.stack([quarters, across_quarters], axis=4).reshape(
-        token_rows, tensor_count, 2 * bc_width
-    )
-    bc_send = jnp.transpose(bc_send, (1, 0, 2))
-    step_send = jnp.transpose(step_raw.reshape(token_rows, tensor_count, heads_here), (1, 0, 2))
-    small_send = jnp.concatenate(
-        [bc_send.reshape(tensor_count, -1), step_send.reshape(tensor_count, -1)], axis=1
-    )
+    bc_rows = jnp.transpose(
+        jnp.stack([quarters, across_quarters], axis=4), (1, 2, 3, 0, 4, 5)
+    ).reshape(tensor_count, token_rows * 2, bc_width)
+    step_rows = jnp.transpose(
+        step_raw.reshape(token_rows, tensor_count, heads_here), (1, 0, 2)
+    ).reshape(tensor_count, token_rows * heads_here // bc_width, bc_width)
+    small_send = jnp.concatenate([bc_rows, step_rows], axis=1)
     small_recv = lax.all_to_all(small_send, TENSOR, 0, 0, tiled=True)
-    bc_end = token_rows * 2 * bc_width
-    head_bc_pair = small_recv[:, :bc_end].reshape(length, 2 * bc_width)
-    head_step = small_recv[:, bc_end:].reshape(length, heads_here)
+    bc_rows_end = token_rows * 2
+    head_bc_pair = small_recv[:, :bc_rows_end].reshape(length, 2 * bc_width)
+    head_step = small_recv[:, bc_rows_end:].reshape(length, heads_here)
 
     x_send = jnp.transpose(inner_x.reshape(token_rows, tensor_count, x_width), (1, 0, 2))
     x_recv = lax.all_to_all(x_send, TENSOR, 0, 0, tiled=True)

time: 182 us -> 181 us (level)
  the two profiles are of different devices: /device:TPU:65 before, /device:TPU:89 now
where the time goes in v10:
time: 181 us; the launch traced here: 180 us
  waiting for transfers between devices  85.6 us (47%)
  starting transfers between devices  28.7 us (16%)
  local copies, waits for them, and re-layouts  27.4 us (15%)
  other arithmetic  25 us (14%)
  matrix products  11.7 us (6%)
    all_to_all x1, waiting for transfers between devices, local(): lax.all_to_all(mixed_y, TENSOR, split_axis=0, concat_axis=1, tiled=True)  42.6 us
    all_to_all x1, waiting for transfers between devices, local(): x_recv = lax.all_to_all(x_send, TENSOR, 0, 0, tiled=True)  23.3 us
    all_to_all x1, waiting for transfers between devices, local(): small_recv = lax.all_to_all(small_send, TENSOR, 0, 0, tiled=True)  19.7 us
    all_to_all x1, starting transfers between devices, local(): small_recv = lax.all_to_all(small_send, TENSOR, 0, 0, tiled=True)  12.6 us
    convert_element_type x4, other arithmetic, local(): weights = jnp.where(causal[None], scores[None] * decayed * step_cols[:, N...  9.55 us
    all_to_all x1, starting transfers between devices, local(): lax.all_to_all(mixed_y, TENSOR, split_axis=0, concat_axis=1, tiled=True)  6.85 us
    all_to_all x1, starting transfers between devices, local(): x_recv = lax.all_to_all(x_send, TENSOR, 0, 0, tiled=True)  6.74 us
    dot_general x4, matrix products, local(): jnp.einsum('hts,hps->htp', weights, values_t[:, :, :row_stop], preferred_...  5.98 us
  transfers between devices with their start and end apart: 4, of which 3 were waited for; matrix products, arithmetic and copies ran while one was open for 20% of the time, Pallas kernels for 0%

profile of v10, /device:TPU:89, one launch (start us, length us, event | category | flops | bytes accessed | tf_op | source)
XLA Modules:
  0.0 179.7 jit_solution(12447699119774553066)
XLA Ops:
  0.6 1.1 reshape.216
  1.7 1.1 stack_reshape.3
  2.9 0.8 copy.118
  4.2 0.7 maximum_bitcast_fusion
  4.9 0.5 copy.117
  5.5 0.9 pad_maximum_fusion.3
  6.4 12.6 %all-to-all-start = ((bf16[16,132,128]{2,1,0:T(8,128)(2,1)}), bf16[16,132,128]{2,1,0:T(8,128)(2,1)S(1)}, u32[]{:S(2)}, u32[]{:S(2)}) async-start(bf16[16,132,128]{2,1,0:T(8,128)(2,1)} %pad_maximum_fusion.3), calls=%async_computation | async-start | bytes 1114112 | tf_op jit(solution)/shard_map/all_to_all | solution.py:76
  19.0 1.1 copy.146
  20.1 0.5 convert_element_type.104
  20.7 0.7 constant_dynamic-slice_fusion.1
  21.4 0.8 fusion.57
  22.2 0.6 gather_fusion
  22.9 0.7 constant_dynamic-slice_fusion.3
  23.6 0.6 pad_clamp_fusion
  24.2 0.5 compare_and_fusion
  24.8 0.6 slice_convert_fusion.5
  25.4 0.8 iota_compare_fusion.2
  26.1 0.9 iota_compare_fusion.1
  27.2 19.7 %all-to-all-done = bf16[16,132,128]{2,1,0:T(8,128)(2,1)S(1)} async-done(((bf16[16,132,128]{2,1,0:T(8,128)(2,1)}), bf16[16,132,128]{2,1,0:T(8,128)(2,1)S(1)}, u32[]{:S(2)}, u32[]{:S(2)}) %all-to-all-start) | async-done | bytes 540704 | tf_op jit(solution)/shard_map/all_to_all | solution.py:76
  47.0 6.7 %all-to-all-start.1 = ((bf16[16,64,512]{2,1,0:T(8,128)(2,1)}), bf16[16,64,512]{2,1,0:T(8,128)(2,1)S(1)}, u32[]{:S(2)}, u32[]{:S(2)}) async-start(bf16[16,64,512]{2,1,0:T(8,128)(2,1)} %bitcast.94), calls=%async_computation.1 | async-start | bytes 2097152 | tf_op jit(solution)/shard_map/all_to_all | solution.py:82
  53.7 0.3 reshape.232
  54.3 2.3 %reduce-window.6 = f32[8,8,128]{2,1,0:T(8,128)S(1)} reduce-window(f32[8,8,128]{2,1,0:T(8,128)S(1)} %copy.125, f32[]{:T(128)} %constant.52.clone.1), window={size=1x1x128 pad=0_0x0_0x127_0}, to_apply=%region_0.1 | reduce-window | flops 1040384 | bytes 65540 | tf_op jit(solution)/shard_map/reduce-window
  57.2 0.7 multiply_convert_fusion.6
  58.2 0.3 copy.122
  58.5 2.5 %collective-permute-start = (bf16[2,1024,128]{2,1,0:T(8,128)(2,1)S(1)}, bf16[2,1024,128]{2,1,0:T(8,128)(2,1)S(1)}, u32[]{:S(2)}, u32[]{:S(2)}) collective-permute-start(bf16[2,1024,128]{2,1,0:T(8,128)(2,1)S(1)} %bitcast.110), channel_id=1, source_target_pairs={{0,1},{1,0},{2,3},{3,2},{4,5},{5,4},{6,7},{7,6},{8,9},{9,8},{10,11... | collective-permute-start | bytes 1572872 | tf_op jit(solution)/shard_map/ppermute | solution.py:111
  61.2 0.7 exponential_multiply_fusion
  61.9 0.6 slice.212
  62.5 0.6 slice.213
  63.1 0.6 slice.207
  63.7 0.6 slice.206
  64.3 0.6 slice.197
  64.9 0.6 fusion.56
  65.5 0.6 fusion.54
  66.2 0.9 gather_fusion.1
  67.1 1.0 copy_bitcast_fusion
  68.1 0.3 fusion.30
  68.5 3.6 %select_convert_fusion = bf16[8,256,1024]{2,1,0:T(8,128)(2,1)} fusion(f32[8,1024]{1,0:T(8,128)S(1)} %get-tuple-element.9, f32[8,1024]{1,0:T(8,128)S(1)} %bitcast.117, f32[8,256]{1,0:T(8,128)S(1)} %copy-done.15, f32[256,1024]{1,0:T(8,128)S(1)} %fusion.30, pred[256,1024]{1,0:T(8,128)(4,1)S(1)} %iota_compare_fusion), kind=kLoop, calls=%fused_computation.3 | loop fusion | flops 12582912 | bytes 5578752 | tf_op jit(solution)/shard_map/convert_element_type | solution.py:146
  72.2 0.3 fusion.32
  72.6 3.0 %select_convert_fusion.1 = bf16[8,256,768]{2,1,0:T(8,128)(2,1)} fusion(f32[8,768]{1,0:T(8,128)S(1)} %copy-done.9, f32[8,768]{1,0:T(8,128)S(1)} %copy-done.8, f32[8,256]{1,0:T(8,128)S(1)} %copy-done.14, f32[256,768]{1,0:T(8,128)S(1)} %fusion.32, pred[256,768]{1,0:T(8,128)(4,1)S(1)} %copy-done.6), kind=kLoop, calls=%fused_computation.4 | loop fusion | flops 9437184 | bytes 4186112 | tf_op jit(solution)/shard_map/convert_element_type | solution.py:146
  75.9 2.3 %select_convert_fusion.2 = bf16[8,256,512]{2,1,0:T(8,128)(2,1)} fusion(f32[8,512]{1,0:T(8,128)S(1)} %copy-done.10, f32[8,512]{1,0:T(8,128)S(1)} %copy-done.11, f32[8,256]{1,0:T(8,128)S(1)} %copy-done.13, f32[256,512]{1,0:T(8,128)S(1)} %fusion.34, pred[256,512]{1,0:T(8,128)(4,1)S(1)} %copy-done.7), kind=kLoop, calls=%fused_computation.8 | loop fusion | flops 6291456 | bytes 2793472 | tf_op jit(solution)/shard_map/convert_element_type | solution.py:146
  78.4 0.6 select_convert_fusion.3
  79.0 23.3 %all-to-all-done.1 = bf16[16,64,512]{2,1,0:T(8,128)(2,1)S(1)} async-done(((bf16[16,64,512]{2,1,0:T(8,128)(2,1)}), bf16[16,64,512]{2,1,0:T(8,128)(2,1)S(1)}, u32[]{:S(2)}, u32[]{:S(2)}) %all-to-all-start.1) | async-done | bytes 1048608 | tf_op jit(solution)/shard_map/all_to_all | solution.py:82
  102.3 0.3 bitcast_convert_fusion
  102.7 0.6 copy-done.3
  103.3 2.2 %multiply_convert_fusion.3 = bf16[1024,512]{1,0:T(8,128)(2,1)} fusion(f32[1024,512]{1,0:T(8,128)S(1)} %bitcast_convert_fusion, f32[3,512]{1,0:T(4,128)S(1)} %convert_element_type.105, f32[512]{0:T(512)S(1)} %bitcast.124, f32[512]{0:T(512)S(1)} %bitcast.125, f32[512]{0:T(512)S(1)} %bitcast.123, f32[512]{0:T(512)S(1)} %bitcast.122, f32[512]{0:T(512)S(1)} %copy-done.20), kind=kLoop, calls=%fused_computation.29 | loop fusion | flops 8388608 | bytes 3162112 | tf_op jit(solution)/shard_map/convert_element_type | solution.py:30
  105.5 1.5 copy.127
  107.0 3.7 %fusion.58 = f32[8,256,64]{1,2,0:T(8,128)S(1)} fusion(bf16[8,256,1024]{2,1,0:T(8,128)(2,1)} %select_convert_fusion, bf16[8,64,1024]{2,1,0:T(8,128)(2,1)S(1)} %bitcast.98), kind=kOutput, calls=%fused_computation.127 | convolution fusion | flops 268435456 | bytes 5767168 | tf_op jit(solution)/shard_map/hts,hps->htp/dot_general | solution.py:149
  110.8 1.1 fusion.26
  111.8 0.5 copy-done.2
  112.3 0.8 fusion.28
  113.1 0.4 fusion.36
  113.6 1.3 fusion.15
  114.9 2.3 %reshape.255 = bf16[16,64,512]{1,0,2:T(8,128)(2,1)} reshape(bf16[1024,8,64]{0,2,1:T(8,128)(2,1)S(1)} %fusion.15) | data formatting | bytes 2097152 | tf_op jit(solution)/shard_map/all_to_all | solution.py:176
  117.2 3.3 %copy.131 = bf16[16,64,512]{2,1,0:T(8,128)(2,1)} copy(bf16[16,64,512]{1,0,2:T(8,128)(2,1)} %reshape.255) | data formatting | bytes 2097152 | tf_op jit(solution)/shard_map/all_to_all | solution.py:176
  120.5 6.8 %all-to-all-start.2 = ((bf16[16,64,512]{2,1,0:T(8,128)(2,1)}), bf16[16,64,512]{2,1,0:T(8,128)(2,1)S(1)}, u32[]{:S(2)}, u32[]{:S(2)}) async-start(bf16[16,64,512]{2,1,0:T(8,128)(2,1)} %copy.131), calls=%async_computation.2 | async-start | bytes 2097152 | tf_op jit(solution)/shard_map/all_to_all | solution.py:176
  127.4 1.3 slice.221
  128.7 1.3 slice.220
  130.0 3.3 %fusion.16 = f32[8,64,256]{2,1,0:T(8,128)} fusion(bf16[8,64,1024]{2,1,0:T(8,128)(2,1)S(1)} %bitcast.103, f32[1024,8]{0,1:T(8,128)S(1)} %copy-done.17, f32[1024,256]{1,0:T(8,128)S(1)} %slice_convert_fusion, f32[8,64,256]{2,1,0:T(8,128)} %param.28, f32[8]{0:T(128)S(1)} %exp.49), kind=kOutput, calls=%fused_computation.34 | convolution fusion | flops 272891904 | bytes 3178528 | tf_op jit(solution)/shard_map/hps,shn->hpn/dot_general | solution.py:171
  133.4 42.6 %all-to-all-done.2 = bf16[16,64,512]{2,1,0:T(8,128)(2,1)S(1)} async-done(((bf16[16,64,512]{2,1,0:T(8,128)(2,1)}), bf16[16,64,512]{2,1,0:T(8,128)(2,1)S(1)}, u32[]{:S(2)}, u32[]{:S(2)}) %all-to-all-start.2) | async-done | bytes 1048608 | tf_op jit(solution)/shard_map/all_to_all | solution.py:176
  176.0 0.3 convert_bitcast_fusion
  176.5 0.3 fusion.3
  176.9 0.3 mul.321
  177.2 1.2 copy.136
  178.4 1.3 multiply_convert_fusion.2
  (103 shorter events, 3.2 us)
Async XLA Ops:
  4.1 14.9 %copy-start.5 = (bf16[64,8192]{1,0:T(8,128)(2,1)S(1)}, bf16[64,8192]{1,0:T(8,128)(2,1)}, u32[]{:S(2)}) copy-start(bf16[64,8192]{1,0:T(8,128)(2,1)} %param.15) | copy-start | bytes 3145732
  5.5 14.7 %copy-start.25 = (bf16[3,512]{1,0:T(4,128)(2,1)S(1)}, bf16[3,512]{1,0:T(4,128)(2,1)}, u32[]{:S(2)}) copy-start(bf16[3,512]{1,0:T(4,128)(2,1)} %param.18) | copy-start | bytes 9220
  5.5 14.6 %copy-start.29 = (bf16[512]{0:T(512)(128)(2,1)S(1)}, bf16[512]{0:T(512)(128)(2,1)}, u32[]{:S(2)}) copy-start(bf16[512]{0:T(512)(128)(2,1)} %param.21) | copy-start | bytes 3076
  5.5 16.7 %copy-start = (s32[4]{0:T(128)S(1)}, s32[4]{0:T(128)}, u32[]{:S(2)}) copy-start(s32[4]{0:T(128)} %constant.58.clone) | copy-start | bytes 52
  6.4 18.4 %copy-start.19 = (bf16[4,512]{1,0:T(4,128)(2,1)S(1)}, bf16[4,512]{1,0:T(4,128)(2,1)}, u32[]{:S(2)}) copy-start(bf16[4,512]{1,0:T(4,128)(2,1)} %param.20) | copy-start | bytes 12292
  6.4 40.6 %all-to-all-start = ((bf16[16,132,128]{2,1,0:T(8,128)(2,1)}), bf16[16,132,128]{2,1,0:T(8,128)(2,1)S(1)}, u32[]{:S(2)}, u32[]{:S(2)}) async-start(bf16[16,132,128]{2,1,0:T(8,128)(2,1)} %pad_maximum_fusion.3), calls=%async_computation | async-start | bytes 1114112 | tf_op jit(solution)/shard_map/all_to_all | solution.py:76
  22.9 31.3 %copy-start.26 = (f32[8]{0:T(128)S(1)}, f32[8]{0:T(128)}, u32[]{:S(2)}) copy-start(f32[8]{0:T(128)} %param.24) | copy-start | bytes 100
  22.9 31.3 %copy-start.30 = (f32[8]{0:T(128)S(1)}, f32[8]{0:T(128)}, u32[]{:S(2)}) copy-start(f32[8]{0:T(128)} %param.25) | copy-start | bytes 100
  47.0 55.3 %all-to-all-start.1 = ((bf16[16,64,512]{2,1,0:T(8,128)(2,1)}), bf16[16,64,512]{2,1,0:T(8,128)(2,1)S(1)}, u32[]{:S(2)}, u32[]{:S(2)}) async-start(bf16[16,64,512]{2,1,0:T(8,128)(2,1)} %bitcast.94), calls=%async_computation.1 | async-start | bytes 2097152 | tf_op jit(solution)/shard_map/all_to_all | solution.py:82
  57.2 1.1 copy-start.4
  58.5 7.6 %collective-permute-start = (bf16[2,1024,128]{2,1,0:T(8,128)(2,1)S(1)}, bf16[2,1024,128]{2,1,0:T(8,128)(2,1)S(1)}, u32[]{:S(2)}, u32[]{:S(2)}) collective-permute-start(bf16[2,1024,128]{2,1,0:T(8,128)(2,1)S(1)} %bitcast.110), channel_id=1, source_target_pairs={{0,1},{1,0},{2,3},{3,2},{4,5},{5,4},{6,7},{7,6},{8,9},{9,8},{10,11... | collective-permute-start | bytes 1572872 | tf_op jit(solution)/shard_map/ppermute | solution.py:111
  61.2 3.1 %copy-start.27 = (f32[8]{0:T(128)}, f32[8]{0:T(128)S(1)}, u32[]{:S(2)}) copy-start(f32[8]{0:T(128)S(1)} %slice_reduce_fusion.1) | copy-start | bytes 100
  67.1 1.4 copy-start.15
  68.5 4.0 %copy-start.6 = (pred[256,768]{1,0:T(8,128)(4,1)S(1)}, pred[256,768]{1,0:T(8,128)(4,1)}, u32[]{:S(2)}) copy-start(pred[256,768]{1,0:T(8,128)(4,1)} %iota_compare_fusion.1) | copy-start | bytes 589828
  68.5 4.0 %copy-start.8 = (f32[8,768]{1,0:T(8,128)S(1)}, f32[8,768]{1,0:T(8,128)}, u32[]{:S(2)}) copy-start(f32[8,768]{1,0:T(8,128)} %slice.212) | copy-start | bytes 73732
  68.5 4.0 %copy-start.9 = (f32[8,768]{1,0:T(8,128)S(1)}, f32[8,768]{1,0:T(8,128)}, u32[]{:S(2)}) copy-start(f32[8,768]{1,0:T(8,128)} %slice.213) | copy-start | bytes 73732
  68.5 4.0 %copy-start.14 = (f32[8,256]{1,0:T(8,128)S(1)}, f32[8,256]{1,0:T(8,128)}, u32[]{:S(2)}) copy-start(f32[8,256]{1,0:T(8,128)} %get-tuple-element.14) | copy-start | bytes 24580
  72.5 3.3 %copy-start.7 = (pred[256,512]{1,0:T(8,128)(4,1)S(1)}, pred[256,512]{1,0:T(8,128)(4,1)}, u32[]{:S(2)}) copy-start(pred[256,512]{1,0:T(8,128)(4,1)} %iota_compare_fusion.2) | copy-start | bytes 393220
  72.5 3.3 %copy-start.10 = (f32[8,512]{1,0:T(8,128)S(1)}, f32[8,512]{1,0:T(8,128)}, u32[]{:S(2)}) copy-start(f32[8,512]{1,0:T(8,128)} %slice.207) | copy-start | bytes 49156
  72.5 3.3 %copy-start.11 = (f32[8,512]{1,0:T(8,128)S(1)}, f32[8,512]{1,0:T(8,128)}, u32[]{:S(2)}) copy-start(f32[8,512]{1,0:T(8,128)} %slice.206) | copy-start | bytes 49156
  72.5 3.3 %copy-start.13 = (f32[8,256]{1,0:T(8,128)S(1)}, f32[8,256]{1,0:T(8,128)}, u32[]{:S(2)}) copy-start(f32[8,256]{1,0:T(8,128)} %get-tuple-element.15) | copy-start | bytes 24580
  75.6 2.8 %copy-start.12 = (f32[8,256]{1,0:T(8,128)S(1)}, f32[8,256]{1,0:T(8,128)}, u32[]{:S(2)}) copy-start(f32[8,256]{1,0:T(8,128)} %slice.197) | copy-start | bytes 24580
  78.4 24.9 %copy-start.20 = (f32[512]{0:T(512)S(1)}, f32[512]{0:T(512)}, u32[]{:S(2)}) copy-start(f32[512]{0:T(512)} %convert_element_type.104) | copy-start | bytes 6148
  78.4 24.9 %copy-start.21 = (f32[1,512]{1,0:T(1,128)S(1)}, f32[1,512]{1,0:T(1,128)}, u32[]{:S(2)}) copy-start(f32[1,512]{1,0:T(1,128)} %get-tuple-element.22) | copy-start | bytes 6148
  78.4 24.9 %copy-start.22 = (f32[1,512]{1,0:T(1,128)S(1)}, f32[1,512]{1,0:T(1,128)}, u32[]{:S(2)}) copy-start(f32[1,512]{1,0:T(1,128)} %get-tuple-element.23) | copy-start | bytes 6148
  78.4 24.9 %copy-start.23 = (f32[1,512]{1,0:T(1,128)S(1)}, f32[1,512]{1,0:T(1,128)}, u32[]{:S(2)}) copy-start(f32[1,512]{1,0:T(1,128)} %get-tuple-element.24) | copy-start | bytes 6148
  78.4 24.9 %copy-start.24 = (f32[1,512]{1,0:T(1,128)S(1)}, f32[1,512]{1,0:T(1,128)}, u32[]{:S(2)}) copy-start(f32[1,512]{1,0:T(1,128)} %get-tuple-element.25) | copy-start | bytes 6148
  102.3 1.0 copy-start.3
  107.0 3.7 %copy-start.1 = (bf16[8,256,768]{2,1,0:T(8,128)(2,1)S(1)}, bf16[8,256,768]{2,1,0:T(8,128)(2,1)}, u32[]{:S(2)}) copy-start(bf16[8,256,768]{2,1,0:T(8,128)(2,1)} %select_convert_fusion.1) | copy-start | bytes 9437188
  110.7 1.6 copy-start.2
  112.3 1.2 copy-start.16
  112.3 1.2 copy-start.31
  112.3 1.2 copy-start.32
  117.2 10.2 %copy-start.18 = (bf16[8192]{0:T(1024)(128)(2,1)S(1)}, bf16[8192]{0:T(1024)(128)(2,1)}, u32[]{:S(2)}) copy-start(bf16[8192]{0:T(1024)(128)(2,1)} %param.27) | copy-start | bytes 49156
  117.2 10.2 %copy-start.28 = (f32[8]{0:T(128)S(1)}, f32[8]{0:T(128)}, u32[]{:S(2)}) copy-start(f32[8]{0:T(128)} %copy-done.27) | copy-start | bytes 100
  120.5 9.5 %copy-start.17 = (f32[1024,8]{0,1:T(8,128)S(1)}, f32[1024,8]{0,1:T(8,128)}, u32[]{:S(2)}) copy-start(f32[1024,8]{0,1:T(8,128)} %get-tuple-element.8) | copy-start | bytes 98308
  120.5 55.4 %all-to-all-start.2 = ((bf16[16,64,512]{2,1,0:T(8,128)(2,1)}), bf16[16,64,512]{2,1,0:T(8,128)(2,1)S(1)}, u32[]{:S(2)}, u32[]{:S(2)}) async-start(bf16[16,64,512]{2,1,0:T(8,128)(2,1)} %copy.131), calls=%async_computation.2 | async-start | bytes 2097152 | tf_op jit(solution)/shard_map/all_to_all | solution.py:176

commit v11 on v10

--- a/solution.py
+++ b/solution.py
@@ -64,10 +64,11 @@
     bc_width = inner_bc.shape[1] // tensor_count
     length = tensor_count * token_rows
 
-    quarters = inner_bc.reshape(token_rows, GROUPS, 2, group_size // 2, bc_width)
-    across_quarters = jnp.flip(quarters, axis=2)
-    bc_rows = jnp.transpose(
-        jnp.stack([quarters, across_quarters], axis=4), (1, 2, 3, 0, 4, 5)
+    quarters = jnp.transpose(
+        inner_bc.reshape(token_rows, GROUPS, 2, group_size // 2, bc_width), (1, 3, 0, 2, 4)
+    )
+    bc_rows = jnp.broadcast_to(
+        quarters[:, None], (GROUPS, 2) + quarters.shape[1:]
     ).reshape(tensor_count, token_rows * 2, bc_width)
     step_rows = jnp.transpose(
         step_raw.reshape(token_rows, tensor_count, heads_here), (1, 0, 2)
@@ -83,8 +84,10 @@
     head_x = x_recv.reshape(length, x_width)
 
     group_rank = lax.axis_index("tj")
-    column_start = device_rank * bc_width
-    across_start = (device_rank ^ 2) * bc_width
+    high_bit = (group_rank // 2) % 2
+    low_bit = group_rank % 2
+    column_start = (device_rank - 2 * high_bit) * bc_width
+    across_start = (device_rank - 2 * high_bit + 2) * bc_width
     pair_state_bc = jnp.concatenate(
         [
             lax.dynamic_slice_in_dim(conv_state_bc, column_start, bc_width, 1),
@@ -111,7 +114,7 @@
     beside = lax.ppermute(pair, "tj", [(source, source ^ 1) for source in range(group_size)])
     stacked = jnp.concatenate([pair, beside], axis=0)
     slot_of = jnp.array([0, 2, 1, 3], dtype=jnp.int32)
-    order = slot_of[jnp.arange(group_size, dtype=jnp.int32) ^ group_rank]
+    order = slot_of[jnp.arange(group_size, dtype=jnp.int32) ^ low_bit]
     ordered = jnp.take(stacked, order, axis=0)
     mixed_bc = jnp.transpose(ordered, (1, 0, 2)).reshape(length, group_size * bc_width)
     input_map = mixed_bc[:, :STATE]
@@ -176,7 +179,9 @@
     token_y = lax.all_to_all(mixed_y, TENSOR, split_axis=0, concat_axis=1, tiled=True)
     normed = group_norm(token_y, norm_weight)
     tail_x = head_x[length - CONV_K + 1 :]
-    tail_bc = head_bc_pair[length - CONV_K + 1 :, :bc_width]
+    tail_bc = lax.dynamic_slice_in_dim(
+        head_bc_pair[length - CONV_K + 1 :], high_bit * bc_width, bc_width, 1
+    )
     return (normed, final_state, tail_x, tail_bc)
 
 

time: 181 us -> 179 us (0.989)
  the two profiles are of different devices: /device:TPU:89 before, /device:TPU:65 now
where the time goes in v11:
time: 179 us; the launch traced here: 178 us
  waiting for transfers between devices  85.6 us (48%)
  starting transfers between devices  28.7 us (16%)
  local copies, waits for them, and re-layouts  26.2 us (15%)
  other arithmetic  24.2 us (14%)
  matrix products  11.7 us (7%)
    all_to_all x1, waiting for transfers between devices, local(): lax.all_to_all(mixed_y, TENSOR, split_axis=0, concat_axis=1, tiled=True)  42.6 us
    all_to_all x1, waiting for transfers between devices, local(): x_recv = lax.all_to_all(x_send, TENSOR, 0, 0, tiled=True)  23.3 us
    all_to_all x1, waiting for transfers between devices, local(): small_recv = lax.all_to_all(small_send, TENSOR, 0, 0, tiled=True)  19.7 us
    all_to_all x1, starting transfers between devices, local(): small_recv = lax.all_to_all(small_send, TENSOR, 0, 0, tiled=True)  12.6 us
    convert_element_type x4, other arithmetic, local(): weights = jnp.where(causal[None], scores[None] * decayed * step_cols[:, N...  9.55 us
    all_to_all x1, starting transfers between devices, local(): lax.all_to_all(mixed_y, TENSOR, split_axis=0, concat_axis=1, tiled=True)  6.85 us
    all_to_all x1, starting transfers between devices, local(): x_recv = lax.all_to_all(x_send, TENSOR, 0, 0, tiled=True)  6.74 us
    dot_general x4, matrix products, local(): jnp.einsum('hts,hps->htp', weights, values_t[:, :, :row_stop], preferred_...  5.98 us
  transfers between devices with their start and end apart: 4, of which 3 were waited for; matrix products, arithmetic and copies ran while one was open for 21% of the time, Pallas kernels for 0%

profile of v11, /device:TPU:65, one launch (start us, length us, event | category | flops | bytes accessed | tf_op | source)
XLA Modules:
  0.0 177.7 jit_solution(3459541729250972658)
XLA Ops:
  0.6 0.8 copy.118
  1.7 1.2 reshape.217
  3.1 0.4 broadcast_in_dim.134
  3.5 0.9 pad_maximum_fusion.3
  4.4 12.6 %all-to-all-start = ((bf16[16,132,128]{2,1,0:T(8,128)(2,1)}), bf16[16,132,128]{2,1,0:T(8,128)(2,1)S(1)}, u32[]{:S(2)}, u32[]{:S(2)}) async-start(bf16[16,132,128]{2,1,0:T(8,128)(2,1)} %pad_maximum_fusion.3), calls=%async_computation | async-start | bytes 1114112 | tf_op jit(solution)/shard_map/all_to_all | solution.py:77
  17.0 1.1 copy.146
  18.1 0.5 convert_element_type.104
  18.7 0.7 constant_dynamic-slice_fusion.2
  19.4 0.8 fusion.57
  20.2 0.6 gather_fusion
  20.9 0.7 constant_dynamic-slice_fusion.4
  21.6 0.6 pad_clamp_fusion
  22.3 0.5 compare_and_fusion
  22.8 0.6 slice_convert_fusion.5
  23.4 0.8 iota_compare_fusion.2
  24.2 0.9 iota_compare_fusion.1
  25.3 19.7 %all-to-all-done = bf16[16,132,128]{2,1,0:T(8,128)(2,1)S(1)} async-done(((bf16[16,132,128]{2,1,0:T(8,128)(2,1)}), bf16[16,132,128]{2,1,0:T(8,128)(2,1)S(1)}, u32[]{:S(2)}, u32[]{:S(2)}) %all-to-all-start) | async-done | bytes 540704 | tf_op jit(solution)/shard_map/all_to_all | solution.py:77
  45.0 6.7 %all-to-all-start.1 = ((bf16[16,64,512]{2,1,0:T(8,128)(2,1)}), bf16[16,64,512]{2,1,0:T(8,128)(2,1)S(1)}, u32[]{:S(2)}, u32[]{:S(2)}) async-start(bf16[16,64,512]{2,1,0:T(8,128)(2,1)} %bitcast.91), calls=%async_computation.1 | async-start | bytes 2097152 | tf_op jit(solution)/shard_map/all_to_all | solution.py:83
  51.8 0.3 reshape.233
  52.4 2.3 %reduce-window.6 = f32[8,8,128]{2,1,0:T(8,128)S(1)} reduce-window(f32[8,8,128]{2,1,0:T(8,128)S(1)} %copy.125, f32[]{:T(128)} %constant.78.clone.1), window={size=1x1x128 pad=0_0x0_0x127_0}, to_apply=%region_0.1 | reduce-window | flops 1040384 | bytes 65540 | tf_op jit(solution)/shard_map/reduce-window
  55.3 0.7 multiply_convert_fusion.6
  56.3 0.3 copy.122
  56.6 2.5 %collective-permute-start = (bf16[2,1024,128]{2,1,0:T(8,128)(2,1)S(1)}, bf16[2,1024,128]{2,1,0:T(8,128)(2,1)S(1)}, u32[]{:S(2)}, u32[]{:S(2)}) collective-permute-start(bf16[2,1024,128]{2,1,0:T(8,128)(2,1)S(1)} %bitcast.107), channel_id=1, source_target_pairs={{0,1},{1,0},{2,3},{3,2},{4,5},{5,4},{6,7},{7,6},{8,9},{9,8},{10,11... | collective-permute-start | bytes 1572872 | tf_op jit(solution)/shard_map/ppermute | solution.py:114
  59.2 0.7 exponential_multiply_fusion
  59.9 0.6 slice.212
  60.5 0.6 slice.213
  61.1 0.6 slice.207
  61.7 0.6 slice.206
  62.3 0.6 slice.197
  62.9 0.6 fusion.56
  63.5 0.6 fusion.54
  64.3 0.9 gather_fusion.1
  65.1 1.0 copy_bitcast_fusion
  66.2 0.3 fusion.30
  66.6 3.6 %select_convert_fusion = bf16[8,256,1024]{2,1,0:T(8,128)(2,1)} fusion(f32[8,1024]{1,0:T(8,128)S(1)} %get-tuple-element.9, f32[8,1024]{1,0:T(8,128)S(1)} %bitcast.115, f32[8,256]{1,0:T(8,128)S(1)} %copy-done.15, f32[256,1024]{1,0:T(8,128)S(1)} %fusion.30, pred[256,1024]{1,0:T(8,128)(4,1)S(1)} %iota_compare_fusion), kind=kLoop, calls=%fused_computation.3 | loop fusion | flops 12582912 | bytes 5578752 | tf_op jit(solution)/shard_map/convert_element_type | solution.py:149
  70.2 0.3 fusion.32
  70.6 3.0 %select_convert_fusion.1 = bf16[8,256,768]{2,1,0:T(8,128)(2,1)} fusion(f32[8,768]{1,0:T(8,128)S(1)} %copy-done.9, f32[8,768]{1,0:T(8,128)S(1)} %copy-done.8, f32[8,256]{1,0:T(8,128)S(1)} %copy-done.14, f32[256,768]{1,0:T(8,128)S(1)} %fusion.32, pred[256,768]{1,0:T(8,128)(4,1)S(1)} %copy-done.6), kind=kLoop, calls=%fused_computation.4 | loop fusion | flops 9437184 | bytes 4186112 | tf_op jit(solution)/shard_map/convert_element_type | solution.py:149
  73.6 0.2 fusion.34
  73.9 2.3 %select_convert_fusion.2 = bf16[8,256,512]{2,1,0:T(8,128)(2,1)} fusion(f32[8,512]{1,0:T(8,128)S(1)} %copy-done.10, f32[8,512]{1,0:T(8,128)S(1)} %copy-done.11, f32[8,256]{1,0:T(8,128)S(1)} %copy-done.13, f32[256,512]{1,0:T(8,128)S(1)} %fusion.34, pred[256,512]{1,0:T(8,128)(4,1)S(1)} %copy-done.7), kind=kLoop, calls=%fused_computation.8 | loop fusion | flops 6291456 | bytes 2793472 | tf_op jit(solution)/shard_map/convert_element_type | solution.py:149
  76.5 0.6 select_convert_fusion.3
  77.1 23.3 %all-to-all-done.1 = bf16[16,64,512]{2,1,0:T(8,128)(2,1)S(1)} async-done(((bf16[16,64,512]{2,1,0:T(8,128)(2,1)}), bf16[16,64,512]{2,1,0:T(8,128)(2,1)S(1)}, u32[]{:S(2)}, u32[]{:S(2)}) %all-to-all-start.1) | async-done | bytes 1048608 | tf_op jit(solution)/shard_map/all_to_all | solution.py:83
  100.3 0.3 bitcast_convert_fusion
  100.7 0.6 copy-done.3
  101.4 2.2 %multiply_convert_fusion.3 = bf16[1024,512]{1,0:T(8,128)(2,1)} fusion(f32[1024,512]{1,0:T(8,128)S(1)} %bitcast_convert_fusion, f32[3,512]{1,0:T(4,128)S(1)} %convert_element_type.105, f32[512]{0:T(512)S(1)} %bitcast.122, f32[512]{0:T(512)S(1)} %bitcast.123, f32[512]{0:T(512)S(1)} %bitcast.121, f32[512]{0:T(512)S(1)} %bitcast.120, f32[512]{0:T(512)S(1)} %copy-done.20), kind=kLoop, calls=%fused_computation.29 | loop fusion | flops 8388608 | bytes 3162112 | tf_op jit(solution)/shard_map/convert_element_type | solution.py:30
  103.5 1.5 copy.127
  105.0 3.7 %fusion.58 = f32[8,256,64]{1,2,0:T(8,128)S(1)} fusion(bf16[8,256,1024]{2,1,0:T(8,128)(2,1)} %select_convert_fusion, bf16[8,64,1024]{2,1,0:T(8,128)(2,1)S(1)} %bitcast.95), kind=kOutput, calls=%fused_computation.126 | convolution fusion | flops 268435456 | bytes 5767168 | tf_op jit(solution)/shard_map/hts,hps->htp/dot_general | solution.py:152
  108.8 1.1 fusion.26
  109.9 0.5 copy-done.2
  110.4 0.8 fusion.28
  111.1 0.4 fusion.36
  111.6 1.3 fusion.15
  112.9 2.3 %reshape.256 = bf16[16,64,512]{1,0,2:T(8,128)(2,1)} reshape(bf16[1024,8,64]{0,2,1:T(8,128)(2,1)S(1)} %fusion.15) | data formatting | bytes 2097152 | tf_op jit(solution)/shard_map/all_to_all | solution.py:179
  115.2 3.3 %copy.131 = bf16[16,64,512]{2,1,0:T(8,128)(2,1)} copy(bf16[16,64,512]{1,0,2:T(8,128)(2,1)} %reshape.256) | data formatting | bytes 2097152 | tf_op jit(solution)/shard_map/all_to_all | solution.py:179
  118.6 6.8 %all-to-all-start.2 = ((bf16[16,64,512]{2,1,0:T(8,128)(2,1)}), bf16[16,64,512]{2,1,0:T(8,128)(2,1)S(1)}, u32[]{:S(2)}, u32[]{:S(2)}) async-start(bf16[16,64,512]{2,1,0:T(8,128)(2,1)} %copy.131), calls=%async_computation.2 | async-start | bytes 2097152 | tf_op jit(solution)/shard_map/all_to_all | solution.py:179
  125.5 0.7 slice.221
  126.2 0.6 constant_dynamic-slice_fusion
  126.8 1.3 slice.220
  128.1 3.3 %fusion.16 = f32[8,64,256]{2,1,0:T(8,128)} fusion(bf16[8,64,1024]{2,1,0:T(8,128)(2,1)S(1)} %bitcast.100, f32[1024,8]{0,1:T(8,128)S(1)} %copy-done.17, f32[1024,256]{1,0:T(8,128)S(1)} %slice_convert_fusion, f32[8,64,256]{2,1,0:T(8,128)} %param.28, f32[8]{0:T(128)S(1)} %exp.49), kind=kOutput, calls=%fused_computation.34 | convolution fusion | flops 272891904 | bytes 3178528 | tf_op jit(solution)/shard_map/hps,shn->hpn/dot_general | solution.py:174
  131.4 42.6 %all-to-all-done.2 = bf16[16,64,512]{2,1,0:T(8,128)(2,1)S(1)} async-done(((bf16[16,64,512]{2,1,0:T(8,128)(2,1)}), bf16[16,64,512]{2,1,0:T(8,128)(2,1)S(1)}, u32[]{:S(2)}, u32[]{:S(2)}) %all-to-all-start.2) | async-done | bytes 1048608 | tf_op jit(solution)/shard_map/all_to_all | solution.py:179
  174.0 0.3 convert_bitcast_fusion
  174.5 0.3 fusion.3
  174.9 0.3 mul.329
  175.3 1.2 copy.136
  176.5 1.3 multiply_convert_fusion.2
  (102 shorter events, 2.9 us)
Async XLA Ops:
  1.7 15.3 %copy-start.5 = (bf16[64,8192]{1,0:T(8,128)(2,1)S(1)}, bf16[64,8192]{1,0:T(8,128)(2,1)}, u32[]{:S(2)}) copy-start(bf16[64,8192]{1,0:T(8,128)(2,1)} %param.15) | copy-start | bytes 3145732
  3.5 14.6 %copy-start.25 = (bf16[3,512]{1,0:T(4,128)(2,1)S(1)}, bf16[3,512]{1,0:T(4,128)(2,1)}, u32[]{:S(2)}) copy-start(bf16[3,512]{1,0:T(4,128)(2,1)} %param.18) | copy-start | bytes 9220
  3.5 14.6 %copy-start.29 = (bf16[512]{0:T(512)(128)(2,1)S(1)}, bf16[512]{0:T(512)(128)(2,1)}, u32[]{:S(2)}) copy-start(bf16[512]{0:T(512)(128)(2,1)} %param.21) | copy-start | bytes 3076
  3.5 16.7 %copy-start = (s32[4]{0:T(128)S(1)}, s32[4]{0:T(128)}, u32[]{:S(2)}) copy-start(s32[4]{0:T(128)} %constant.84.clone) | copy-start | bytes 52
  4.4 18.4 %copy-start.19 = (bf16[4,512]{1,0:T(4,128)(2,1)S(1)}, bf16[4,512]{1,0:T(4,128)(2,1)}, u32[]{:S(2)}) copy-start(bf16[4,512]{1,0:T(4,128)(2,1)} %param.20) | copy-start | bytes 12292
  4.4 40.6 %all-to-all-start = ((bf16[16,132,128]{2,1,0:T(8,128)(2,1)}), bf16[16,132,128]{2,1,0:T(8,128)(2,1)S(1)}, u32[]{:S(2)}, u32[]{:S(2)}) async-start(bf16[16,132,128]{2,1,0:T(8,128)(2,1)} %pad_maximum_fusion.3), calls=%async_computation | async-start | bytes 1114112 | tf_op jit(solution)/shard_map/all_to_all | solution.py:77
  20.9 31.3 %copy-start.26 = (f32[8]{0:T(128)S(1)}, f32[8]{0:T(128)}, u32[]{:S(2)}) copy-start(f32[8]{0:T(128)} %param.24) | copy-start | bytes 100
  20.9 31.3 %copy-start.30 = (f32[8]{0:T(128)S(1)}, f32[8]{0:T(128)}, u32[]{:S(2)}) copy-start(f32[8]{0:T(128)} %param.25) | copy-start | bytes 100
  45.0 55.3 %all-to-all-start.1 = ((bf16[16,64,512]{2,1,0:T(8,128)(2,1)}), bf16[16,64,512]{2,1,0:T(8,128)(2,1)S(1)}, u32[]{:S(2)}, u32[]{:S(2)}) async-start(bf16[16,64,512]{2,1,0:T(8,128)(2,1)} %bitcast.91), calls=%async_computation.1 | async-start | bytes 2097152 | tf_op jit(solution)/shard_map/all_to_all | solution.py:83
  55.2 1.1 copy-start.4
  56.6 7.6 %collective-permute-start = (bf16[2,1024,128]{2,1,0:T(8,128)(2,1)S(1)}, bf16[2,1024,128]{2,1,0:T(8,128)(2,1)S(1)}, u32[]{:S(2)}, u32[]{:S(2)}) collective-permute-start(bf16[2,1024,128]{2,1,0:T(8,128)(2,1)S(1)} %bitcast.107), channel_id=1, source_target_pairs={{0,1},{1,0},{2,3},{3,2},{4,5},{5,4},{6,7},{7,6},{8,9},{9,8},{10,11... | collective-permute-start | bytes 1572872 | tf_op jit(solution)/shard_map/ppermute | solution.py:114
  59.2 3.1 %copy-start.27 = (f32[8]{0:T(128)}, f32[8]{0:T(128)S(1)}, u32[]{:S(2)}) copy-start(f32[8]{0:T(128)S(1)} %slice_reduce_fusion.1) | copy-start | bytes 100
  65.1 1.4 copy-start.15
  66.5 4.0 %copy-start.6 = (pred[256,768]{1,0:T(8,128)(4,1)S(1)}, pred[256,768]{1,0:T(8,128)(4,1)}, u32[]{:S(2)}) copy-start(pred[256,768]{1,0:T(8,128)(4,1)} %iota_compare_fusion.1) | copy-start | bytes 589828
  66.5 4.0 %copy-start.8 = (f32[8,768]{1,0:T(8,128)S(1)}, f32[8,768]{1,0:T(8,128)}, u32[]{:S(2)}) copy-start(f32[8,768]{1,0:T(8,128)} %slice.212) | copy-start | bytes 73732
  66.5 4.0 %copy-start.9 = (f32[8,768]{1,0:T(8,128)S(1)}, f32[8,768]{1,0:T(8,128)}, u32[]{:S(2)}) copy-start(f32[8,768]{1,0:T(8,128)} %slice.213) | copy-start | bytes 73732
  66.5 4.0 %copy-start.14 = (f32[8,256]{1,0:T(8,128)S(1)}, f32[8,256]{1,0:T(8,128)}, u32[]{:S(2)}) copy-start(f32[8,256]{1,0:T(8,128)} %get-tuple-element.14) | copy-start | bytes 24580
  70.5 3.3 %copy-start.7 = (pred[256,512]{1,0:T(8,128)(4,1)S(1)}, pred[256,512]{1,0:T(8,128)(4,1)}, u32[]{:S(2)}) copy-start(pred[256,512]{1,0:T(8,128)(4,1)} %iota_compare_fusion.2) | copy-start | bytes 393220
  70.6 3.3 %copy-start.10 = (f32[8,512]{1,0:T(8,128)S(1)}, f32[8,512]{1,0:T(8,128)}, u32[]{:S(2)}) copy-start(f32[8,512]{1,0:T(8,128)} %slice.207) | copy-start | bytes 49156
  70.6 3.3 %copy-start.11 = (f32[8,512]{1,0:T(8,128)S(1)}, f32[8,512]{1,0:T(8,128)}, u32[]{:S(2)}) copy-start(f32[8,512]{1,0:T(8,128)} %slice.206) | copy-start | bytes 49156
  70.6 3.3 %copy-start.13 = (f32[8,256]{1,0:T(8,128)S(1)}, f32[8,256]{1,0:T(8,128)}, u32[]{:S(2)}) copy-start(f32[8,256]{1,0:T(8,128)} %get-tuple-element.15) | copy-start | bytes 24580
  73.6 2.8 %copy-start.12 = (f32[8,256]{1,0:T(8,128)S(1)}, f32[8,256]{1,0:T(8,128)}, u32[]{:S(2)}) copy-start(f32[8,256]{1,0:T(8,128)} %slice.197) | copy-start | bytes 24580
  76.4 24.9 %copy-start.20 = (f32[512]{0:T(512)S(1)}, f32[512]{0:T(512)}, u32[]{:S(2)}) copy-start(f32[512]{0:T(512)} %convert_element_type.104) | copy-start | bytes 6148
  76.4 24.9 %copy-start.21 = (f32[1,512]{1,0:T(1,128)S(1)}, f32[1,512]{1,0:T(1,128)}, u32[]{:S(2)}) copy-start(f32[1,512]{1,0:T(1,128)} %get-tuple-element.22) | copy-start | bytes 6148
  76.4 24.9 %copy-start.22 = (f32[1,512]{1,0:T(1,128)S(1)}, f32[1,512]{1,0:T(1,128)}, u32[]{:S(2)}) copy-start(f32[1,512]{1,0:T(1,128)} %get-tuple-element.23) | copy-start | bytes 6148
  76.4 24.9 %copy-start.23 = (f32[1,512]{1,0:T(1,128)S(1)}, f32[1,512]{1,0:T(1,128)}, u32[]{:S(2)}) copy-start(f32[1,512]{1,0:T(1,128)} %get-tuple-element.24) | copy-start | bytes 6148
  76.4 24.9 %copy-start.24 = (f32[1,512]{1,0:T(1,128)S(1)}, f32[1,512]{1,0:T(1,128)}, u32[]{:S(2)}) copy-start(f32[1,512]{1,0:T(1,128)} %get-tuple-element.25) | copy-start | bytes 6148
  100.3 1.0 copy-start.3
  105.0 3.7 %copy-start.1 = (bf16[8,256,768]{2,1,0:T(8,128)(2,1)S(1)}, bf16[8,256,768]{2,1,0:T(8,128)(2,1)}, u32[]{:S(2)}) copy-start(bf16[8,256,768]{2,1,0:T(8,128)(2,1)} %select_convert_fusion.1) | copy-start | bytes 9437188
  108.8 1.6 copy-start.2
  110.4 1.2 copy-start.16
  110.4 1.2 copy-start.31
  110.4 1.2 copy-start.32
  115.2 10.2 %copy-start.18 = (bf16[8192]{0:T(1024)(128)(2,1)S(1)}, bf16[8192]{0:T(1024)(128)(2,1)}, u32[]{:S(2)}) copy-start(bf16[8192]{0:T(1024)(128)(2,1)} %param.27) | copy-start | bytes 49156
  115.2 10.2 %copy-start.28 = (f32[8]{0:T(128)S(1)}, f32[8]{0:T(128)}, u32[]{:S(2)}) copy-start(f32[8]{0:T(128)} %copy-done.27) | copy-start | bytes 100
  118.6 9.5 %copy-start.17 = (f32[1024,8]{0,1:T(8,128)S(1)}, f32[1024,8]{0,1:T(8,128)}, u32[]{:S(2)}) copy-start(f32[1024,8]{0,1:T(8,128)} %get-tuple-element.8) | copy-start | bytes 98308
  118.6 55.4 %all-to-all-start.2 = ((bf16[16,64,512]{2,1,0:T(8,128)(2,1)}), bf16[16,64,512]{2,1,0:T(8,128)(2,1)S(1)}, u32[]{:S(2)}, u32[]{:S(2)}) async-start(bf16[16,64,512]{2,1,0:T(8,128)(2,1)} %copy.131), calls=%async_computation.2 | async-start | bytes 2097152 | tf_op jit(solution)/shard_map/all_to_all | solution.py:179

commit v12 on v11

--- a/solution.py
+++ b/solution.py
@@ -129,7 +129,7 @@
     values = mixed_x.reshape(length, heads_here, HEAD_DIM)
     values_t = jnp.transpose(values, (1, 2, 0))
 
-    query_rows = min(256, length)
+    query_rows = min(128, length)
     pieces = []
     for row_start in range(0, length, query_rows):
         row_stop = row_start + query_rows

time: 179 us -> 180 us (level)
  the two profiles are of different devices: /device:TPU:65 before, /device:TPU:75 now
where the time goes in v12:
time: 180 us
  waiting for transfers between devices  75 us (42%)
  local copies, waits for them, and re-layouts  31.9 us (18%)
  other arithmetic  29.2 us (16%)
  starting transfers between devices  28.7 us (16%)
  matrix products  13.3 us (7%)
    all_to_all x1, waiting for transfers between devices, local(): lax.all_to_all(mixed_y, TENSOR, split_axis=0, concat_axis=1, tiled=True)  42.6 us
    all_to_all x1, waiting for transfers between devices, local(): small_recv = lax.all_to_all(small_send, TENSOR, 0, 0, tiled=True)  16.9 us
    all_to_all x1, waiting for transfers between devices, local(): x_recv = lax.all_to_all(x_send, TENSOR, 0, 0, tiled=True)  15.5 us
    all_to_all x1, starting transfers between devices, local(): small_recv = lax.all_to_all(small_send, TENSOR, 0, 0, tiled=True)  12.6 us
    convert_element_type x8, other arithmetic, local(): weights = jnp.where(causal[None], scores[None] * decayed * step_cols[:, N...  12.1 us
    all_to_all x1, starting transfers between devices, local(): lax.all_to_all(mixed_y, TENSOR, split_axis=0, concat_axis=1, tiled=True)  6.85 us
    all_to_all x1, starting transfers between devices, local(): x_recv = lax.all_to_all(x_send, TENSOR, 0, 0, tiled=True)  6.74 us
    dot_general x8, matrix products, local(): jnp.einsum('hts,hps->htp', weights, values_t[:, :, :row_stop], preferred_...  6.73 us
  transfers between devices with their start and end apart: 4, of which 3 were waited for; matrix products, arithmetic and copies ran while one was open for 26% of the time, Pallas kernels for 0%

profile of v12, /device:TPU:75, one launch (start us, length us, event | category | flops | bytes accessed | tf_op | source)
XLA Modules:
  0.0 179.6 jit_solution(15313925935287669948)
XLA Ops:
  0.6 0.8 copy.138
  1.7 1.2 reshape.285
  3.5 0.9 pad_maximum_fusion.3
  4.4 12.6 %all-to-all-start = ((bf16[16,132,128]{2,1,0:T(8,128)(2,1)}), bf16[16,132,128]{2,1,0:T(8,128)(2,1)S(1)}, u32[]{:S(2)}, u32[]{:S(2)}) async-start(bf16[16,132,128]{2,1,0:T(8,128)(2,1)} %pad_maximum_fusion.3), calls=%async_computation | async-start | bytes 1114112 | tf_op jit(solution)/shard_map/all_to_all | solution.py:77
  17.0 0.6 iota_compare_fusion.7
  17.7 1.1 copy.166
  19.9 0.7 constant_dynamic-slice_fusion.2
  20.6 0.7 constant_dynamic-slice_fusion.4
  21.3 0.8 fusion.70
  22.2 0.6 gather_fusion
  22.9 0.6 slice_convert_fusion.5
  23.5 0.7 iota_compare_fusion.6
  24.3 0.7 iota_compare_fusion.5
  25.0 0.7 iota_compare_fusion.4
  25.8 0.8 iota_compare_fusion.2
  26.6 0.8 iota_compare_fusion.1
  27.3 0.8 iota_compare_fusion
  28.1 16.9 %all-to-all-done = bf16[16,132,128]{2,1,0:T(8,128)(2,1)S(1)} async-done(((bf16[16,132,128]{2,1,0:T(8,128)(2,1)}), bf16[16,132,128]{2,1,0:T(8,128)(2,1)S(1)}, u32[]{:S(2)}, u32[]{:S(2)}) %all-to-all-start) | async-done | bytes 540704 | tf_op jit(solution)/shard_map/all_to_all | solution.py:77
  45.0 6.7 %all-to-all-start.1 = ((bf16[16,64,512]{2,1,0:T(8,128)(2,1)}), bf16[16,64,512]{2,1,0:T(8,128)(2,1)S(1)}, u32[]{:S(2)}, u32[]{:S(2)}) async-start(bf16[16,64,512]{2,1,0:T(8,128)(2,1)} %bitcast.99), calls=%async_computation.1 | async-start | bytes 2097152 | tf_op jit(solution)/shard_map/all_to_all | solution.py:83
  52.3 2.3 %reduce-window.6 = f32[8,8,128]{2,1,0:T(8,128)S(1)} reduce-window(f32[8,8,128]{2,1,0:T(8,128)S(1)} %copy.145, f32[]{:T(128)} %constant.82.clone.1), window={size=1x1x128 pad=0_0x0_0x127_0}, to_apply=%region_0.1 | reduce-window | flops 1040384 | bytes 65540 | tf_op jit(solution)/shard_map/reduce-window
  55.5 0.7 multiply_convert_fusion.6
  56.7 2.5 %collective-permute-start = (bf16[2,1024,128]{2,1,0:T(8,128)(2,1)S(1)}, bf16[2,1024,128]{2,1,0:T(8,128)(2,1)S(1)}, u32[]{:S(2)}, u32[]{:S(2)}) collective-permute-start(bf16[2,1024,128]{2,1,0:T(8,128)(2,1)S(1)} %bitcast.119), channel_id=1, source_target_pairs={{0,1},{1,0},{2,3},{3,2},{4,5},{5,4},{6,7},{7,6},{8,9},{9,8},{10,11... | collective-permute-start | bytes 1572872 | tf_op jit(solution)/shard_map/ppermute | solution.py:114
  59.2 0.7 exponential_multiply_fusion
  61.7 0.6 slice.317
  62.3 0.6 slice.316
  62.9 0.6 slice.323
  63.5 0.6 slice.322
  64.1 0.6 slice.329
  64.7 0.6 slice.328
  65.3 0.6 slice.335
  65.9 0.6 slice.334
  66.5 0.6 slice.341
  67.1 0.6 slice.340
  67.8 0.6 fusion.69
  68.4 0.6 fusion.67
  69.1 0.7 gather_fusion.1
  71.1 1.1 select_convert_fusion.6
  72.4 1.5 select_convert_fusion.5
  74.2 0.6 select_convert_fusion.4
  75.1 1.8 %select_convert_fusion.3 = bf16[8,128,640]{2,1,0:T(8,128)(2,1)} fusion(f32[8,640]{1,0:T(8,128)S(1)} %copy-done.20, f32[8,640]{1,0:T(8,128)S(1)} %copy-done.21, f32[8,128]{1,0:T(8,128)S(1)} %copy-done.35, f32[128,640]{1,0:T(8,128)S(1)} %fusion.37, pred[128,640]{1,0:T(8,128)(4,1)S(1)} %iota_compare_fusion.3), kind=kLoop, calls=%fused_computation.13 | loop fusion | flops 3932160 | bytes 1765376 | tf_op jit(solution)/shard_map/convert_element_type | solution.py:149
  77.3 2.1 %select_convert_fusion.2 = bf16[8,128,768]{2,1,0:T(8,128)(2,1)} fusion(f32[8,768]{1,0:T(8,128)S(1)} %copy-done.18, f32[8,768]{1,0:T(8,128)S(1)} %copy-done.19, f32[8,128]{1,0:T(8,128)S(1)} %copy-done.34, f32[128,768]{1,0:T(8,128)S(1)} %fusion.34, pred[128,768]{1,0:T(8,128)(4,1)S(1)} %copy-done.11), kind=kLoop, calls=%fused_computation.8 | loop fusion | flops 4718592 | bytes 2117632 | tf_op jit(solution)/shard_map/convert_element_type | solution.py:149
  79.7 2.3 %select_convert_fusion.1 = bf16[8,128,896]{2,1,0:T(8,128)(2,1)} fusion(f32[8,896]{1,0:T(8,128)S(1)} %copy-done.16, f32[8,896]{1,0:T(8,128)S(1)} %copy-done.17, f32[8,128]{1,0:T(8,128)S(1)} %copy-done.33, f32[128,896]{1,0:T(8,128)S(1)} %fusion.32, pred[128,896]{1,0:T(8,128)(4,1)S(1)} %copy-done.10), kind=kLoop, calls=%fused_computation.7 | loop fusion | flops 5505024 | bytes 2469888 | tf_op jit(solution)/shard_map/convert_element_type | solution.py:149
  82.3 2.5 %select_convert_fusion = bf16[8,128,1024]{2,1,0:T(8,128)(2,1)} fusion(f32[8,1024]{1,0:T(8,128)S(1)} %get-tuple-element.9, f32[8,1024]{1,0:T(8,128)S(1)} %bitcast.129, f32[8,128]{1,0:T(8,128)S(1)} %copy-done.32, f32[128,1024]{1,0:T(8,128)S(1)} %fusion.30, pred[128,1024]{1,0:T(8,128)(4,1)S(1)} %copy-done.8), kind=kLoop, calls=%fused_computation.6 | loop fusion | flops 6291456 | bytes 2822144 | tf_op jit(solution)/shard_map/convert_element_type | solution.py:149
  84.8 15.5 %all-to-all-done.1 = bf16[16,64,512]{2,1,0:T(8,128)(2,1)S(1)} async-done(((bf16[16,64,512]{2,1,0:T(8,128)(2,1)}), bf16[16,64,512]{2,1,0:T(8,128)(2,1)S(1)}, u32[]{:S(2)}, u32[]{:S(2)}) %all-to-all-start.1) | async-done | bytes 1048608 | tf_op jit(solution)/shard_map/all_to_all | solution.py:83
  100.7 0.7 copy-done.2
  101.4 2.4 %multiply_convert_fusion.3 = bf16[1024,512]{1,0:T(8,128)(2,1)} fusion(f32[1024,512]{1,0:T(8,128)S(1)} %bitcast_convert_fusion, f32[3,512]{1,0:T(4,128)S(1)} %copy-done.28, f32[512]{0:T(512)S(1)} %bitcast.138, f32[512]{0:T(512)S(1)} %bitcast.139, f32[512]{0:T(512)S(1)} %bitcast.137, f32[512]{0:T(512)S(1)} %bitcast.136, f32[512]{0:T(512)S(1)} %copy-done.42), kind=kLoop, calls=%fused_computation.31 | loop fusion | flops 8388608 | bytes 3162112 | tf_op jit(solution)/shard_map/convert_element_type | solution.py:30
  103.8 1.5 copy.147
  105.5 1.5 convolution_dynamic-update-slice_fusion.4
  107.0 1.6 convolution_dynamic-update-slice_fusion.7
  109.1 0.6 convolution_dynamic-update-slice_fusion.2
  110.0 0.6 convolution_dynamic-update-slice_fusion.1
  110.7 0.8 convolution_dynamic-update-slice_fusion
  111.5 0.8 copy-done.1
  112.3 0.8 convolution_dynamic-update-slice_fusion.6
  113.4 1.4 fusion.15
  114.7 2.3 %reshape.324 = bf16[16,64,512]{1,0,2:T(8,128)(2,1)} reshape(bf16[1024,8,64]{0,2,1:T(8,128)(2,1)S(1)} %fusion.15) | data formatting | bytes 2097152 | tf_op jit(solution)/shard_map/all_to_all | solution.py:179
  117.1 3.3 %copy.151 = bf16[16,64,512]{2,1,0:T(8,128)(2,1)} copy(bf16[16,64,512]{1,0,2:T(8,128)(2,1)} %reshape.324) | data formatting | bytes 2097152 | tf_op jit(solution)/shard_map/all_to_all | solution.py:179
  120.4 6.8 %all-to-all-start.2 = ((bf16[16,64,512]{2,1,0:T(8,128)(2,1)}), bf16[16,64,512]{2,1,0:T(8,128)(2,1)S(1)}, u32[]{:S(2)}, u32[]{:S(2)}) async-start(bf16[16,64,512]{2,1,0:T(8,128)(2,1)} %copy.151), calls=%async_computation.2 | async-start | bytes 2097152 | tf_op jit(solution)/shard_map/all_to_all | solution.py:179
  127.3 0.7 slice.349
  128.6 1.3 slice.348
  129.9 3.3 %fusion.16 = f32[8,64,256]{2,1,0:T(8,128)} fusion(bf16[8,64,1024]{2,1,0:T(8,128)(2,1)S(1)} %bitcast.112, f32[1024,8]{0,1:T(8,128)S(1)} %copy-done.31, f32[1024,256]{1,0:T(8,128)S(1)} %slice_convert_fusion, f32[8,64,256]{2,1,0:T(8,128)} %param.28, f32[8]{0:T(128)S(1)} %exp.65), kind=kOutput, calls=%fused_computation.36 | convolution fusion | flops 272891904 | bytes 3178528 | tf_op jit(solution)/shard_map/hps,shn->hpn/dot_general | solution.py:174
  133.2 42.6 %all-to-all-done.2 = bf16[16,64,512]{2,1,0:T(8,128)(2,1)S(1)} async-done(((bf16[16,64,512]{2,1,0:T(8,128)(2,1)}), bf16[16,64,512]{2,1,0:T(8,128)(2,1)S(1)}, u32[]{:S(2)}, u32[]{:S(2)}) %all-to-all-start.2) | async-done | bytes 1048608 | tf_op jit(solution)/shard_map/all_to_all | solution.py:179
  177.1 1.2 copy.156
  178.3 1.3 multiply_convert_fusion.2
  (172 shorter events, 12.1 us)
Async XLA Ops:
  1.7 15.9 %copy-start.7 = (bf16[64,8192]{1,0:T(8,128)(2,1)S(1)}, bf16[64,8192]{1,0:T(8,128)(2,1)}, u32[]{:S(2)}) copy-start(bf16[64,8192]{1,0:T(8,128)(2,1)} %param.15) | copy-start | bytes 3145732
  3.5 15.3 %copy-start.47 = (bf16[3,512]{1,0:T(4,128)(2,1)S(1)}, bf16[3,512]{1,0:T(4,128)(2,1)}, u32[]{:S(2)}) copy-start(bf16[3,512]{1,0:T(4,128)(2,1)} %param.18) | copy-start | bytes 9220
  3.5 15.8 %copy-start.51 = (bf16[512]{0:T(512)(128)(2,1)S(1)}, bf16[512]{0:T(512)(128)(2,1)}, u32[]{:S(2)}) copy-start(bf16[512]{0:T(512)(128)(2,1)} %param.21) | copy-start | bytes 3076
  3.5 18.7 %copy-start = (s32[4]{0:T(128)S(1)}, s32[4]{0:T(128)}, u32[]{:S(2)}) copy-start(s32[4]{0:T(128)} %constant.91.clone) | copy-start | bytes 52
  4.4 18.6 %copy-start.41 = (bf16[4,512]{1,0:T(4,128)(2,1)S(1)}, bf16[4,512]{1,0:T(4,128)(2,1)}, u32[]{:S(2)}) copy-start(bf16[4,512]{1,0:T(4,128)(2,1)} %param.20) | copy-start | bytes 12292
  4.4 40.6 %all-to-all-start = ((bf16[16,132,128]{2,1,0:T(8,128)(2,1)}), bf16[16,132,128]{2,1,0:T(8,128)(2,1)S(1)}, u32[]{:S(2)}, u32[]{:S(2)}) async-start(bf16[16,132,128]{2,1,0:T(8,128)(2,1)} %pad_maximum_fusion.3), calls=%async_computation | async-start | bytes 1114112 | tf_op jit(solution)/shard_map/all_to_all | solution.py:77
  22.2 30.0 %copy-start.48 = (f32[8]{0:T(128)S(1)}, f32[8]{0:T(128)}, u32[]{:S(2)}) copy-start(f32[8]{0:T(128)} %param.24) | copy-start | bytes 100
  22.2 30.0 %copy-start.52 = (f32[8]{0:T(128)S(1)}, f32[8]{0:T(128)}, u32[]{:S(2)}) copy-start(f32[8]{0:T(128)} %param.25) | copy-start | bytes 100
  45.0 55.3 %all-to-all-start.1 = ((bf16[16,64,512]{2,1,0:T(8,128)(2,1)}), bf16[16,64,512]{2,1,0:T(8,128)(2,1)S(1)}, u32[]{:S(2)}, u32[]{:S(2)}) async-start(bf16[16,64,512]{2,1,0:T(8,128)(2,1)} %bitcast.99), calls=%async_computation.1 | async-start | bytes 2097152 | tf_op jit(solution)/shard_map/all_to_all | solution.py:83
  55.2 4.0 %copy-start.49 = (f32[8]{0:T(128)}, f32[8]{0:T(128)S(1)}, u32[]{:S(2)}) copy-start(f32[8]{0:T(128)S(1)} %slice_reduce_fusion.1) | copy-start | bytes 100
  55.5 1.0 copy-start.3
  56.7 12.3 %collective-permute-start = (bf16[2,1024,128]{2,1,0:T(8,128)(2,1)S(1)}, bf16[2,1024,128]{2,1,0:T(8,128)(2,1)S(1)}, u32[]{:S(2)}, u32[]{:S(2)}) collective-permute-start(bf16[2,1024,128]{2,1,0:T(8,128)(2,1)S(1)} %bitcast.119), channel_id=1, source_target_pairs={{0,1},{1,0},{2,3},{3,2},{4,5},{5,4},{6,7},{7,6},{8,9},{9,8},{10,11... | collective-permute-start | bytes 1572872 | tf_op jit(solution)/shard_map/ppermute | solution.py:114
  69.9 0.7 copy-start.24
  69.9 0.7 copy-start.27
  69.9 0.7 copy-start.39
  69.9 1.1 copy-start.15
  69.9 1.1 copy-start.29
  69.9 1.1 copy-start.30
  69.9 1.1 copy-start.38
  69.9 2.5 %copy-start.13 = (pred[128,384]{1,0:T(8,128)(4,1)S(1)}, pred[128,384]{1,0:T(8,128)(4,1)}, u32[]{:S(2)}) copy-start(pred[128,384]{1,0:T(8,128)(4,1)} %iota_compare_fusion.5) | copy-start | bytes 147460
  70.0 2.5 %copy-start.25 = (f32[8,384]{1,0:T(8,128)S(1)}, f32[8,384]{1,0:T(8,128)}, u32[]{:S(2)}) copy-start(f32[8,384]{1,0:T(8,128)} %slice.317) | copy-start | bytes 36868
  70.0 2.5 %copy-start.26 = (f32[8,384]{1,0:T(8,128)S(1)}, f32[8,384]{1,0:T(8,128)}, u32[]{:S(2)}) copy-start(f32[8,384]{1,0:T(8,128)} %slice.316) | copy-start | bytes 36868
  70.0 2.5 %copy-start.37 = (f32[8,128]{1,0:T(8,128)S(1)}, f32[8,128]{1,0:T(8,128)}, u32[]{:S(2)}) copy-start(f32[8,128]{1,0:T(8,128)} %get-tuple-element.17) | copy-start | bytes 12292
  70.4 3.8 %copy-start.12 = (pred[128,512]{1,0:T(8,128)(4,1)S(1)}, pred[128,512]{1,0:T(8,128)(4,1)}, u32[]{:S(2)}) copy-start(pred[128,512]{1,0:T(8,128)(4,1)} %iota_compare_fusion.4) | copy-start | bytes 196612
  70.4 3.8 %copy-start.22 = (f32[8,512]{1,0:T(8,128)S(1)}, f32[8,512]{1,0:T(8,128)}, u32[]{:S(2)}) copy-start(f32[8,512]{1,0:T(8,128)} %slice.323) | copy-start | bytes 49156
  70.4 3.8 %copy-start.23 = (f32[8,512]{1,0:T(8,128)S(1)}, f32[8,512]{1,0:T(8,128)}, u32[]{:S(2)}) copy-start(f32[8,512]{1,0:T(8,128)} %slice.322) | copy-start | bytes 49156
  70.4 3.8 %copy-start.36 = (f32[8,128]{1,0:T(8,128)S(1)}, f32[8,128]{1,0:T(8,128)}, u32[]{:S(2)}) copy-start(f32[8,128]{1,0:T(8,128)} %get-tuple-element.16) | copy-start | bytes 12292
  72.2 2.9 %copy-start.20 = (f32[8,640]{1,0:T(8,128)S(1)}, f32[8,640]{1,0:T(8,128)}, u32[]{:S(2)}) copy-start(f32[8,640]{1,0:T(8,128)} %slice.329) | copy-start | bytes 61444
  72.2 2.9 %copy-start.21 = (f32[8,640]{1,0:T(8,128)S(1)}, f32[8,640]{1,0:T(8,128)}, u32[]{:S(2)}) copy-start(f32[8,640]{1,0:T(8,128)} %slice.328) | copy-start | bytes 61444
  72.2 2.9 %copy-start.35 = (f32[8,128]{1,0:T(8,128)S(1)}, f32[8,128]{1,0:T(8,128)}, u32[]{:S(2)}) copy-start(f32[8,128]{1,0:T(8,128)} %get-tuple-element.15) | copy-start | bytes 12292
  74.2 3.1 %copy-start.11 = (pred[128,768]{1,0:T(8,128)(4,1)S(1)}, pred[128,768]{1,0:T(8,128)(4,1)}, u32[]{:S(2)}) copy-start(pred[128,768]{1,0:T(8,128)(4,1)} %iota_compare_fusion.2) | copy-start | bytes 294916
  74.2 3.1 %copy-start.18 = (f32[8,768]{1,0:T(8,128)S(1)}, f32[8,768]{1,0:T(8,128)}, u32[]{:S(2)}) copy-start(f32[8,768]{1,0:T(8,128)} %slice.335) | copy-start | bytes 73732
  74.2 3.1 %copy-start.19 = (f32[8,768]{1,0:T(8,128)S(1)}, f32[8,768]{1,0:T(8,128)}, u32[]{:S(2)}) copy-start(f32[8,768]{1,0:T(8,128)} %slice.334) | copy-start | bytes 73732
  74.2 3.1 %copy-start.34 = (f32[8,128]{1,0:T(8,128)S(1)}, f32[8,128]{1,0:T(8,128)}, u32[]{:S(2)}) copy-start(f32[8,128]{1,0:T(8,128)} %get-tuple-element.14) | copy-start | bytes 12292
  76.9 2.7 %copy-start.10 = (pred[128,896]{1,0:T(8,128)(4,1)S(1)}, pred[128,896]{1,0:T(8,128)(4,1)}, u32[]{:S(2)}) copy-start(pred[128,896]{1,0:T(8,128)(4,1)} %iota_compare_fusion.1) | copy-start | bytes 344068
  76.9 2.7 %copy-start.16 = (f32[8,896]{1,0:T(8,128)S(1)}, f32[8,896]{1,0:T(8,128)}, u32[]{:S(2)}) copy-start(f32[8,896]{1,0:T(8,128)} %slice.341) | copy-start | bytes 86020
  77.0 2.7 %copy-start.17 = (f32[8,896]{1,0:T(8,128)S(1)}, f32[8,896]{1,0:T(8,128)}, u32[]{:S(2)}) copy-start(f32[8,896]{1,0:T(8,128)} %slice.340) | copy-start | bytes 86020
  77.0 2.7 %copy-start.33 = (f32[8,128]{1,0:T(8,128)S(1)}, f32[8,128]{1,0:T(8,128)}, u32[]{:S(2)}) copy-start(f32[8,128]{1,0:T(8,128)} %get-tuple-element.13) | copy-start | bytes 12292
  79.3 2.9 %copy-start.8 = (pred[128,1024]{1,0:T(8,128)(4,1)S(1)}, pred[128,1024]{1,0:T(8,128)(4,1)}, u32[]{:S(2)}) copy-start(pred[128,1024]{1,0:T(8,128)(4,1)} %iota_compare_fusion) | copy-start | bytes 393220
  79.3 2.9 %copy-start.32 = (f32[8,128]{1,0:T(8,128)S(1)}, f32[8,128]{1,0:T(8,128)}, u32[]{:S(2)}) copy-start(f32[8,128]{1,0:T(8,128)} %get-tuple-element.12) | copy-start | bytes 12292
  84.8 16.6 %copy-start.28 = (f32[3,512]{1,0:T(4,128)S(1)}, f32[3,512]{1,0:T(4,128)}, u32[]{:S(2)}) copy-start(f32[3,512]{1,0:T(4,128)} %convert_element_type.117) | copy-start | bytes 18436
  84.8 16.6 %copy-start.42 = (f32[512]{0:T(512)S(1)}, f32[512]{0:T(512)}, u32[]{:S(2)}) copy-start(f32[512]{0:T(512)} %convert_element_type.116) | copy-start | bytes 6148
  84.8 16.6 %copy-start.43 = (f32[1,512]{1,0:T(1,128)S(1)}, f32[1,512]{1,0:T(1,128)}, u32[]{:S(2)}) copy-start(f32[1,512]{1,0:T(1,128)} %get-tuple-element.26) | copy-start | bytes 6148
  84.8 16.6 %copy-start.44 = (f32[1,512]{1,0:T(1,128)S(1)}, f32[1,512]{1,0:T(1,128)}, u32[]{:S(2)}) copy-start(f32[1,512]{1,0:T(1,128)} %get-tuple-element.27) | copy-start | bytes 6148
  84.8 16.6 %copy-start.45 = (f32[1,512]{1,0:T(1,128)S(1)}, f32[1,512]{1,0:T(1,128)}, u32[]{:S(2)}) copy-start(f32[1,512]{1,0:T(1,128)} %get-tuple-element.28) | copy-start | bytes 6148
  84.8 16.6 %copy-start.46 = (f32[1,512]{1,0:T(1,128)S(1)}, f32[1,512]{1,0:T(1,128)}, u32[]{:S(2)}) copy-start(f32[1,512]{1,0:T(1,128)} %get-tuple-element.29) | copy-start | bytes 6148
  100.3 1.0 copy-start.2
  105.5 3.6 %copy-start.6 = (bf16[8,128,640]{2,1,0:T(8,128)(2,1)S(1)}, bf16[8,128,640]{2,1,0:T(8,128)(2,1)}, u32[]{:S(2)}) copy-start(bf16[8,128,640]{2,1,0:T(8,128)(2,1)} %select_convert_fusion.3) | copy-start | bytes 3932164
  108.6 1.4 copy-start.5
  109.1 1.6 copy-start.4
  110.7 1.6 copy-start.1
  112.3 1.0 copy-start.9
  112.3 1.0 copy-start.14
  112.3 1.0 copy-start.53
  117.1 10.2 %copy-start.40 = (bf16[8192]{0:T(1024)(128)(2,1)S(1)}, bf16[8192]{0:T(1024)(128)(2,1)}, u32[]{:S(2)}) copy-start(bf16[8192]{0:T(1024)(128)(2,1)} %param.27) | copy-start | bytes 49156
  117.1 10.2 %copy-start.50 = (f32[8]{0:T(128)S(1)}, f32[8]{0:T(128)}, u32[]{:S(2)}) copy-start(f32[8]{0:T(128)} %copy-done.49) | copy-start | bytes 100
  120.4 9.5 %copy-start.31 = (f32[1024,8]{0,1:T(8,128)S(1)}, f32[1024,8]{0,1:T(8,128)}, u32[]{:S(2)}) copy-start(f32[1024,8]{0,1:T(8,128)} %get-tuple-element.8) | copy-start | bytes 98308
  120.4 55.4 %all-to-all-start.2 = ((bf16[16,64,512]{2,1,0:T(8,128)(2,1)}), bf16[16,64,512]{2,1,0:T(8,128)(2,1)S(1)}, u32[]{:S(2)}, u32[]{:S(2)}) async-start(bf16[16,64,512]{2,1,0:T(8,128)(2,1)} %copy.151), calls=%async_computation.2 | async-start | bytes 2097152 | tf_op jit(solution)/shard_map/all_to_all | solution.py:179
